TPU v7x, 768 devices: a whole 4x8x12 slice. The times are simulated.
768 devices in a mesh: rad: 12 (over z_lo, core), azi: 64 (over z_hi, x, y).
Axes of the slice: x: 4, y: 8, z: 12 (z_hi: 2, z_lo: 6; z = z_hi * 6 + z_lo), core: 2. Of those that a mesh axis runs over, the one named last changes fastest.
Arguments:
- fields: float32 [3, 8, 96, 8192], P(None, None, 'rad', 'azi'), may hold values from -6 to 6
- viscosity: float32 [96, 8192], P('rad', 'azi'), may hold values from 0.05 to 0.5
- rotation: float32 [96], replicated, may hold values from 0.2 to 2
- shift_blocks: int32 [1, 96], replicated, may hold values from 0 to 127
Outputs:
- fields_out: float32 [3, 8, 96, 8192], P(None, None, 'rad', 'azi')
Inputs may be any that keep to these rules, and one draw needn't show every extreme that they name: `shift_blocks`: shift of radius r after step t, in blocks of 64 azimuth cells.
All inputs are finite; a program needn't handle non-finite values.
Results may differ from a plain program's by a relative error of at most 0.00002.
Values sent between devices are 32-bit elements; how exact they have to be, the bound alone decides.
No kernel may reach another device: no remote copies, remote signals or barrier semaphores. Data moves between devices by JAX's collectives and lax.ppermute only.
A program may use at most 32 MiB of HBM per device.

v0:
```python
import jax
import jax.numpy as jnp
from jax import lax
from jax.sharding import PartitionSpec as P

BLOCK = 64


time_step = 0.3


def with_halo(cells, sides, width, closed):
    for axis, dim in sides:
        count = lax.axis_size(axis)
        ends = count if closed else count - 1
        head = lax.slice_in_dim(cells, 0, width, axis=dim)
        tail = lax.slice_in_dim(cells, cells.shape[dim] - width, cells.shape[dim], axis=dim)
        cells = jnp.concatenate(
            [
                lax.ppermute(tail, axis, [(i, (i + 1) % count) for i in range(ends)]),
                cells,
                lax.ppermute(head, axis, [((i + 1) % count, i) for i in range(ends)]),
            ],
            axis=dim,
        )
    return cells


def neighbour_rates(centre, north, south, ahead, behind, viscosity, spin):
    above = jnp.concatenate([centre[:, 1:], centre[:, -1:]], axis=1)
    below = jnp.concatenate([centre[:, :1], centre[:, :-1]], axis=1)
    spread = viscosity * (north + south + ahead + behind + above + below - 6.0 * centre)
    radial_grad = 0.5 * (north - south)
    azimuth_grad = 0.5 * (ahead - behind)
    rate_density = spread[0] - radial_grad[1] - azimuth_grad[2]
    rate_radial = spread[1] - radial_grad[0] + 2.0 * spin * centre[2]
    rate_azimuth = spread[2] - azimuth_grad[0] - 0.5 * spin * centre[1]
    return jnp.stack([rate_density, rate_radial, rate_azimuth])


def body(fields, viscosity, rotation, shift_blocks):
    radii = fields.shape[2]
    band = lax.axis_index("rad")
    first_row = band * radii
    own_spin = lax.dynamic_slice_in_dim(rotation, first_row, radii)[:, None]

    def section_rates(state):
        edge_rows = jnp.stack([state[:, :, 0], state[:, :, -1]], axis=2)
        got_rows = with_halo(edge_rows, (("rad", 2),), 1, False)
        edge_cols = jnp.stack([state[..., 0], state[..., -1]], axis=3)
        got_cols = with_halo(edge_cols, (("azi", 3),), 1, True)
        south = jnp.concatenate([got_rows[:, :, 0:1], state[:, :, :-1]], axis=2)
        north = jnp.concatenate([state[:, :, 1:], got_rows[:, :, 3:4]], axis=2)
        behind = jnp.concatenate([got_cols[..., 0:1], state[..., :-1]], axis=3)
        ahead = jnp.concatenate([state[..., 1:], got_cols[..., 3:4]], axis=3)
        return neighbour_rates(state, north, south, ahead, behind, viscosity, own_spin)

    state = fields
    first = state + time_step * section_rates(state)
    second = 0.75 * state + 0.25 * (first + time_step * section_rates(first))
    state = state / 3.0 + 2.0 / 3.0 * (second + time_step * section_rates(second))
    local_shift = lax.dynamic_slice_in_dim(shift_blocks[0], first_row, radii)
    heights = state.shape[1]
    cells = state.shape[3]
    rows = state.reshape(3, heights * radii, cells)
    part = lax.all_to_all(rows, "azi", split_axis=1, concat_axis=2, tiled=True)
    per_device = part.shape[1]
    cycle = part.shape[2]
    count = cycle // BLOCK
    line = lax.axis_index("azi") * per_device + lax.iota(jnp.int32, per_device)
    radius = line % radii
    matches = radius[:, None] == lax.iota(jnp.int32, radii)[None, :]
    amount = jnp.sum(jnp.where(matches, local_shift[None, :], 0), axis=1)
    offsets = (count - amount) % count * BLOCK
    doubled = jnp.concatenate([part, part], axis=2)

    def roll_row(item):
        row_pair, offset = item
        return lax.dynamic_slice_in_dim(row_pair, offset, cycle, 1)

    rolled = lax.map(roll_row, (jnp.swapaxes(doubled, 0, 1), offsets))
    moved = jnp.swapaxes(rolled, 0, 1)
    state = lax.all_to_all(moved, "azi", split_axis=2, concat_axis=1, tiled=True).reshape(
        3, heights, radii, cells
    )
    return state


def solution(mesh):
    return jax.shard_map(
        body,
        mesh=mesh,
        in_specs=(P(None, None, "rad", "azi"), P("rad", "azi"), P(), P()),
        out_specs=P(None, None, "rad", "azi"),
        check_vma=False,
    )
```

profile of v0, /device:TPU:64, one launch (start us, length us, event | category | flops | bytes accessed | tf_op | source)
XLA Modules:
  0.0 210.3 jit_solution(6602233674195548883)
XLA Ops:
  0.0 1.1 fusion.37
  1.1 1.9 collective-permute-start
  3.0 2.4 %collective-permute-start.1 = (f32[3,8,1,128]{3,2,1,0:T(1,128)S(1)}, f32[3,8,1,128]{3,2,1,0:T(1,128)S(1)}, u32[]{:S(2)}, u32[]{:S(2)}) collective-permute-start(f32[3,8,1,128]{3,2,1,0:T(1,128)S(1)} %get-tuple-element.59), channel_id=1, source_target_pairs={{0,64},{64,128},{128,192},{192,256},{256,320},{320,384},{384,448},... | collective-permute-start | bytes 36872 | tf_op jit(solution)/shard_map/ppermute | solution.py:20
  5.4 1.1 fusion.41
  6.5 19.3 %collective-permute-start.2 = (f32[3,8,8,1]{3,2,1,0:T(8,128)S(1)}, f32[3,8,8,1]{3,2,1,0:T(8,128)S(1)}, u32[]{:S(2)}, u32[]{:S(2)}) collective-permute-start(f32[3,8,8,1]{3,2,1,0:T(8,128)S(1)} %get-tuple-element.66), channel_id=1, source_target_pairs={{1,0},{2,1},{3,2},{4,3},{5,4},{6,5},{7,6},{8,7},{9,8},{10,9},{11,1... | collective-permute-start | bytes 2312 | tf_op jit(solution)/shard_map/ppermute | solution.py:22
  25.8 1.9 collective-permute-start.3
  28.5 1.0 fusion.39
  29.5 1.1 fusion.40
  30.5 1.0 fusion.36
  32.3 10.6 %collective-permute-done.3 = f32[3,8,8,1]{3,2,1,0:T(8,128)S(1)} collective-permute-done((f32[3,8,8,1]{3,2,1,0:T(8,128)S(1)}, f32[3,8,8,1]{3,2,1,0:T(8,128)S(1)}, u32[]{:S(2)}, u32[]{:S(2)}) %collective-permute-start.3) | collective-permute-done | bytes 800 | tf_op jit(solution)/shard_map/ppermute | solution.py:20
  43.0 1.0 fusion.3
  44.9 0.9 fusion.4
  46.0 3.9 %collective-permute-start.4 = (f32[3,8,1,128]{3,2,1,0:T(1,128)S(1)}, f32[3,8,1,128]{3,2,1,0:T(1,128)S(1)}, u32[]{:S(2)}, u32[]{:S(2)}) collective-permute-start(f32[3,8,1,128]{3,2,1,0:T(1,128)S(1)} %get-tuple-element.46), channel_id=1, source_target_pairs={{64,0},{128,64},{192,128},{256,192},{320,256},{384,320},{448,384},... | collective-permute-start | bytes 36872 | tf_op jit(solution)/shard_map/ppermute | solution.py:22
  50.0 4.9 %collective-permute-start.5 = (f32[3,8,1,128]{3,2,1,0:T(1,128)S(1)}, f32[3,8,1,128]{3,2,1,0:T(1,128)S(1)}, u32[]{:S(2)}, u32[]{:S(2)}) collective-permute-start(f32[3,8,1,128]{3,2,1,0:T(1,128)S(1)} %get-tuple-element.47), channel_id=1, source_target_pairs={{0,64},{64,128},{128,192},{192,256},{256,320},{320,384},{384,448},... | collective-permute-start | bytes 36872 | tf_op jit(solution)/shard_map/ppermute | solution.py:20
  54.9 1.9 collective-permute-start.6
  56.8 3.9 %collective-permute-start.7 = (f32[3,8,8,1]{3,2,1,0:T(8,128)S(1)}, f32[3,8,8,1]{3,2,1,0:T(8,128)S(1)}, u32[]{:S(2)}, u32[]{:S(2)}) collective-permute-start(f32[3,8,8,1]{3,2,1,0:T(8,128)S(1)} %get-tuple-element.55), channel_id=1, source_target_pairs={{0,1},{1,2},{2,3},{3,4},{4,5},{5,6},{6,7},{7,8},{8,9},{9,10},{10,1... | collective-permute-start | bytes 2312 | tf_op jit(solution)/shard_map/ppermute | solution.py:20
  60.8 0.9 collective-permute-done.6
  61.7 15.4 %collective-permute-done.7 = f32[3,8,8,1]{3,2,1,0:T(8,128)S(1)} collective-permute-done((f32[3,8,8,1]{3,2,1,0:T(8,128)S(1)}, f32[3,8,8,1]{3,2,1,0:T(8,128)S(1)}, u32[]{:S(2)}, u32[]{:S(2)}) %collective-permute-start.7) | collective-permute-done | bytes 800 | tf_op jit(solution)/shard_map/ppermute | solution.py:20
  77.7 1.9 collective-permute-start.8
  79.6 3.3 %collective-permute-start.9 = (f32[3,8,1,128]{3,2,1,0:T(1,128)S(1)}, f32[3,8,1,128]{3,2,1,0:T(1,128)S(1)}, u32[]{:S(2)}, u32[]{:S(2)}) collective-permute-start(f32[3,8,1,128]{3,2,1,0:T(1,128)S(1)} %get-tuple-element.35), channel_id=1, source_target_pairs={{0,64},{64,128},{128,192},{192,256},{256,320},{320,384},{384,448},... | collective-permute-start | bytes 36872 | tf_op jit(solution)/shard_map/ppermute | solution.py:20
  82.9 1.9 collective-permute-start.10
  84.8 3.9 %collective-permute-start.11 = (f32[3,8,8,1]{3,2,1,0:T(8,128)S(1)}, f32[3,8,8,1]{3,2,1,0:T(8,128)S(1)}, u32[]{:S(2)}, u32[]{:S(2)}) collective-permute-start(f32[3,8,8,1]{3,2,1,0:T(8,128)S(1)} %get-tuple-element.43), channel_id=1, source_target_pairs={{0,1},{1,2},{2,3},{3,4},{4,5},{5,6},{6,7},{7,8},{8,9},{9,10},{10,1... | collective-permute-start | bytes 2312 | tf_op jit(solution)/shard_map/ppermute | solution.py:20
  88.8 0.9 collective-permute-done.10
  89.7 14.1 %collective-permute-done.11 = f32[3,8,8,1]{3,2,1,0:T(8,128)S(1)} collective-permute-done((f32[3,8,8,1]{3,2,1,0:T(8,128)S(1)}, f32[3,8,8,1]{3,2,1,0:T(8,128)S(1)}, u32[]{:S(2)}, u32[]{:S(2)}) %collective-permute-start.11) | collective-permute-done | bytes 800 | tf_op jit(solution)/shard_map/ppermute | solution.py:20
  104.8 4.6 %all-to-all-start = ((f32[3,64,128]{2,0,1:T(4,128)}), f32[3,64,128]{2,0,1:T(4,128)S(1)}, u32[]{:S(2)}, u32[]{:S(2)}) async-start(f32[3,64,128]{2,0,1:T(4,128)} %bitcast), calls=%async_computation | async-start | bytes 262144 | tf_op jit(solution)/shard_map/all_to_all | solution.py:66
  110.8 16.3 %all-to-all-done = f32[3,64,128]{2,0,1:T(4,128)S(1)} async-done(((f32[3,64,128]{2,0,1:T(4,128)}), f32[3,64,128]{2,0,1:T(4,128)S(1)}, u32[]{:S(2)}, u32[]{:S(2)}) %all-to-all-start) | async-done | bytes 98336 | tf_op jit(solution)/shard_map/all_to_all | solution.py:66
  127.4 6.4 %copy.6 = f32[3,1,8192]{0,1,2:T(1,128)} copy(f32[3,1,8192]{2,0,1:T(4,128)S(1)} %fusion) | data formatting | bytes 196608 | tf_op jit(solution)/shard_map/while/body/eval_jaxpr/dynamic_slice | solution.py:79
  134.4 38.5 %reduce.1 = f32[8192,3]{1,0:T(8,128)} reduce(f32[8192,1,3]{2,1,0:T(1,128)} %bitcast.9, f32[]{:T(128)} %broadcast.65), dimensions={1}, to_apply=%bitcast.7.reduce_sub_computation | reduce | bytes 196612
  172.8 4.6 %reshape.48 = f32[64,1,384]{2,1,0:T(1,128)S(1)} reshape(f32[8192,3]{1,0:T(8,128)} %reduce.1) | data formatting | bytes 196608
  177.5 21.1 %all_to_all.21 = f32[64,1,384]{2,1,0:T(1,128)S(1)} all-to-all(f32[64,1,384]{2,1,0:T(1,128)S(1)} %reshape.48), channel_id=1, replica_groups=mesh['rad'=12,'azi'=64] {'azi'}, dimensions={0} | all-to-all | bytes 196608 | tf_op jit(solution)/shard_map/all_to_all | solution.py:83
  199.4 7.4 %reshape.49 = f32[8192,1,3]{2,1,0:T(1,128)} reshape(f32[64,384]{1,0:T(8,128)S(1)} %reduce.2) | data formatting | bytes 196608
  206.8 3.5 %copy.8 = f32[3,8,8,128]{3,2,1,0:T(8,128)} copy(f32[3,8,8,128]{0,3,2,1:T(8,128)} %bitcast.10) | data formatting | bytes 196608 | tf_op jit(solution)/shard_map/reshape | solution.py:83
  (42 shorter events, 6.6 us)
Async XLA Ops:
  0.0 77.1 %copy-start = (f32[3,8,8,128]{3,2,1,0:T(8,128)S(1)}, f32[3,8,8,128]{3,2,1,0:T(8,128)}, u32[]{:S(2)}) copy-start(f32[3,8,8,128]{3,2,1,0:T(8,128)} %param.4) | copy-start | bytes 294916
  0.0 77.1 %copy-start.1 = (f32[8,128]{1,0:T(8,128)S(1)}, f32[8,128]{1,0:T(8,128)}, u32[]{:S(2)}) copy-start(f32[8,128]{1,0:T(8,128)} %param.5) | copy-start | bytes 12292
  1.1 31.2 %collective-permute-start = (f32[3,8,1,128]{3,2,1,0:T(1,128)S(1)}, f32[3,8,1,128]{3,2,1,0:T(1,128)S(1)}, u32[]{:S(2)}, u32[]{:S(2)}) collective-permute-start(f32[3,8,1,128]{3,2,1,0:T(1,128)S(1)} %get-tuple-element.58), channel_id=1, source_target_pairs={{64,0},{128,64},{192,128},{256,192},{320,256},{384,320},{448,384},... | collective-permute-start | bytes 36872 | tf_op jit(solution)/shard_map/ppermute | solution.py:22
  3.0 29.3 %collective-permute-start.1 = (f32[3,8,1,128]{3,2,1,0:T(1,128)S(1)}, f32[3,8,1,128]{3,2,1,0:T(1,128)S(1)}, u32[]{:S(2)}, u32[]{:S(2)}) collective-permute-start(f32[3,8,1,128]{3,2,1,0:T(1,128)S(1)} %get-tuple-element.59), channel_id=1, source_target_pairs={{0,64},{64,128},{128,192},{192,256},{256,320},{320,384},{384,448},... | collective-permute-start | bytes 36872 | tf_op jit(solution)/shard_map/ppermute | solution.py:20
  6.5 25.8 %collective-permute-start.2 = (f32[3,8,8,1]{3,2,1,0:T(8,128)S(1)}, f32[3,8,8,1]{3,2,1,0:T(8,128)S(1)}, u32[]{:S(2)}, u32[]{:S(2)}) collective-permute-start(f32[3,8,8,1]{3,2,1,0:T(8,128)S(1)} %get-tuple-element.66), channel_id=1, source_target_pairs={{1,0},{2,1},{3,2},{4,3},{5,4},{6,5},{7,6},{8,7},{9,8},{10,9},{11,1... | collective-permute-start | bytes 2312 | tf_op jit(solution)/shard_map/ppermute | solution.py:22
  25.8 17.1 %collective-permute-start.3 = (f32[3,8,8,1]{3,2,1,0:T(8,128)S(1)}, f32[3,8,8,1]{3,2,1,0:T(8,128)S(1)}, u32[]{:S(2)}, u32[]{:S(2)}) collective-permute-start(f32[3,8,8,1]{3,2,1,0:T(8,128)S(1)} %get-tuple-element.67), channel_id=1, source_target_pairs={{0,1},{1,2},{2,3},{3,4},{4,5},{5,6},{6,7},{7,8},{8,9},{9,10},{10,1... | collective-permute-start | bytes 2312 | tf_op jit(solution)/shard_map/ppermute | solution.py:20
  45.8 63.6 %copy-start.2 = (s32[1,96]{1,0:T(1,128)S(1)}, s32[1,96]{1,0:T(1,128)}, u32[]{:S(2)}) copy-start(s32[1,96]{1,0:T(1,128)} %param.7) | copy-start | bytes 1156
  46.0 14.7 %collective-permute-start.4 = (f32[3,8,1,128]{3,2,1,0:T(1,128)S(1)}, f32[3,8,1,128]{3,2,1,0:T(1,128)S(1)}, u32[]{:S(2)}, u32[]{:S(2)}) collective-permute-start(f32[3,8,1,128]{3,2,1,0:T(1,128)S(1)} %get-tuple-element.46), channel_id=1, source_target_pairs={{64,0},{128,64},{192,128},{256,192},{320,256},{384,320},{448,384},... | collective-permute-start | bytes 36872 | tf_op jit(solution)/shard_map/ppermute | solution.py:22
  50.0 10.8 %collective-permute-start.5 = (f32[3,8,1,128]{3,2,1,0:T(1,128)S(1)}, f32[3,8,1,128]{3,2,1,0:T(1,128)S(1)}, u32[]{:S(2)}, u32[]{:S(2)}) collective-permute-start(f32[3,8,1,128]{3,2,1,0:T(1,128)S(1)} %get-tuple-element.47), channel_id=1, source_target_pairs={{0,64},{64,128},{128,192},{192,256},{256,320},{320,384},{384,448},... | collective-permute-start | bytes 36872 | tf_op jit(solution)/shard_map/ppermute | solution.py:20
  54.9 6.8 %collective-permute-start.6 = (f32[3,8,8,1]{3,2,1,0:T(8,128)S(1)}, f32[3,8,8,1]{3,2,1,0:T(8,128)S(1)}, u32[]{:S(2)}, u32[]{:S(2)}) collective-permute-start(f32[3,8,8,1]{3,2,1,0:T(8,128)S(1)} %get-tuple-element.54), channel_id=1, source_target_pairs={{1,0},{2,1},{3,2},{4,3},{5,4},{6,5},{7,6},{8,7},{9,8},{10,9},{11,1... | collective-permute-start | bytes 2312 | tf_op jit(solution)/shard_map/ppermute | solution.py:22
  56.8 20.3 %collective-permute-start.7 = (f32[3,8,8,1]{3,2,1,0:T(8,128)S(1)}, f32[3,8,8,1]{3,2,1,0:T(8,128)S(1)}, u32[]{:S(2)}, u32[]{:S(2)}) collective-permute-start(f32[3,8,8,1]{3,2,1,0:T(8,128)S(1)} %get-tuple-element.55), channel_id=1, source_target_pairs={{0,1},{1,2},{2,3},{3,4},{4,5},{5,6},{6,7},{7,8},{8,9},{9,10},{10,1... | collective-permute-start | bytes 2312 | tf_op jit(solution)/shard_map/ppermute | solution.py:20
  77.7 11.1 %collective-permute-start.8 = (f32[3,8,1,128]{3,2,1,0:T(1,128)S(1)}, f32[3,8,1,128]{3,2,1,0:T(1,128)S(1)}, u32[]{:S(2)}, u32[]{:S(2)}) collective-permute-start(f32[3,8,1,128]{3,2,1,0:T(1,128)S(1)} %get-tuple-element.34), channel_id=1, source_target_pairs={{64,0},{128,64},{192,128},{256,192},{320,256},{384,320},{448,384},... | collective-permute-start | bytes 36872 | tf_op jit(solution)/shard_map/ppermute | solution.py:22
  79.6 9.1 %collective-permute-start.9 = (f32[3,8,1,128]{3,2,1,0:T(1,128)S(1)}, f32[3,8,1,128]{3,2,1,0:T(1,128)S(1)}, u32[]{:S(2)}, u32[]{:S(2)}) collective-permute-start(f32[3,8,1,128]{3,2,1,0:T(1,128)S(1)} %get-tuple-element.35), channel_id=1, source_target_pairs={{0,64},{64,128},{128,192},{192,256},{256,320},{320,384},{384,448},... | collective-permute-start | bytes 36872 | tf_op jit(solution)/shard_map/ppermute | solution.py:20
  82.9 6.8 %collective-permute-start.10 = (f32[3,8,8,1]{3,2,1,0:T(8,128)S(1)}, f32[3,8,8,1]{3,2,1,0:T(8,128)S(1)}, u32[]{:S(2)}, u32[]{:S(2)}) collective-permute-start(f32[3,8,8,1]{3,2,1,0:T(8,128)S(1)} %get-tuple-element.42), channel_id=1, source_target_pairs={{1,0},{2,1},{3,2},{4,3},{5,4},{6,5},{7,6},{8,7},{9,8},{10,9},{11,1... | collective-permute-start | bytes 2312 | tf_op jit(solution)/shard_map/ppermute | solution.py:22
  84.8 19.0 %collective-permute-start.11 = (f32[3,8,8,1]{3,2,1,0:T(8,128)S(1)}, f32[3,8,8,1]{3,2,1,0:T(8,128)S(1)}, u32[]{:S(2)}, u32[]{:S(2)}) collective-permute-start(f32[3,8,8,1]{3,2,1,0:T(8,128)S(1)} %get-tuple-element.43), channel_id=1, source_target_pairs={{0,1},{1,2},{2,3},{3,4},{4,5},{5,6},{6,7},{7,8},{8,9},{9,10},{10,1... | collective-permute-start | bytes 2312 | tf_op jit(solution)/shard_map/ppermute | solution.py:20
  104.8 22.3 %all-to-all-start = ((f32[3,64,128]{2,0,1:T(4,128)}), f32[3,64,128]{2,0,1:T(4,128)S(1)}, u32[]{:S(2)}, u32[]{:S(2)}) async-start(f32[3,64,128]{2,0,1:T(4,128)} %bitcast), calls=%async_computation | async-start | bytes 262144 | tf_op jit(solution)/shard_map/all_to_all | solution.py:66
where the time goes:
time: 211 us; the launch traced here: 210 us
  waiting for transfers between devices  58.3 us (28%)
  starting transfers between devices  55.9 us (26%)
  other arithmetic  44.6 us (21%)
  local copies, waits for them, and re-layouts  29.5 us (14%)
  blocking collectives  21.1 us (10%)
    ppermute x6, waiting for transfers between devices, with_halo(): lax.ppermute(tail, axis, [(i, (i + 1) % count) for i in range(ends)])  40.2 us
    unnamed x1, other arithmetic  38.5 us
    ppermute x6, starting transfers between devices, with_halo(): lax.ppermute(head, axis, [((i + 1) % count, i) for i in range(ends)])  31 us
    all_to_all x1, blocking collectives, body(): lax.all_to_all(moved, 'azi', split_axis=2, concat_axis=1, tiled=True)  21.1 us
    ppermute x6, starting transfers between devices, with_halo(): lax.ppermute(tail, axis, [(i, (i + 1) % count) for i in range(ends)])  20.3 us
    all_to_all x1, waiting for transfers between devices, body(): part = lax.all_to_all(rows, 'azi', split_axis=1, concat_axis=2, tiled=True)  16.3 us
    unnamed x9, local copies, waits for them, and re-layouts  12.6 us
    dynamic_slice x1, local copies, waits for them, and re-layouts, roll_row(): return lax.dynamic_slice_in_dim(row_pair, offset, cycle, 1)  6.42 us
  transfers between devices with their start and end apart: 13, of which 6 were waited for; matrix products, arithmetic and copies ran while one was open for 3% of the time, Pallas kernels for 0%

commit v1 on v0

v1 whole, which is shorter than its diff:
```python
import jax
import jax.numpy as jnp
from jax import lax
from jax.sharding import PartitionSpec as P

BLOCK = 64
HALO = 3


time_step = 0.3


def exchange_halo(cells, width):
    n_r = lax.axis_size("rad")
    n_a = lax.axis_size("azi")
    both = ("rad", "azi")

    def lin(r, a):
        return r * n_a + a

    up = [(i, i + 1) for i in range(n_r - 1)]
    down = [(i + 1, i) for i in range(n_r - 1)]
    fwd = [(i, (i + 1) % n_a) for i in range(n_a)]
    back = [((i + 1) % n_a, i) for i in range(n_a)]

    def diag(pairs_r, pairs_a):
        return [(lin(r0, a0), lin(r1, a1)) for r0, r1 in pairs_r for a0, a1 in pairs_a]

    top = cells[:, :width, :]
    bottom = cells[:, -width:, :]
    south = lax.ppermute(bottom, "rad", up)
    north = lax.ppermute(top, "rad", down)
    behind = lax.ppermute(cells[:, :, -width:], "azi", fwd)
    ahead = lax.ppermute(cells[:, :, :width], "azi", back)
    south_behind = lax.ppermute(bottom[:, :, -width:], both, diag(up, fwd))
    south_ahead = lax.ppermute(bottom[:, :, :width], both, diag(up, back))
    north_behind = lax.ppermute(top[:, :, -width:], both, diag(down, fwd))
    north_ahead = lax.ppermute(top[:, :, :width], both, diag(down, back))
    rows_south = jnp.concatenate([south_behind, south, south_ahead], axis=2)
    rows_mid = jnp.concatenate([behind, cells, ahead], axis=2)
    rows_north = jnp.concatenate([north_behind, north, north_ahead], axis=2)
    return jnp.concatenate([rows_south, rows_mid, rows_north], axis=1)


def rates(state, viscosity, spin):
    centre = state[:, :, 1:-1, 1:-1]
    north = state[:, :, 2:, 1:-1]
    south = state[:, :, :-2, 1:-1]
    ahead = state[:, :, 1:-1, 2:]
    behind = state[:, :, 1:-1, :-2]
    above = jnp.concatenate([centre[:, 1:], centre[:, -1:]], axis=1)
    below = jnp.concatenate([centre[:, :1], centre[:, :-1]], axis=1)
    spread = viscosity * (north + south + ahead + behind + above + below - 6.0 * centre)
    radial_grad = 0.5 * (north - south)
    azimuth_grad = 0.5 * (ahead - behind)
    rate_density = spread[0] - radial_grad[1] - azimuth_grad[2]
    rate_radial = spread[1] - radial_grad[0] + 2.0 * spin * centre[2]
    rate_azimuth = spread[2] - azimuth_grad[0] - 0.5 * spin * centre[1]
    return jnp.stack([rate_density, rate_radial, rate_azimuth])


def advect(state, shift_row, first_row):
    fields, heights, radii, cells = state.shape
    lines = jnp.swapaxes(state.reshape(fields, heights * radii, cells), 0, 1)
    ring = lax.all_to_all(lines, "azi", 0, 0, tiled=True)
    chunks = ring.shape[0]
    me = lax.axis_index("azi")
    shift = lax.dynamic_index_in_dim(shift_row, first_row + me % radii, keepdims=False)
    per_chunk = cells // BLOCK
    count = chunks * per_chunk
    shift = shift % count
    whole = shift // per_chunk
    part = shift % per_chunk
    doubled = jnp.concatenate([ring, ring], axis=0)
    lane = lax.broadcasted_iota(jnp.int32, ring.shape, 2)
    base = lax.dynamic_slice_in_dim(doubled, (chunks - whole) % chunks, chunks, 0)
    earlier = lax.dynamic_slice_in_dim(doubled, (chunks - whole - 1) % chunks, chunks, 0)
    rolled = base
    for step in range(1, per_chunk):
        mixed = jnp.roll(jnp.where(lane < cells - step * BLOCK, base, earlier), step * BLOCK, axis=2)
        rolled = jnp.where(part == step, mixed, rolled)
    back = lax.all_to_all(rolled, "azi", 0, 0, tiled=True)
    return jnp.swapaxes(back, 0, 1).reshape(fields, heights, radii, cells)


def body(fields, viscosity, rotation, shift_blocks):
    n_f, heights, radii, cells = fields.shape
    w = HALO
    band = lax.axis_index("rad")
    first_row = band * radii
    total_rows = rotation.shape[0]
    packed = jnp.concatenate([fields.reshape(n_f * heights, radii, cells), viscosity[None]], axis=0)
    ext = exchange_halo(packed, w)
    u0 = ext[: n_f * heights].reshape(n_f, heights, radii + 2 * w, cells + 2 * w)
    visc = ext[n_f * heights]
    rot = jnp.concatenate([jnp.zeros((w,), rotation.dtype), rotation, jnp.zeros((w,), rotation.dtype)])
    spin = lax.dynamic_slice_in_dim(rot, first_row, radii + 2 * w)[:, None]
    row = first_row - w + lax.iota(jnp.int32, radii + 2 * w)
    inside = ((row >= 0) & (row < total_rows))[:, None]

    def trim(x, k):
        return x[..., k : x.shape[-2] - k, k : x.shape[-1] - k]

    def rates_at(state, k):
        return rates(state, trim(visc, k), spin[k : spin.shape[0] - k])

    def keep(state, k):
        return jnp.where(inside[k : inside.shape[0] - k], state, 0.0)

    state = u0
    first = keep(trim(state, 1) + time_step * rates_at(state, 1), 1)
    second = keep(0.75 * trim(state, 2) + 0.25 * (trim(first, 1) + time_step * rates_at(first, 2)), 2)
    state = trim(state, 3) / 3.0 + 2.0 / 3.0 * (trim(second, 1) + time_step * rates_at(second, 3))
    for t in range(shift_blocks.shape[0]):
        state = advect(state, shift_blocks[t], first_row)
    return state


def solution(mesh):
    return jax.shard_map(
        body,
        mesh=mesh,
        in_specs=(P(None, None, "rad", "azi"), P("rad", "azi"), P(), P()),
        out_specs=P(None, None, "rad", "azi"),
        check_vma=False,
    )
```

time: 211 us -> 131 us (0.62)
  other arithmetic: 44.6 us -> 2.79 us
  waiting for transfers between devices: 58.3 us -> 24.4 us
  local copies, waits for them, and re-layouts: 29.5 us -> 5.26 us
  starting transfers between devices: 55.9 us -> 73.4 us
    unnamed x1 -> x0, other arithmetic: 38.5 us -> none
    ppermute x12 -> x8, waiting for transfers between devices: 42 us -> 9.16 us  [the longest x1 7.69 us: exchange_halo(): behind = lax.ppermute(cells[:, :, -width:], 'azi', fwd)]
    all_to_all x1, starting transfers between devices: 4.6 us -> 15.6 us  [advect(): ring = lax.all_to_all(lines, 'azi', 0, 0, tiled=True)]
    unnamed x9, local copies, waits for them, and re-layouts: 12.6 us -> 1.61 us
    ppermute x12 -> x8, starting transfers between devices: 51.3 us -> 57.8 us  [the longest x1 16.9 us: exchange_halo(): south_ahead = lax.ppermute(bottom[:, :, :width], both, diag(up, back))]
    dynamic_slice x1 -> x2, local copies, waits for them, and re-layouts: 6.42 us -> 0.66 us  [the longest x1 0.59 us: advect(): lax.dynamic_index_in_dim(shift_row, first_row + me % radii, keepdims=False)]
    slice x18 -> x12, local copies, waits for them, and re-layouts: 6.3 us -> 1.54 us  [the longest x6 1.04 us: rates(): below = jnp.concatenate([centre[:, :1], centre[:, :-1]], axis=1)]
    reshape x1 -> x2, local copies, waits for them, and re-layouts: 3.47 us -> 0.67 us  [the longest x1 0.65 us: advect(): return jnp.swapaxes(back, 0, 1).reshape(fields, heights, radii, cells)]
  transfers between devices with their start and end apart: 13 -> 9, of which waited for: 6 -> 3; matrix products, arithmetic and copies ran while one was open for 3% -> 1% of each run, Pallas kernels for 0% -> 0%
where the time goes in v1:
time: 131 us; the launch traced here: 130 us
  starting transfers between devices  73.4 us (56%)
  waiting for transfers between devices  24.4 us (19%)
  blocking collectives  22 us (17%)
  local copies, waits for them, and re-layouts  5.26 us (4%)
  other arithmetic  2.79 us (2%)
  between operations  2.39 us (2%)
    all_to_all x1, blocking collectives, advect(): back = lax.all_to_all(rolled, 'azi', 0, 0, tiled=True)  22 us
    ppermute x1, starting transfers between devices, exchange_halo(): south_ahead = lax.ppermute(bottom[:, :, :width], both, diag(up, back))  16.9 us
    all_to_all x1, starting transfers between devices, advect(): ring = lax.all_to_all(lines, 'azi', 0, 0, tiled=True)  15.6 us
    all_to_all x1, waiting for transfers between devices, advect(): ring = lax.all_to_all(lines, 'azi', 0, 0, tiled=True)  15.2 us
    ppermute x1, starting transfers between devices, exchange_halo(): ahead = lax.ppermute(cells[:, :, :width], 'azi', back)  14.5 us
    ppermute x1, starting transfers between devices, exchange_halo(): north_ahead = lax.ppermute(top[:, :, :width], both, diag(down, back))  13.3 us
    ppermute x1, waiting for transfers between devices, exchange_halo(): behind = lax.ppermute(cells[:, :, -width:], 'azi', fwd)  7.69 us
    ppermute x1, starting transfers between devices, exchange_halo(): south_behind = lax.ppermute(bottom[:, :, -width:], both, diag(up, fwd))  3.84 us
  transfers between devices with their start and end apart: 9, of which 3 were waited for; matrix products, arithmetic and copies ran while one was open for 1% of the time, Pallas kernels for 0%

profile of v1, /device:TPU:64, one launch (start us, length us, event | category | flops | bytes accessed | tf_op | source)
XLA Modules:
  0.0 130.3 jit_solution(12323706845804363559)
XLA Ops:
  0.0 0.9 copy.17
  1.0 1.9 %collective-permute-start.1 = (f32[25,3,128]{2,0,1:T(8,128)S(1)}, f32[25,3,128]{2,0,1:T(8,128)S(1)}, u32[]{:S(2)}, u32[]{:S(2)}) collective-permute-start(f32[25,3,128]{2,0,1:T(8,128)S(1)} %get-tuple-element.41), channel_id=1, source_target_pairs={{0,64},{64,128},{128,192},{192,256},{256,320},{320,384},{384,448},... | collective-permute-start | bytes 115208 | tf_op jit(solution)/shard_map/ppermute | solution.py:31
  2.9 3.6 %collective-permute-start.6 = (f32[25,3,128]{2,0,1:T(8,128)S(1)}, f32[25,3,128]{2,0,1:T(8,128)S(1)}, u32[]{:S(2)}, u32[]{:S(2)}) collective-permute-start(f32[25,3,128]{2,0,1:T(8,128)S(1)} %get-tuple-element.42), channel_id=1, source_target_pairs={{64,0},{128,64},{192,128},{256,192},{320,256},{384,320},{448,384},... | collective-permute-start | bytes 115208 | tf_op jit(solution)/shard_map/ppermute | solution.py:32
  6.6 3.8 %collective-permute-start = (f32[25,3,3]{2,0,1:T(8,128)S(1)}, f32[25,3,3]{2,0,1:T(8,128)S(1)}, u32[]{:S(2)}, u32[]{:S(2)}) collective-permute-start(f32[25,3,3]{2,0,1:T(8,128)S(1)} %get-tuple-element.37), channel_id=1, source_target_pairs={{0,65},{1,66},{2,67},{3,68},{4,69},{5,70},{6,71},{7,72},{8,73},{9,... | collective-permute-start | bytes 2708 | tf_op jit(solution)/shard_map/ppermute | solution.py:35
  10.5 16.9 %collective-permute-start.2 = (f32[25,3,3]{2,0,1:T(8,128)S(1)}, f32[25,3,3]{2,0,1:T(8,128)S(1)}, u32[]{:S(2)}, u32[]{:S(2)}) collective-permute-start(f32[25,3,3]{2,0,1:T(8,128)S(1)} %get-tuple-element.38), channel_id=1, source_target_pairs={{1,64},{2,65},{3,66},{4,67},{5,68},{6,69},{7,70},{8,71},{9,72},{10... | collective-permute-start | bytes 2708 | tf_op jit(solution)/shard_map/ppermute | solution.py:36
  27.4 1.9 %collective-permute-start.5 = (f32[25,3,3]{2,0,1:T(8,128)S(1)}, f32[25,3,3]{2,0,1:T(8,128)S(1)}, u32[]{:S(2)}, u32[]{:S(2)}) collective-permute-start(f32[25,3,3]{2,0,1:T(8,128)S(1)} %get-tuple-element.39), channel_id=1, source_target_pairs={{64,1},{65,2},{66,3},{67,4},{68,5},{69,6},{70,7},{71,8},{72,9},{73... | collective-permute-start | bytes 2708 | tf_op jit(solution)/shard_map/ppermute | solution.py:37
  29.3 0.6 copy-done.2
  30.5 13.3 %collective-permute-start.7 = (f32[25,3,3]{2,0,1:T(8,128)S(1)}, f32[25,3,3]{2,0,1:T(8,128)S(1)}, u32[]{:S(2)}, u32[]{:S(2)}) collective-permute-start(f32[25,3,3]{2,0,1:T(8,128)S(1)} %get-tuple-element.40), channel_id=1, source_target_pairs={{65,0},{66,1},{67,2},{68,3},{69,4},{70,5},{71,6},{72,7},{73,8},{74... | collective-permute-start | bytes 2708 | tf_op jit(solution)/shard_map/ppermute | solution.py:38
  43.7 1.9 %collective-permute-start.3 = (f32[25,8,3]{2,0,1:T(8,128)S(1)}, f32[25,8,3]{2,0,1:T(8,128)S(1)}, u32[]{:S(2)}, u32[]{:S(2)}) collective-permute-start(f32[25,8,3]{2,0,1:T(8,128)S(1)} %get-tuple-element.43), channel_id=1, source_target_pairs={{0,1},{1,2},{2,3},{3,4},{4,5},{5,6},{6,7},{7,8},{8,9},{9,10},{10,1... | collective-permute-start | bytes 7208 | tf_op jit(solution)/shard_map/ppermute | solution.py:33
  45.7 14.5 %collective-permute-start.4 = (f32[25,8,3]{2,0,1:T(8,128)S(1)}, f32[25,8,3]{2,0,1:T(8,128)S(1)}, u32[]{:S(2)}, u32[]{:S(2)}) collective-permute-start(f32[25,8,3]{2,0,1:T(8,128)S(1)} %get-tuple-element.44), channel_id=1, source_target_pairs={{1,0},{2,1},{3,2},{4,3},{5,4},{6,5},{7,6},{8,7},{9,8},{10,9},{11,1... | collective-permute-start | bytes 7208 | tf_op jit(solution)/shard_map/ppermute | solution.py:34
  60.3 7.7 %collective-permute-done.3 = f32[25,8,3]{2,0,1:T(8,128)S(1)} collective-permute-done((f32[25,8,3]{2,0,1:T(8,128)S(1)}, f32[25,8,3]{2,0,1:T(8,128)S(1)}, u32[]{:S(2)}, u32[]{:S(2)}) %collective-permute-start.3) | collective-permute-done | bytes 2432 | tf_op jit(solution)/shard_map/ppermute | solution.py:33
  68.0 1.5 %collective-permute-done.4 = f32[25,8,3]{2,0,1:T(8,128)S(1)} collective-permute-done((f32[25,8,3]{2,0,1:T(8,128)S(1)}, f32[25,8,3]{2,0,1:T(8,128)S(1)}, u32[]{:S(2)}, u32[]{:S(2)}) %collective-permute-start.4) | collective-permute-done | bytes 2432 | tf_op jit(solution)/shard_map/ppermute | solution.py:34
  69.8 0.2 maximum_maximum_fusion
  70.1 0.2 fusion.31
  70.3 0.2 fusion.32
  70.5 0.4 subtract_multiply_fusion.1
  70.9 0.1 fusion.15
  71.1 0.2 fusion.4
  71.2 0.2 fusion.33
  71.4 0.2 fusion.34
  71.6 0.3 subtract_multiply_fusion.3
  72.0 0.1 fusion.23
  72.1 0.2 fusion.6
  72.6 0.2 subtract_multiply_fusion.5
  73.0 0.7 copy.10
  73.7 15.6 %all-to-all-start = ((f32[64,3,128]{2,1,0:T(4,128)}), f32[64,3,128]{2,1,0:T(4,128)S(1)}, u32[]{:S(2)}, u32[]{:S(2)}) async-start(f32[64,3,128]{2,1,0:T(4,128)} %copy.10), calls=%async_computation | async-start | bytes 262144 | tf_op jit(solution)/shard_map/all_to_all | solution.py:65
  89.4 0.6 constant_dynamic-slice_fusion
  92.0 15.2 %all-to-all-done = f32[64,3,128]{2,1,0:T(4,128)S(1)} async-done(((f32[64,3,128]{2,1,0:T(4,128)}), f32[64,3,128]{2,1,0:T(4,128)S(1)}, u32[]{:S(2)}, u32[]{:S(2)}) %all-to-all-start) | async-done | bytes 98336 | tf_op jit(solution)/shard_map/all_to_all | solution.py:65
  107.3 0.1 fusion.37
  107.4 0.1 maximum_select_fusion
  107.6 22.0 %all_to_all.10 = f32[64,3,128]{2,1,0:T(4,128)S(1)} all-to-all(f32[64,3,128]{2,1,0:T(4,128)S(1)} %maximum_select_fusion), channel_id=1, replica_groups=mesh['rad'=12,'azi'=64] {'azi'}, dimensions={0} | all-to-all | bytes 196608 | tf_op jit(solution)/shard_map/all_to_all | solution.py:82
  129.6 0.6 copy.11
  (38 shorter events, 1.7 us)
Async XLA Ops:
  0.0 89.3 %copy-start = (s32[1,96]{1,0:T(1,128)S(1)}, s32[1,96]{1,0:T(1,128)}, u32[]{:S(2)}) copy-start(s32[1,96]{1,0:T(1,128)} %param.7) | copy-start | bytes 1156
  0.0 0.9 copy-start.1
  1.0 68.5 %collective-permute-start.1 = (f32[25,3,128]{2,0,1:T(8,128)S(1)}, f32[25,3,128]{2,0,1:T(8,128)S(1)}, u32[]{:S(2)}, u32[]{:S(2)}) collective-permute-start(f32[25,3,128]{2,0,1:T(8,128)S(1)} %get-tuple-element.41), channel_id=1, source_target_pairs={{0,64},{64,128},{128,192},{192,256},{256,320},{320,384},{384,448},... | collective-permute-start | bytes 115208 | tf_op jit(solution)/shard_map/ppermute | solution.py:31
  2.9 66.6 %collective-permute-start.6 = (f32[25,3,128]{2,0,1:T(8,128)S(1)}, f32[25,3,128]{2,0,1:T(8,128)S(1)}, u32[]{:S(2)}, u32[]{:S(2)}) collective-permute-start(f32[25,3,128]{2,0,1:T(8,128)S(1)} %get-tuple-element.42), channel_id=1, source_target_pairs={{64,0},{128,64},{192,128},{256,192},{320,256},{384,320},{448,384},... | collective-permute-start | bytes 115208 | tf_op jit(solution)/shard_map/ppermute | solution.py:32
  6.6 23.8 %collective-permute-start = (f32[25,3,3]{2,0,1:T(8,128)S(1)}, f32[25,3,3]{2,0,1:T(8,128)S(1)}, u32[]{:S(2)}, u32[]{:S(2)}) collective-permute-start(f32[25,3,3]{2,0,1:T(8,128)S(1)} %get-tuple-element.37), channel_id=1, source_target_pairs={{0,65},{1,66},{2,67},{3,68},{4,69},{5,70},{6,71},{7,72},{8,73},{9,... | collective-permute-start | bytes 2708 | tf_op jit(solution)/shard_map/ppermute | solution.py:35
  10.5 33.2 %collective-permute-start.2 = (f32[25,3,3]{2,0,1:T(8,128)S(1)}, f32[25,3,3]{2,0,1:T(8,128)S(1)}, u32[]{:S(2)}, u32[]{:S(2)}) collective-permute-start(f32[25,3,3]{2,0,1:T(8,128)S(1)} %get-tuple-element.38), channel_id=1, source_target_pairs={{1,64},{2,65},{3,66},{4,67},{5,68},{6,69},{7,70},{8,71},{9,72},{10... | collective-permute-start | bytes 2708 | tf_op jit(solution)/shard_map/ppermute | solution.py:36
  27.4 18.3 %collective-permute-start.5 = (f32[25,3,3]{2,0,1:T(8,128)S(1)}, f32[25,3,3]{2,0,1:T(8,128)S(1)}, u32[]{:S(2)}, u32[]{:S(2)}) collective-permute-start(f32[25,3,3]{2,0,1:T(8,128)S(1)} %get-tuple-element.39), channel_id=1, source_target_pairs={{64,1},{65,2},{66,3},{67,4},{68,5},{69,6},{70,7},{71,8},{72,9},{73... | collective-permute-start | bytes 2708 | tf_op jit(solution)/shard_map/ppermute | solution.py:37
  29.3 0.7 copy-start.2
  30.5 29.8 %collective-permute-start.7 = (f32[25,3,3]{2,0,1:T(8,128)S(1)}, f32[25,3,3]{2,0,1:T(8,128)S(1)}, u32[]{:S(2)}, u32[]{:S(2)}) collective-permute-start(f32[25,3,3]{2,0,1:T(8,128)S(1)} %get-tuple-element.40), channel_id=1, source_target_pairs={{65,0},{66,1},{67,2},{68,3},{69,4},{70,5},{71,6},{72,7},{73,8},{74... | collective-permute-start | bytes 2708 | tf_op jit(solution)/shard_map/ppermute | solution.py:38
  43.7 24.3 %collective-permute-start.3 = (f32[25,8,3]{2,0,1:T(8,128)S(1)}, f32[25,8,3]{2,0,1:T(8,128)S(1)}, u32[]{:S(2)}, u32[]{:S(2)}) collective-permute-start(f32[25,8,3]{2,0,1:T(8,128)S(1)} %get-tuple-element.43), channel_id=1, source_target_pairs={{0,1},{1,2},{2,3},{3,4},{4,5},{5,6},{6,7},{7,8},{8,9},{9,10},{10,1... | collective-permute-start | bytes 7208 | tf_op jit(solution)/shard_map/ppermute | solution.py:33
  45.7 23.8 %collective-permute-start.4 = (f32[25,8,3]{2,0,1:T(8,128)S(1)}, f32[25,8,3]{2,0,1:T(8,128)S(1)}, u32[]{:S(2)}, u32[]{:S(2)}) collective-permute-start(f32[25,8,3]{2,0,1:T(8,128)S(1)} %get-tuple-element.44), channel_id=1, source_target_pairs={{1,0},{2,1},{3,2},{4,3},{5,4},{6,5},{7,6},{8,7},{9,8},{10,9},{11,1... | collective-permute-start | bytes 7208 | tf_op jit(solution)/shard_map/ppermute | solution.py:34
  73.7 33.4 %all-to-all-start = ((f32[64,3,128]{2,1,0:T(4,128)}), f32[64,3,128]{2,1,0:T(4,128)S(1)}, u32[]{:S(2)}, u32[]{:S(2)}) async-start(f32[64,3,128]{2,1,0:T(4,128)} %copy.10), calls=%async_computation | async-start | bytes 262144 | tf_op jit(solution)/shard_map/all_to_all | solution.py:65

commit v2 on v1

--- a/solution.py
+++ b/solution.py
@@ -13,33 +13,16 @@
 def exchange_halo(cells, width):
     n_r = lax.axis_size("rad")
     n_a = lax.axis_size("azi")
-    both = ("rad", "azi")
-
-    def lin(r, a):
-        return r * n_a + a
-
     up = [(i, i + 1) for i in range(n_r - 1)]
     down = [(i + 1, i) for i in range(n_r - 1)]
     fwd = [(i, (i + 1) % n_a) for i in range(n_a)]
     back = [((i + 1) % n_a, i) for i in range(n_a)]
-
-    def diag(pairs_r, pairs_a):
-        return [(lin(r0, a0), lin(r1, a1)) for r0, r1 in pairs_r for a0, a1 in pairs_a]
-
-    top = cells[:, :width, :]
-    bottom = cells[:, -width:, :]
-    south = lax.ppermute(bottom, "rad", up)
-    north = lax.ppermute(top, "rad", down)
     behind = lax.ppermute(cells[:, :, -width:], "azi", fwd)
     ahead = lax.ppermute(cells[:, :, :width], "azi", back)
-    south_behind = lax.ppermute(bottom[:, :, -width:], both, diag(up, fwd))
-    south_ahead = lax.ppermute(bottom[:, :, :width], both, diag(up, back))
-    north_behind = lax.ppermute(top[:, :, -width:], both, diag(down, fwd))
-    north_ahead = lax.ppermute(top[:, :, :width], both, diag(down, back))
-    rows_south = jnp.concatenate([south_behind, south, south_ahead], axis=2)
-    rows_mid = jnp.concatenate([behind, cells, ahead], axis=2)
-    rows_north = jnp.concatenate([north_behind, north, north_ahead], axis=2)
-    return jnp.concatenate([rows_south, rows_mid, rows_north], axis=1)
+    wide = jnp.concatenate([behind, cells, ahead], axis=2)
+    south = lax.ppermute(wide[:, -width:, :], "rad", up)
+    north = lax.ppermute(wide[:, :width, :], "rad", down)
+    return jnp.concatenate([south, wide, north], axis=1)
 
 
 def rates(state, viscosity, spin):

time: 131 us -> 98.9 us (0.75)
  the two profiles are of different devices: /device:TPU:64 before, /device:TPU:1 now
where the time goes in v2:
time: 98.9 us; the launch traced here: 98.5 us
  starting transfers between devices  49.9 us (50%)
  blocking collectives  20 us (20%)
  waiting for transfers between devices  18.3 us (19%)
  local copies, waits for them, and re-layouts  5.26 us (5%)
  other arithmetic  2.74 us (3%)
  between operations  2.32 us (2%)
    all_to_all x1, blocking collectives, advect(): back = lax.all_to_all(rolled, 'azi', 0, 0, tiled=True)  20 us
    ppermute x1, starting transfers between devices, exchange_halo(): ahead = lax.ppermute(cells[:, :, :width], 'azi', back)  18.7 us
    all_to_all x1, starting transfers between devices, advect(): ring = lax.all_to_all(lines, 'azi', 0, 0, tiled=True)  15.7 us
    all_to_all x1, waiting for transfers between devices, advect(): ring = lax.all_to_all(lines, 'azi', 0, 0, tiled=True)  13.5 us
    ppermute x1, starting transfers between devices, exchange_halo(): south = lax.ppermute(wide[:, -width:, :], 'rad', up)  9.53 us
    ppermute x1, starting transfers between devices, exchange_halo(): behind = lax.ppermute(cells[:, :, -width:], 'azi', fwd)  4.03 us
    ppermute x1, waiting for transfers between devices, exchange_halo(): north = lax.ppermute(wide[:, :width, :], 'rad', down)  3.84 us
  transfers between devices with their start and end apart: 5, of which 3 were waited for; matrix products, arithmetic and copies ran while one was open for 1% of the time, Pallas kernels for 0%

profile of v2, /device:TPU:1, one launch (start us, length us, event | category | flops | bytes accessed | tf_op | source)
XLA Modules:
  0.0 98.5 jit_solution(16177360161615970315)
XLA Ops:
  0.0 0.9 copy.17
  1.1 4.0 %collective-permute-start = (f32[25,8,3]{2,0,1:T(8,128)S(1)}, f32[25,8,3]{2,0,1:T(8,128)S(1)}, u32[]{:S(2)}, u32[]{:S(2)}) collective-permute-start(f32[25,8,3]{2,0,1:T(8,128)S(1)} %get-tuple-element.39), channel_id=1, source_target_pairs={{0,1},{1,2},{2,3},{3,4},{4,5},{5,6},{6,7},{7,8},{8,9},{9,10},{10,1... | collective-permute-start | bytes 7208 | tf_op jit(solution)/shard_map/ppermute | solution.py:20
  5.1 18.7 %collective-permute-start.1 = (f32[25,8,3]{2,0,1:T(8,128)S(1)}, f32[25,8,3]{2,0,1:T(8,128)S(1)}, u32[]{:S(2)}, u32[]{:S(2)}) collective-permute-start(f32[25,8,3]{2,0,1:T(8,128)S(1)} %get-tuple-element.40), channel_id=1, source_target_pairs={{1,0},{2,1},{3,2},{4,3},{5,4},{6,5},{7,6},{8,7},{9,8},{10,9},{11,1... | collective-permute-start | bytes 7208 | tf_op jit(solution)/shard_map/ppermute | solution.py:21
  23.8 0.6 copy-done.2
  24.8 0.9 collective-permute-done.1
  25.7 0.1 pad_maximum_fusion.5
  25.9 9.5 %collective-permute-start.2 = (f32[25,3,134]{2,0,1:T(8,128)S(1)}, f32[25,3,134]{2,0,1:T(8,128)S(1)}, u32[]{:S(2)}, u32[]{:S(2)}) collective-permute-start(f32[25,3,134]{2,0,1:T(8,128)S(1)} %get-tuple-element.11), channel_id=1, source_target_pairs={{0,64},{64,128},{128,192},{192,256},{256,320},{320,384},{384,448},... | collective-permute-start | bytes 120608 | tf_op jit(solution)/shard_map/ppermute | solution.py:23
  35.4 1.9 %collective-permute-start.3 = (f32[25,3,134]{2,0,1:T(8,128)S(1)}, f32[25,3,134]{2,0,1:T(8,128)S(1)}, u32[]{:S(2)}, u32[]{:S(2)}) collective-permute-start(f32[25,3,134]{2,0,1:T(8,128)S(1)} %get-tuple-element.12), channel_id=1, source_target_pairs={{64,0},{128,64},{192,128},{256,192},{320,256},{384,320},{448,384},... | collective-permute-start | bytes 120608 | tf_op jit(solution)/shard_map/ppermute | solution.py:24
  37.5 3.8 %collective-permute-done.3 = f32[25,3,134]{2,0,1:T(8,128)S(1)} collective-permute-done((f32[25,3,134]{2,0,1:T(8,128)S(1)}, f32[25,3,134]{2,0,1:T(8,128)S(1)}, u32[]{:S(2)}, u32[]{:S(2)}) %collective-permute-start.3) | collective-permute-done | bytes 40232 | tf_op jit(solution)/shard_map/ppermute | solution.py:24
  41.7 0.2 pad_maximum_fusion
  41.9 0.2 fusion.24
  42.1 0.2 fusion.25
  42.3 0.4 subtract_multiply_fusion.1
  42.7 0.1 fusion.13
  42.9 0.2 fusion.4
  43.0 0.2 fusion.26
  43.2 0.2 fusion.27
  43.4 0.3 subtract_multiply_fusion.3
  43.7 0.1 fusion.21
  43.9 0.2 fusion.6
  44.1 0.1 fusion.28
  44.2 0.1 fusion.29
  44.3 0.2 subtract_multiply_fusion.5
  44.6 0.1 fusion.14
  44.8 0.7 copy.10
  45.5 15.7 %all-to-all-start = ((f32[64,3,128]{2,1,0:T(4,128)}), f32[64,3,128]{2,1,0:T(4,128)S(1)}, u32[]{:S(2)}, u32[]{:S(2)}) async-start(f32[64,3,128]{2,1,0:T(4,128)} %copy.10), calls=%async_computation | async-start | bytes 262144 | tf_op jit(solution)/shard_map/all_to_all | solution.py:48
  61.3 0.6 constant_dynamic-slice_fusion
  63.9 13.5 %all-to-all-done = f32[64,3,128]{2,1,0:T(4,128)S(1)} async-done(((f32[64,3,128]{2,1,0:T(4,128)}), f32[64,3,128]{2,1,0:T(4,128)S(1)}, u32[]{:S(2)}, u32[]{:S(2)}) %all-to-all-start) | async-done | bytes 98336 | tf_op jit(solution)/shard_map/all_to_all | solution.py:48
  77.5 0.1 fusion.30
  77.7 0.1 maximum_select_fusion
  77.8 20.0 %all_to_all.10 = f32[64,3,128]{2,1,0:T(4,128)S(1)} all-to-all(f32[64,3,128]{2,1,0:T(4,128)S(1)} %maximum_select_fusion), channel_id=1, replica_groups=mesh['rad'=12,'azi'=64] {'azi'}, dimensions={0} | all-to-all | bytes 196608 | tf_op jit(solution)/shard_map/all_to_all | solution.py:65
  97.9 0.6 copy.11
  (29 shorter events, 1.2 us)
Async XLA Ops:
  0.0 61.2 %copy-start = (s32[1,96]{1,0:T(1,128)S(1)}, s32[1,96]{1,0:T(1,128)}, u32[]{:S(2)}) copy-start(s32[1,96]{1,0:T(1,128)} %param.7) | copy-start | bytes 1156
  0.0 0.9 copy-start.1
  1.1 23.8 %collective-permute-start = (f32[25,8,3]{2,0,1:T(8,128)S(1)}, f32[25,8,3]{2,0,1:T(8,128)S(1)}, u32[]{:S(2)}, u32[]{:S(2)}) collective-permute-start(f32[25,8,3]{2,0,1:T(8,128)S(1)} %get-tuple-element.39), channel_id=1, source_target_pairs={{0,1},{1,2},{2,3},{3,4},{4,5},{5,6},{6,7},{7,8},{8,9},{9,10},{10,1... | collective-permute-start | bytes 7208 | tf_op jit(solution)/shard_map/ppermute | solution.py:20
  5.1 20.6 %collective-permute-start.1 = (f32[25,8,3]{2,0,1:T(8,128)S(1)}, f32[25,8,3]{2,0,1:T(8,128)S(1)}, u32[]{:S(2)}, u32[]{:S(2)}) collective-permute-start(f32[25,8,3]{2,0,1:T(8,128)S(1)} %get-tuple-element.40), channel_id=1, source_target_pairs={{1,0},{2,1},{3,2},{4,3},{5,4},{6,5},{7,6},{8,7},{9,8},{10,9},{11,1... | collective-permute-start | bytes 7208 | tf_op jit(solution)/shard_map/ppermute | solution.py:21
  23.8 0.7 copy-start.2
  25.9 11.6 %collective-permute-start.2 = (f32[25,3,134]{2,0,1:T(8,128)S(1)}, f32[25,3,134]{2,0,1:T(8,128)S(1)}, u32[]{:S(2)}, u32[]{:S(2)}) collective-permute-start(f32[25,3,134]{2,0,1:T(8,128)S(1)} %get-tuple-element.11), channel_id=1, source_target_pairs={{0,64},{64,128},{128,192},{192,256},{256,320},{320,384},{384,448},... | collective-permute-start | bytes 120608 | tf_op jit(solution)/shard_map/ppermute | solution.py:23
  35.4 5.9 %collective-permute-start.3 = (f32[25,3,134]{2,0,1:T(8,128)S(1)}, f32[25,3,134]{2,0,1:T(8,128)S(1)}, u32[]{:S(2)}, u32[]{:S(2)}) collective-permute-start(f32[25,3,134]{2,0,1:T(8,128)S(1)} %get-tuple-element.12), channel_id=1, source_target_pairs={{64,0},{128,64},{192,128},{256,192},{320,256},{384,320},{448,384},... | collective-permute-start | bytes 120608 | tf_op jit(solution)/shard_map/ppermute | solution.py:24
  45.5 31.9 %all-to-all-start = ((f32[64,3,128]{2,1,0:T(4,128)}), f32[64,3,128]{2,1,0:T(4,128)S(1)}, u32[]{:S(2)}, u32[]{:S(2)}) async-start(f32[64,3,128]{2,1,0:T(4,128)} %copy.10), calls=%async_computation | async-start | bytes 262144 | tf_op jit(solution)/shard_map/all_to_all | solution.py:48

commit v3 on v2

v3 whole, which is shorter than its diff:
```python
import jax
import jax.numpy as jnp
from jax import lax
from jax.sharding import PartitionSpec as P

BLOCK = 64
HALO = 3


time_step = 0.3


def exchange_halo(cells, width):
    n_r = lax.axis_size("rad")
    n_a = lax.axis_size("azi")
    up = [(i, i + 1) for i in range(n_r - 1)]
    down = [(i + 1, i) for i in range(n_r - 1)]
    fwd = [(i, (i + 1) % n_a) for i in range(n_a)]
    back = [((i + 1) % n_a, i) for i in range(n_a)]
    behind = lax.ppermute(cells[:, :, -width:], "azi", fwd)
    ahead = lax.ppermute(cells[:, :, :width], "azi", back)
    wide = jnp.concatenate([behind, cells, ahead], axis=2)
    south = lax.ppermute(wide[:, -width:, :], "rad", up)
    north = lax.ppermute(wide[:, :width, :], "rad", down)
    return jnp.concatenate([south, wide, north], axis=1)


def rates(state, viscosity, spin):
    centre = state[:, :, 1:-1, 1:-1]
    north = state[:, :, 2:, 1:-1]
    south = state[:, :, :-2, 1:-1]
    ahead = state[:, :, 1:-1, 2:]
    behind = state[:, :, 1:-1, :-2]
    above = jnp.concatenate([centre[:, 1:], centre[:, -1:]], axis=1)
    below = jnp.concatenate([centre[:, :1], centre[:, :-1]], axis=1)
    spread = viscosity * (north + south + ahead + behind + above + below - 6.0 * centre)
    radial_grad = 0.5 * (north - south)
    azimuth_grad = 0.5 * (ahead - behind)
    rate_density = spread[0] - radial_grad[1] - azimuth_grad[2]
    rate_radial = spread[1] - radial_grad[0] + 2.0 * spin * centre[2]
    rate_azimuth = spread[2] - azimuth_grad[0] - 0.5 * spin * centre[1]
    return jnp.stack([rate_density, rate_radial, rate_azimuth])


def exchange_rows(cells, width):
    n_r = lax.axis_size("rad")
    up = [(i, i + 1) for i in range(n_r - 1)]
    down = [(i + 1, i) for i in range(n_r - 1)]
    south = lax.ppermute(cells[:, -width:], "rad", up)
    north = lax.ppermute(cells[:, :width], "rad", down)
    return jnp.concatenate([south, cells, north], axis=1)


def rates_ring(state, viscosity, spin):
    centre = state[:, :, 1:-1]
    north = state[:, :, 2:]
    south = state[:, :, :-2]
    ahead = jnp.roll(centre, -1, axis=-1)
    behind = jnp.roll(centre, 1, axis=-1)
    above = jnp.concatenate([centre[:, 1:], centre[:, -1:]], axis=1)
    below = jnp.concatenate([centre[:, :1], centre[:, :-1]], axis=1)
    spread = viscosity * (north + south + ahead + behind + above + below - 6.0 * centre)
    radial_grad = 0.5 * (north - south)
    azimuth_grad = 0.5 * (ahead - behind)
    rate_density = spread[0] - radial_grad[1] - azimuth_grad[2]
    rate_radial = spread[1] - radial_grad[0] + 2.0 * spin * centre[2]
    rate_azimuth = spread[2] - azimuth_grad[0] - 0.5 * spin * centre[1]
    return jnp.stack([rate_density, rate_radial, rate_azimuth])


def runge_kutta(u0, rates_at, keep, trim):
    first = keep(trim(u0, 1) + time_step * rates_at(u0, 1), 1)
    second = keep(0.75 * trim(u0, 2) + 0.25 * (trim(first, 1) + time_step * rates_at(first, 2)), 2)
    return trim(u0, 3) / 3.0 + 2.0 / 3.0 * (trim(second, 1) + time_step * rates_at(second, 3))


def body(fields, viscosity, rotation, shift_blocks):
    n_f, heights, radii, cells = fields.shape
    w = HALO
    edge = 2 * w
    band = lax.axis_index("rad")
    first_row = band * radii
    total_rows = rotation.shape[0]
    planes = n_f * heights
    packed = jnp.concatenate([fields.reshape(planes, radii, cells), viscosity[None]], axis=0)
    rows = exchange_rows(packed, w)
    rot = jnp.concatenate([jnp.zeros((w,), rotation.dtype), rotation, jnp.zeros((w,), rotation.dtype)])

    ext = jnp.pad(rows, ((0, 0), (0, 0), (w, w)))
    u0 = ext[:planes].reshape(n_f, heights, radii + 2 * w, cells + 2 * w)
    visc = ext[planes]
    spin = lax.dynamic_slice_in_dim(rot, first_row, radii + 2 * w)[:, None]
    row = first_row - w + lax.iota(jnp.int32, radii + 2 * w)
    inside = ((row >= 0) & (row < total_rows))[:, None]

    def trim(x, k):
        return x[..., k : x.shape[-2] - k, k : x.shape[-1] - k]

    def rates_at(state, k):
        return rates(state, trim(visc, k), spin[k : spin.shape[0] - k])

    def keep(state, k):
        return jnp.where(inside[k : inside.shape[0] - k], state, 0.0)

    state = runge_kutta(u0, rates_at, keep, trim)

    lines = jnp.swapaxes(state.reshape(n_f, heights * radii, cells), 0, 1)
    chunks = lines.shape[0]
    edges = jnp.concatenate([rows[:, :, :edge], rows[:, :, cells - edge :]], axis=2)
    wins = jnp.stack([edges[:, r : r + 2 * w + 1] for r in range(radii)])
    win_size = wins[0].size
    win_rows = -(-win_size // cells)
    wins = jnp.pad(wins.reshape(radii, win_size), ((0, 0), (0, win_rows * cells - win_size)))
    wins = jnp.tile(wins.reshape(radii, win_rows, cells), (chunks // radii, 1, 1))
    ring = lax.all_to_all(jnp.concatenate([lines, wins], axis=1), "azi", 0, 0, tiled=True)
    line = ring[:, :n_f]
    raw = ring[:, n_f:].reshape(chunks, win_rows * cells)[:, :win_size]
    raw = raw.reshape(chunks, planes + 1, 2 * w + 1, 2 * edge)

    me = lax.axis_index("azi")
    my_h = me // radii
    my_r = me % radii
    window = jnp.concatenate([jnp.roll(raw, 1, axis=0)[..., edge:], raw[..., :edge]], axis=-1)
    window = jnp.transpose(window, (1, 2, 0, 3)).reshape(planes + 1, 2 * w + 1, chunks * 2 * edge)
    b0 = window[:planes].reshape(n_f, heights, 2 * w + 1, chunks * 2 * edge)
    b_visc = window[planes]
    b_spin = lax.dynamic_slice_in_dim(rot, first_row + my_r, 2 * w + 1)[:, None]
    b_row = first_row + my_r - w + lax.iota(jnp.int32, 2 * w + 1)
    b_inside = ((b_row >= 0) & (b_row < total_rows))[:, None]

    def b_trim(x, k):
        return x[..., k : x.shape[-2] - k, :]

    def b_rates_at(state, k):
        return rates_ring(state, b_visc[k : b_visc.shape[0] - k], b_spin[k : b_spin.shape[0] - k])

    def b_keep(state, k):
        return jnp.where(b_inside[k : b_inside.shape[0] - k], state, 0.0)

    fixed = runge_kutta(b0, b_rates_at, b_keep, b_trim)[:, :, 0]
    fixed = lax.dynamic_index_in_dim(fixed, my_h, axis=1, keepdims=False)
    fixed = jnp.swapaxes(fixed.reshape(n_f, chunks, 2 * edge), 0, 1)
    line = jnp.concatenate(
        [fixed[:, :, edge : edge + w], line[:, :, w : cells - w], jnp.roll(fixed, -1, axis=0)[:, :, edge - w : edge]],
        axis=2,
    )

    for t in range(shift_blocks.shape[0]):
        shift = lax.dynamic_index_in_dim(shift_blocks[t], first_row + my_r, keepdims=False)
        per_chunk = cells // BLOCK
        count = chunks * per_chunk
        shift = shift % count
        whole = shift // per_chunk
        part = shift % per_chunk
        doubled = jnp.concatenate([line, line], axis=0)
        lane = lax.broadcasted_iota(jnp.int32, line.shape, 2)
        base = lax.dynamic_slice_in_dim(doubled, (chunks - whole) % chunks, chunks, 0)
        earlier = lax.dynamic_slice_in_dim(doubled, (chunks - whole - 1) % chunks, chunks, 0)
        rolled = base
        for step in range(1, per_chunk):
            mixed = jnp.roll(jnp.where(lane < cells - step * BLOCK, base, earlier), step * BLOCK, axis=2)
            rolled = jnp.where(part == step, mixed, rolled)
        line = rolled
    back = lax.all_to_all(line, "azi", 0, 0, tiled=True)
    return jnp.swapaxes(back, 0, 1).reshape(n_f, heights, radii, cells)


def solution(mesh):
    return jax.shard_map(
        body,
        mesh=mesh,
        in_specs=(P(None, None, "rad", "azi"), P("rad", "azi"), P(), P()),
        out_specs=P(None, None, "rad", "azi"),
        check_vma=False,
    )
```

time: 98.9 us -> 126 us (1.27)
  the two profiles are of different devices: /device:TPU:1 before, /device:TPU:64 now
where the time goes in v3:
time: 126 us; the launch traced here: 125 us
  waiting for transfers between devices  34.9 us (28%)
  starting transfers between devices  28.1 us (22%)
  local copies, waits for them, and re-layouts  25.7 us (20%)
  blocking collectives  23.3 us (18%)
  other arithmetic  9.41 us (7%)
  between operations  3.94 us (3%)
    all_to_all x1, waiting for transfers between devices, body(): lax.all_to_all(jnp.concatenate([lines, wins], axis=1), 'azi', 0, 0, tiled...  34.4 us
    all_to_all x1, blocking collectives, body(): back = lax.all_to_all(line, 'azi', 0, 0, tiled=True)  23.3 us
    all_to_all x1, starting transfers between devices, body(): lax.all_to_all(jnp.concatenate([lines, wins], axis=1), 'azi', 0, 0, tiled...  22.5 us
    reshape x1, local copies, waits for them, and re-layouts, body(): b0 = window[:planes].reshape(n_f, heights, 2 * w + 1, chunks * 2 * edge)  5.82 us
    slice x2, local copies, waits for them, and re-layouts, body(): b0 = window[:planes].reshape(n_f, heights, 2 * w + 1, chunks * 2 * edge)  3.9 us
    ppermute x1, starting transfers between devices, exchange_rows(): north = lax.ppermute(cells[:, :width], 'rad', down)  3.64 us
  transfers between devices with their start and end apart: 3, of which 2 were waited for; matrix products, arithmetic and copies ran while one was open for 2% of the time, Pallas kernels for 0%

profile of v3, /device:TPU:64, one launch (start us, length us, event | category | flops | bytes accessed | tf_op | source)
XLA Modules:
  0.0 125.3 jit_solution(17051267870470785342)
XLA Ops:
  0.0 1.0 fusion.43
  1.0 1.9 %collective-permute-start = (f32[25,3,128]{2,1,0:T(4,128)S(1)}, f32[25,3,128]{2,1,0:T(4,128)S(1)}, u32[]{:S(2)}, u32[]{:S(2)}) collective-permute-start(f32[25,3,128]{2,1,0:T(4,128)S(1)} %get-tuple-element.82), channel_id=1, source_target_pairs={{0,64},{64,128},{128,192},{192,256},{256,320},{320,384},{384,448},... | collective-permute-start | bytes 115208 | tf_op jit(solution)/shard_map/ppermute | solution.py:49
  2.9 3.6 %collective-permute-start.1 = (f32[25,3,128]{2,1,0:T(4,128)S(1)}, f32[25,3,128]{2,1,0:T(4,128)S(1)}, u32[]{:S(2)}, u32[]{:S(2)}) collective-permute-start(f32[25,3,128]{2,1,0:T(4,128)S(1)} %get-tuple-element.83), channel_id=1, source_target_pairs={{64,0},{128,64},{192,128},{256,192},{320,256},{384,320},{448,384},... | collective-permute-start | bytes 115208 | tf_op jit(solution)/shard_map/ppermute | solution.py:50
  6.6 0.7 pad_maximum_fusion.12
  7.8 0.5 collective-permute-done.1
  8.3 1.0 pad_maximum_fusion.6
  10.1 0.2 fusion.69
  10.3 0.2 fusion.70
  10.5 0.4 subtract_multiply_fusion.3
  11.6 0.3 subtract_multiply_fusion.5
  12.8 0.2 copy.79
  15.9 1.0 pad_maximum_fusion.1
  16.9 22.5 %all-to-all-start = ((f32[64,20,128]{2,1,0:T(8,128)}), f32[64,20,128]{2,1,0:T(8,128)S(1)}, u32[]{:S(2)}, u32[]{:S(2)}) async-start(f32[64,20,128]{2,1,0:T(8,128)} %pad_maximum_fusion.1), calls=%async_computation | async-start | bytes 1572864 | tf_op jit(solution)/shard_map/all_to_all | solution.py:115
  39.4 0.6 constant_dynamic-slice_fusion
  42.3 0.6 slice.739
  44.4 34.4 %all-to-all-done = f32[64,20,128]{2,1,0:T(8,128)S(1)} async-done(((f32[64,20,128]{2,1,0:T(8,128)}), f32[64,20,128]{2,1,0:T(8,128)S(1)}, u32[]{:S(2)}, u32[]{:S(2)}) %all-to-all-start) | async-done | bytes 655392 | tf_op jit(solution)/shard_map/all_to_all | solution.py:115
  78.9 0.7 copy-done.2
  79.6 0.4 copy.91
  80.1 0.4 copy.93
  80.5 1.2 reshape.249
  81.7 2.0 %slice.833 = f32[64,25,7,6]{0,3,2,1:T(8,128)} slice(f32[64,25,7,12]{0,3,2,1:T(8,128)} %reshape.249), slice={[0:64], [0:25], [0:7], [0:6]} | slice | bytes 537600 | tf_op jit(solution)/shard_map/slice | solution.py:123
  83.7 0.4 slice.751
  84.1 1.8 %fusion.1 = f32[25,7,64,12]{2,3,1,0:T(8,128)S(1)} fusion(f32[63,25,7,12]{0,3,2,1:T(8,128)S(1)} %slice.669, f32[1,25,7,12]{0,3,2,1:T(8,128)S(1)} %slice.751, f32[64,25,7,6]{0,3,2,1:T(8,128)} %slice.833), kind=kLoop, calls=%fused_computation.2 | loop fusion | flops 268800 | bytes 1344000 | tf_op jit(solution)/shard_map/transpose | solution.py:124
  86.1 3.8 %copy.94 = f32[24,7,64,12]{3,2,0,1:T(8,128)} copy(f32[24,7,64,12]{2,3,1,0:T(8,128)S(1)} %slice.834) | data formatting | bytes 1032192 | tf_op jit(solution)/shard_map/slice | solution.py:125
  89.9 5.8 %reshape.250 = f32[3,8,7,768]{3,1,0,2:T(8,128)S(1)} reshape(f32[24,7,64,12]{3,2,0,1:T(8,128)} %copy.94) | data formatting | bytes 1032192 | tf_op jit(solution)/shard_map/reshape | solution.py:125
  96.4 0.4 fusion.4
  97.4 0.2 fusion.23
  98.4 0.3 slice-done
  99.6 1.1 slice.901
  100.7 0.3 maximum_maximum_fusion
  101.4 23.3 %all_to_all.10 = f32[64,3,128]{2,1,0:T(4,128)S(1)} all-to-all(f32[64,3,128]{2,1,0:T(4,128)S(1)} %maximum_select_fusion), channel_id=1, replica_groups=mesh['rad'=12,'azi'=64] {'azi'}, dimensions={0} | all-to-all | bytes 196608 | tf_op jit(solution)/shard_map/all_to_all | solution.py:164
  124.7 0.6 copy.110
  (109 shorter events, 9.4 us)
Async XLA Ops:
  0.0 39.4 %copy-start = (s32[1,96]{1,0:T(1,128)S(1)}, s32[1,96]{1,0:T(1,128)}, u32[]{:S(2)}) copy-start(s32[1,96]{1,0:T(1,128)} %param.7) | copy-start | bytes 1156
  1.0 6.8 %collective-permute-start = (f32[25,3,128]{2,1,0:T(4,128)S(1)}, f32[25,3,128]{2,1,0:T(4,128)S(1)}, u32[]{:S(2)}, u32[]{:S(2)}) collective-permute-start(f32[25,3,128]{2,1,0:T(4,128)S(1)} %get-tuple-element.82), channel_id=1, source_target_pairs={{0,64},{64,128},{128,192},{192,256},{256,320},{320,384},{384,448},... | collective-permute-start | bytes 115208 | tf_op jit(solution)/shard_map/ppermute | solution.py:49
  2.9 5.4 %collective-permute-start.1 = (f32[25,3,128]{2,1,0:T(4,128)S(1)}, f32[25,3,128]{2,1,0:T(4,128)S(1)}, u32[]{:S(2)}, u32[]{:S(2)}) collective-permute-start(f32[25,3,128]{2,1,0:T(4,128)S(1)} %get-tuple-element.83), channel_id=1, source_target_pairs={{64,0},{128,64},{192,128},{256,192},{320,256},{384,320},{448,384},... | collective-permute-start | bytes 115208 | tf_op jit(solution)/shard_map/ppermute | solution.py:50
  16.9 61.8 %all-to-all-start = ((f32[64,20,128]{2,1,0:T(8,128)}), f32[64,20,128]{2,1,0:T(8,128)S(1)}, u32[]{:S(2)}, u32[]{:S(2)}) async-start(f32[64,20,128]{2,1,0:T(8,128)} %pad_maximum_fusion.1), calls=%async_computation | async-start | bytes 1572864 | tf_op jit(solution)/shard_map/all_to_all | solution.py:115
  78.7 0.9 copy-start.2
  95.7 2.1 %copy-start.1 = (f32[3,8,7,768]{3,1,0,2:T(8,128)}, f32[3,8,7,768]{3,1,0,2:T(8,128)S(1)}, u32[]{:S(2)}) copy-start(f32[3,8,7,768]{3,1,0,2:T(8,128)S(1)} %reshape.250) | copy-start | bytes 1548292
  97.9 0.9 slice-start

commit v4 on v2

--- a/solution.py
+++ b/solution.py
@@ -16,10 +16,8 @@
     up = [(i, i + 1) for i in range(n_r - 1)]
     down = [(i + 1, i) for i in range(n_r - 1)]
     fwd = [(i, (i + 1) % n_a) for i in range(n_a)]
-    back = [((i + 1) % n_a, i) for i in range(n_a)]
-    behind = lax.ppermute(cells[:, :, -width:], "azi", fwd)
-    ahead = lax.ppermute(cells[:, :, :width], "azi", back)
-    wide = jnp.concatenate([behind, cells, ahead], axis=2)
+    behind = lax.ppermute(cells[:, :, cells.shape[2] - 2 * width :], "azi", fwd)
+    wide = jnp.concatenate([behind, cells], axis=2)
     south = lax.ppermute(wide[:, -width:, :], "rad", up)
     north = lax.ppermute(wide[:, :width, :], "rad", down)
     return jnp.concatenate([south, wide, north], axis=1)
@@ -42,10 +40,11 @@
     return jnp.stack([rate_density, rate_radial, rate_azimuth])
 
 
-def advect(state, shift_row, first_row):
+def advect(state, shift_row, first_row, lag):
     fields, heights, radii, cells = state.shape
     lines = jnp.swapaxes(state.reshape(fields, heights * radii, cells), 0, 1)
     ring = lax.all_to_all(lines, "azi", 0, 0, tiled=True)
+    ring = jnp.concatenate([ring[:, :, lag:], jnp.roll(ring, -1, axis=0)[:, :, :lag]], axis=2)
     chunks = ring.shape[0]
     me = lax.axis_index("azi")
     shift = lax.dynamic_index_in_dim(shift_row, first_row + me % radii, keepdims=False)
@@ -95,7 +94,7 @@
     second = keep(0.75 * trim(state, 2) + 0.25 * (trim(first, 1) + time_step * rates_at(first, 2)), 2)
     state = trim(state, 3) / 3.0 + 2.0 / 3.0 * (trim(second, 1) + time_step * rates_at(second, 3))
     for t in range(shift_blocks.shape[0]):
-        state = advect(state, shift_blocks[t], first_row)
+        state = advect(state, shift_blocks[t], first_row, w)
     return state
 
 

time: 98.9 us -> 92.1 us (0.931)
  starting transfers between devices: 49.9 us -> 25.5 us
  waiting for transfers between devices: 18.3 us -> 35.5 us
    ppermute x2 -> x1, starting transfers between devices: 22.7 us -> 4.03 us  [exchange_halo(): behind = lax.ppermute(cells[:, :, cells.shape[2] - 2 * width:], 'azi', fwd)]
    ppermute x2 -> x1, waiting for transfers between devices: 0.88 us -> 18.2 us  [exchange_halo(): behind = lax.ppermute(cells[:, :, cells.shape[2] - 2 * width:], 'azi', fwd)]
    all_to_all x1, starting transfers between devices: 15.7 us -> 9.83 us  [advect(): ring = lax.all_to_all(lines, 'azi', 0, 0, tiled=True)]
  transfers between devices with their start and end apart: 5 -> 4, of which waited for: 3 -> 3; matrix products, arithmetic and copies ran while one was open for 1% -> 1% of each run, Pallas kernels for 0% -> 0%
where the time goes in v4:
time: 92.1 us; the launch traced here: 91.8 us
  waiting for transfers between devices  35.5 us (39%)
  starting transfers between devices  25.5 us (28%)
  blocking collectives  20.2 us (22%)
  local copies, waits for them, and re-layouts  5.34 us (6%)
  other arithmetic  2.91 us (3%)
  between operations  2.31 us (3%)
    all_to_all x1, blocking collectives, advect(): back = lax.all_to_all(rolled, 'azi', 0, 0, tiled=True)  20.2 us
    ppermute x1, waiting for transfers between devices, exchange_halo(): behind = lax.ppermute(cells[:, :, cells.shape[2] - 2 * width:], 'azi', fwd)  18.2 us
    all_to_all x1, waiting for transfers between devices, advect(): ring = lax.all_to_all(lines, 'azi', 0, 0, tiled=True)  13.4 us
    all_to_all x1, starting transfers between devices, advect(): ring = lax.all_to_all(lines, 'azi', 0, 0, tiled=True)  9.83 us
    ppermute x1, starting transfers between devices, exchange_halo(): south = lax.ppermute(wide[:, -width:, :], 'rad', up)  9.76 us
    ppermute x1, starting transfers between devices, exchange_halo(): behind = lax.ppermute(cells[:, :, cells.shape[2] - 2 * width:], 'azi', fwd)  4.03 us
    ppermute x1, waiting for transfers between devices, exchange_halo(): north = lax.ppermute(wide[:, :width, :], 'rad', down)  3.84 us
    ppermute x1, starting transfers between devices, exchange_halo(): north = lax.ppermute(wide[:, :width, :], 'rad', down)  1.92 us
  transfers between devices with their start and end apart: 4, of which 3 were waited for; matrix products, arithmetic and copies ran while one was open for 1% of the time, Pallas kernels for 0%

profile of v4, /device:TPU:1, one launch (start us, length us, event | category | flops | bytes accessed | tf_op | source)
XLA Modules:
  0.0 91.8 jit_solution(3176057537263876292)
XLA Ops:
  0.0 0.9 %copy.17 = f32[3,8,8,128]{3,1,0,2:T(8,128)S(1)} copy(f32[3,8,8,128]{3,2,1,0:T(8,128)} %param.4) | data formatting | bytes 196608 | tf_op args[0]
  1.1 4.0 %collective-permute-start = (f32[25,8,6]{2,0,1:T(8,128)S(1)}, f32[25,8,6]{2,0,1:T(8,128)S(1)}, u32[]{:S(2)}, u32[]{:S(2)}) collective-permute-start(f32[25,8,6]{2,0,1:T(8,128)S(1)} %pad_maximum_fusion.2), channel_id=1, source_target_pairs={{0,1},{1,2},{2,3},{3,4},{4,5},{5,6},{6,7},{7,8},{8,9},{9,10},{10,1... | collective-permute-start | bytes 14408 | tf_op jit(solution)/shard_map/ppermute | solution.py:19
  5.1 0.6 copy-done.2
  6.1 18.2 %collective-permute-done = f32[25,8,6]{2,0,1:T(8,128)S(1)} collective-permute-done((f32[25,8,6]{2,0,1:T(8,128)S(1)}, f32[25,8,6]{2,0,1:T(8,128)S(1)}, u32[]{:S(2)}, u32[]{:S(2)}) %collective-permute-start) | collective-permute-done | bytes 4832 | tf_op jit(solution)/shard_map/ppermute | solution.py:19
  24.4 0.1 pad_maximum_fusion.5
  24.5 9.8 %collective-permute-start.1 = (f32[25,3,134]{2,0,1:T(8,128)S(1)}, f32[25,3,134]{2,0,1:T(8,128)S(1)}, u32[]{:S(2)}, u32[]{:S(2)}) collective-permute-start(f32[25,3,134]{2,0,1:T(8,128)S(1)} %get-tuple-element.35), channel_id=1, source_target_pairs={{0,64},{64,128},{128,192},{192,256},{256,320},{320,384},{384,448},... | collective-permute-start | bytes 120608 | tf_op jit(solution)/shard_map/ppermute | solution.py:21
  34.3 1.9 %collective-permute-start.2 = (f32[25,3,134]{2,0,1:T(8,128)S(1)}, f32[25,3,134]{2,0,1:T(8,128)S(1)}, u32[]{:S(2)}, u32[]{:S(2)}) collective-permute-start(f32[25,3,134]{2,0,1:T(8,128)S(1)} %get-tuple-element.36), channel_id=1, source_target_pairs={{64,0},{128,64},{192,128},{256,192},{320,256},{384,320},{448,384},... | collective-permute-start | bytes 120608 | tf_op jit(solution)/shard_map/ppermute | solution.py:22
  36.4 3.8 %collective-permute-done.2 = f32[25,3,134]{2,0,1:T(8,128)S(1)} collective-permute-done((f32[25,3,134]{2,0,1:T(8,128)S(1)}, f32[25,3,134]{2,0,1:T(8,128)S(1)}, u32[]{:S(2)}, u32[]{:S(2)}) %collective-permute-start.2) | collective-permute-done | bytes 40232 | tf_op jit(solution)/shard_map/ppermute | solution.py:22
  40.5 0.1 pad_maximum_fusion
  40.7 0.2 fusion.24
  40.9 0.2 fusion.25
  41.1 0.4 subtract_multiply_fusion.1
  41.5 0.1 fusion.13
  41.7 0.2 fusion.4
  41.8 0.2 fusion.26
  42.0 0.2 fusion.27
  42.2 0.3 subtract_multiply_fusion.3
  42.6 0.1 fusion.21
  42.7 0.2 fusion.6
  43.0 0.1 fusion.29
  43.2 0.2 subtract_multiply_fusion.5
  43.4 0.1 fusion.14
  43.6 0.7 copy.10
  44.3 9.8 %all-to-all-start = ((f32[64,3,128]{2,1,0:T(4,128)}), f32[64,3,128]{2,1,0:T(4,128)S(1)}, u32[]{:S(2)}, u32[]{:S(2)}) async-start(f32[64,3,128]{2,1,0:T(4,128)} %copy.10), calls=%async_computation | async-start | bytes 262144 | tf_op jit(solution)/shard_map/all_to_all | solution.py:46
  54.2 0.6 constant_dynamic-slice_fusion
  56.8 13.4 %all-to-all-done = f32[64,3,128]{2,1,0:T(4,128)S(1)} async-done(((f32[64,3,128]{2,1,0:T(4,128)}), f32[64,3,128]{2,1,0:T(4,128)S(1)}, u32[]{:S(2)}, u32[]{:S(2)}) %all-to-all-start) | async-done | bytes 98336 | tf_op jit(solution)/shard_map/all_to_all | solution.py:46
  70.3 0.1 slice.390
  70.4 0.2 maximum_maximum_fusion
  70.7 0.1 fusion.30
  70.8 0.1 maximum_select_fusion
  71.0 20.2 %all_to_all.10 = f32[64,3,128]{2,1,0:T(4,128)S(1)} all-to-all(f32[64,3,128]{2,1,0:T(4,128)S(1)} %maximum_select_fusion), channel_id=1, replica_groups=mesh['rad'=12,'azi'=64] {'azi'}, dimensions={0} | all-to-all | bytes 196608 | tf_op jit(solution)/shard_map/all_to_all | solution.py:64
  91.1 0.6 copy.11
  (30 shorter events, 1.3 us)
Async XLA Ops:
  0.0 54.2 %copy-start = (s32[1,96]{1,0:T(1,128)S(1)}, s32[1,96]{1,0:T(1,128)}, u32[]{:S(2)}) copy-start(s32[1,96]{1,0:T(1,128)} %param.7) | copy-start | bytes 1156
  0.0 0.9 %copy-start.1 = (f32[8,128]{1,0:T(8,128)S(1)}, f32[8,128]{1,0:T(8,128)}, u32[]{:S(2)}) copy-start(f32[8,128]{1,0:T(8,128)} %param.5) | copy-start | bytes 12292
  1.1 23.3 %collective-permute-start = (f32[25,8,6]{2,0,1:T(8,128)S(1)}, f32[25,8,6]{2,0,1:T(8,128)S(1)}, u32[]{:S(2)}, u32[]{:S(2)}) collective-permute-start(f32[25,8,6]{2,0,1:T(8,128)S(1)} %pad_maximum_fusion.2), channel_id=1, source_target_pairs={{0,1},{1,2},{2,3},{3,4},{4,5},{5,6},{6,7},{7,8},{8,9},{9,10},{10,1... | collective-permute-start | bytes 14408 | tf_op jit(solution)/shard_map/ppermute | solution.py:19
  5.1 0.7 copy-start.2
  24.5 11.9 %collective-permute-start.1 = (f32[25,3,134]{2,0,1:T(8,128)S(1)}, f32[25,3,134]{2,0,1:T(8,128)S(1)}, u32[]{:S(2)}, u32[]{:S(2)}) collective-permute-start(f32[25,3,134]{2,0,1:T(8,128)S(1)} %get-tuple-element.35), channel_id=1, source_target_pairs={{0,64},{64,128},{128,192},{192,256},{256,320},{320,384},{384,448},... | collective-permute-start | bytes 120608 | tf_op jit(solution)/shard_map/ppermute | solution.py:21
  34.3 5.9 %collective-permute-start.2 = (f32[25,3,134]{2,0,1:T(8,128)S(1)}, f32[25,3,134]{2,0,1:T(8,128)S(1)}, u32[]{:S(2)}, u32[]{:S(2)}) collective-permute-start(f32[25,3,134]{2,0,1:T(8,128)S(1)} %get-tuple-element.36), channel_id=1, source_target_pairs={{64,0},{128,64},{192,128},{256,192},{320,256},{384,320},{448,384},... | collective-permute-start | bytes 120608 | tf_op jit(solution)/shard_map/ppermute | solution.py:22
  44.3 25.9 %all-to-all-start = ((f32[64,3,128]{2,1,0:T(4,128)}), f32[64,3,128]{2,1,0:T(4,128)S(1)}, u32[]{:S(2)}, u32[]{:S(2)}) async-start(f32[64,3,128]{2,1,0:T(4,128)} %copy.10), calls=%async_computation | async-start | bytes 262144 | tf_op jit(solution)/shard_map/all_to_all | solution.py:46

commit v5 on v4

--- a/solution.py
+++ b/solution.py
@@ -16,11 +16,24 @@
     up = [(i, i + 1) for i in range(n_r - 1)]
     down = [(i + 1, i) for i in range(n_r - 1)]
     fwd = [(i, (i + 1) % n_a) for i in range(n_a)]
-    behind = lax.ppermute(cells[:, :, cells.shape[2] - 2 * width :], "azi", fwd)
-    wide = jnp.concatenate([behind, cells], axis=2)
-    south = lax.ppermute(wide[:, -width:, :], "rad", up)
-    north = lax.ppermute(wide[:, :width, :], "rad", down)
-    return jnp.concatenate([south, wide, north], axis=1)
+
+    def diag(pairs_r):
+        return [(r0 * n_a + a0, r1 * n_a + a1) for r0, r1 in pairs_r for a0, a1 in fwd]
+
+    tail = cells[:, :, cells.shape[2] - 2 * width :]
+    behind = lax.ppermute(tail, "azi", fwd)
+    south_behind = lax.ppermute(tail[:, -width:], ("rad", "azi"), diag(up))
+    north_behind = lax.ppermute(tail[:, :width], ("rad", "azi"), diag(down))
+    south = lax.ppermute(cells[:, -width:], "rad", up)
+    north = lax.ppermute(cells[:, :width], "rad", down)
+    return jnp.concatenate(
+        [
+            jnp.concatenate([south_behind, south], axis=2),
+            jnp.concatenate([behind, cells], axis=2),
+            jnp.concatenate([north_behind, north], axis=2),
+        ],
+        axis=1,
+    )
 
 
 def rates(state, viscosity, spin):

time: 92.1 us -> 97.2 us (1.055)
  the two profiles are of different devices: /device:TPU:1 before, /device:TPU:64 now
where the time goes in v5:
time: 97.2 us; the launch traced here: 96.9 us
  starting transfers between devices  32.8 us (34%)
  waiting for transfers between devices  32.2 us (33%)
  blocking collectives  21.2 us (22%)
  local copies, waits for them, and re-layouts  5.35 us (6%)
  other arithmetic  2.95 us (3%)
  between operations  2.34 us (2%)
    all_to_all x1, blocking collectives, advect(): back = lax.all_to_all(rolled, 'azi', 0, 0, tiled=True)  21.2 us
    all_to_all x1, starting transfers between devices, advect(): ring = lax.all_to_all(lines, 'azi', 0, 0, tiled=True)  16.2 us
    all_to_all x1, waiting for transfers between devices, advect(): ring = lax.all_to_all(lines, 'azi', 0, 0, tiled=True)  14.4 us
    ppermute x1, waiting for transfers between devices, exchange_halo(): south_behind = lax.ppermute(tail[:, -width:], ('rad', 'azi'), diag(up))  7.25 us
    ppermute x1, waiting for transfers between devices, exchange_halo(): behind = lax.ppermute(tail, 'azi', fwd)  5.98 us
    ppermute x1, waiting for transfers between devices, exchange_halo(): north_behind = lax.ppermute(tail[:, :width], ('rad', 'azi'), diag(down))  4.5 us
    ppermute x1, starting transfers between devices, exchange_halo(): south_behind = lax.ppermute(tail[:, -width:], ('rad', 'azi'), diag(up))  3.84 us
    ppermute x1, starting transfers between devices, exchange_halo(): north_behind = lax.ppermute(tail[:, :width], ('rad', 'azi'), diag(down))  3.74 us
  transfers between devices with their start and end apart: 6, of which 4 were waited for; matrix products, arithmetic and copies ran while one was open for 1% of the time, Pallas kernels for 0%

profile of v5, /device:TPU:64, one launch (start us, length us, event | category | flops | bytes accessed | tf_op | source)
XLA Modules:
  0.0 96.9 jit_solution(4167763132091738632)
XLA Ops:
  0.0 0.9 copy.17
  1.0 1.9 %collective-permute-start.1 = (f32[25,3,128]{2,0,1:T(8,128)S(1)}, f32[25,3,128]{2,0,1:T(8,128)S(1)}, u32[]{:S(2)}, u32[]{:S(2)}) collective-permute-start(f32[25,3,128]{2,0,1:T(8,128)S(1)} %get-tuple-element.39), channel_id=1, source_target_pairs={{0,64},{64,128},{128,192},{192,256},{256,320},{320,384},{384,448},... | collective-permute-start | bytes 115208 | tf_op jit(solution)/shard_map/ppermute | solution.py:27
  2.9 3.6 %collective-permute-start.4 = (f32[25,3,128]{2,0,1:T(8,128)S(1)}, f32[25,3,128]{2,0,1:T(8,128)S(1)}, u32[]{:S(2)}, u32[]{:S(2)}) collective-permute-start(f32[25,3,128]{2,0,1:T(8,128)S(1)} %get-tuple-element.40), channel_id=1, source_target_pairs={{64,0},{128,64},{192,128},{256,192},{320,256},{384,320},{448,384},... | collective-permute-start | bytes 115208 | tf_op jit(solution)/shard_map/ppermute | solution.py:28
  6.6 3.8 %collective-permute-start = (f32[25,3,6]{2,0,1:T(8,128)S(1)}, f32[25,3,6]{2,0,1:T(8,128)S(1)}, u32[]{:S(2)}, u32[]{:S(2)}) collective-permute-start(f32[25,3,6]{2,0,1:T(8,128)S(1)} %get-tuple-element.37), channel_id=1, source_target_pairs={{0,65},{1,66},{2,67},{3,68},{4,69},{5,70},{6,71},{7,72},{8,73},{9,... | collective-permute-start | bytes 5408 | tf_op jit(solution)/shard_map/ppermute | solution.py:25
  10.5 3.7 %collective-permute-start.3 = (f32[25,3,6]{2,0,1:T(8,128)S(1)}, f32[25,3,6]{2,0,1:T(8,128)S(1)}, u32[]{:S(2)}, u32[]{:S(2)}) collective-permute-start(f32[25,3,6]{2,0,1:T(8,128)S(1)} %get-tuple-element.38), channel_id=1, source_target_pairs={{64,1},{65,2},{66,3},{67,4},{68,5},{69,6},{70,7},{71,8},{72,9},{73... | collective-permute-start | bytes 5408 | tf_op jit(solution)/shard_map/ppermute | solution.py:26
  14.3 3.5 %collective-permute-start.2 = (f32[25,8,6]{2,0,1:T(8,128)S(1)}, f32[25,8,6]{2,0,1:T(8,128)S(1)}, u32[]{:S(2)}, u32[]{:S(2)}) collective-permute-start(f32[25,8,6]{2,0,1:T(8,128)S(1)} %fusion.12), channel_id=1, source_target_pairs={{0,1},{1,2},{2,3},{3,4},{4,5},{5,6},{6,7},{7,8},{8,9},{9,10},{10,1... | collective-permute-start | bytes 14408 | tf_op jit(solution)/shard_map/ppermute | solution.py:24
  17.9 0.6 copy-done.2
  19.0 7.3 %collective-permute-done = f32[25,3,6]{2,0,1:T(8,128)S(1)} collective-permute-done((f32[25,3,6]{2,0,1:T(8,128)S(1)}, f32[25,3,6]{2,0,1:T(8,128)S(1)}, u32[]{:S(2)}, u32[]{:S(2)}) %collective-permute-start) | collective-permute-done | bytes 1832 | tf_op jit(solution)/shard_map/ppermute | solution.py:25
  26.3 4.5 %collective-permute-done.3 = f32[25,3,6]{2,0,1:T(8,128)S(1)} collective-permute-done((f32[25,3,6]{2,0,1:T(8,128)S(1)}, f32[25,3,6]{2,0,1:T(8,128)S(1)}, u32[]{:S(2)}, u32[]{:S(2)}) %collective-permute-start.3) | collective-permute-done | bytes 1832 | tf_op jit(solution)/shard_map/ppermute | solution.py:26
  30.8 6.0 %collective-permute-done.2 = f32[25,8,6]{2,0,1:T(8,128)S(1)} collective-permute-done((f32[25,8,6]{2,0,1:T(8,128)S(1)}, f32[25,8,6]{2,0,1:T(8,128)S(1)}, u32[]{:S(2)}, u32[]{:S(2)}) %collective-permute-start.2) | collective-permute-done | bytes 4832 | tf_op jit(solution)/shard_map/ppermute | solution.py:24
  37.1 0.2 maximum_maximum_fusion
  37.3 0.2 fusion.28
  37.6 0.2 fusion.29
  37.8 0.4 subtract_multiply_fusion.1
  38.2 0.1 fusion.14
  38.3 0.2 fusion.4
  38.5 0.2 fusion.30
  38.7 0.2 fusion.31
  38.9 0.3 subtract_multiply_fusion.3
  39.2 0.1 fusion.22
  39.4 0.2 fusion.6
  39.8 0.2 subtract_multiply_fusion.5
  40.2 0.7 copy.10
  41.0 16.2 %all-to-all-start = ((f32[64,3,128]{2,1,0:T(4,128)}), f32[64,3,128]{2,1,0:T(4,128)S(1)}, u32[]{:S(2)}, u32[]{:S(2)}) async-start(f32[64,3,128]{2,1,0:T(4,128)} %copy.10), calls=%async_computation | async-start | bytes 262144 | tf_op jit(solution)/shard_map/all_to_all | solution.py:59
  57.2 0.6 constant_dynamic-slice_fusion
  59.8 14.4 %all-to-all-done = f32[64,3,128]{2,1,0:T(4,128)S(1)} async-done(((f32[64,3,128]{2,1,0:T(4,128)}), f32[64,3,128]{2,1,0:T(4,128)S(1)}, u32[]{:S(2)}, u32[]{:S(2)}) %all-to-all-start) | async-done | bytes 98336 | tf_op jit(solution)/shard_map/all_to_all | solution.py:59
  74.3 0.1 slice.408
  74.4 0.2 maximum_maximum_fusion.1
  74.7 0.1 fusion.34
  74.8 0.1 maximum_select_fusion
  75.0 21.2 %all_to_all.10 = f32[64,3,128]{2,1,0:T(4,128)S(1)} all-to-all(f32[64,3,128]{2,1,0:T(4,128)S(1)} %maximum_select_fusion), channel_id=1, replica_groups=mesh['rad'=12,'azi'=64] {'azi'}, dimensions={0} | all-to-all | bytes 196608 | tf_op jit(solution)/shard_map/all_to_all | solution.py:77
  96.2 0.6 copy.11
  (35 shorter events, 1.6 us)
Async XLA Ops:
  0.0 57.2 %copy-start = (s32[1,96]{1,0:T(1,128)S(1)}, s32[1,96]{1,0:T(1,128)}, u32[]{:S(2)}) copy-start(s32[1,96]{1,0:T(1,128)} %param.7) | copy-start | bytes 1156
  0.0 0.9 copy-start.1
  1.0 35.8 %collective-permute-start.1 = (f32[25,3,128]{2,0,1:T(8,128)S(1)}, f32[25,3,128]{2,0,1:T(8,128)S(1)}, u32[]{:S(2)}, u32[]{:S(2)}) collective-permute-start(f32[25,3,128]{2,0,1:T(8,128)S(1)} %get-tuple-element.39), channel_id=1, source_target_pairs={{0,64},{64,128},{128,192},{192,256},{256,320},{320,384},{384,448},... | collective-permute-start | bytes 115208 | tf_op jit(solution)/shard_map/ppermute | solution.py:27
  2.9 33.9 %collective-permute-start.4 = (f32[25,3,128]{2,0,1:T(8,128)S(1)}, f32[25,3,128]{2,0,1:T(8,128)S(1)}, u32[]{:S(2)}, u32[]{:S(2)}) collective-permute-start(f32[25,3,128]{2,0,1:T(8,128)S(1)} %get-tuple-element.40), channel_id=1, source_target_pairs={{64,0},{128,64},{192,128},{256,192},{320,256},{384,320},{448,384},... | collective-permute-start | bytes 115208 | tf_op jit(solution)/shard_map/ppermute | solution.py:28
  6.6 19.7 %collective-permute-start = (f32[25,3,6]{2,0,1:T(8,128)S(1)}, f32[25,3,6]{2,0,1:T(8,128)S(1)}, u32[]{:S(2)}, u32[]{:S(2)}) collective-permute-start(f32[25,3,6]{2,0,1:T(8,128)S(1)} %get-tuple-element.37), channel_id=1, source_target_pairs={{0,65},{1,66},{2,67},{3,68},{4,69},{5,70},{6,71},{7,72},{8,73},{9,... | collective-permute-start | bytes 5408 | tf_op jit(solution)/shard_map/ppermute | solution.py:25
  10.5 20.3 %collective-permute-start.3 = (f32[25,3,6]{2,0,1:T(8,128)S(1)}, f32[25,3,6]{2,0,1:T(8,128)S(1)}, u32[]{:S(2)}, u32[]{:S(2)}) collective-permute-start(f32[25,3,6]{2,0,1:T(8,128)S(1)} %get-tuple-element.38), channel_id=1, source_target_pairs={{64,1},{65,2},{66,3},{67,4},{68,5},{69,6},{70,7},{71,8},{72,9},{73... | collective-permute-start | bytes 5408 | tf_op jit(solution)/shard_map/ppermute | solution.py:26
  14.3 22.4 %collective-permute-start.2 = (f32[25,8,6]{2,0,1:T(8,128)S(1)}, f32[25,8,6]{2,0,1:T(8,128)S(1)}, u32[]{:S(2)}, u32[]{:S(2)}) collective-permute-start(f32[25,8,6]{2,0,1:T(8,128)S(1)} %fusion.12), channel_id=1, source_target_pairs={{0,1},{1,2},{2,3},{3,4},{4,5},{5,6},{6,7},{7,8},{8,9},{9,10},{10,1... | collective-permute-start | bytes 14408 | tf_op jit(solution)/shard_map/ppermute | solution.py:24
  17.9 0.7 copy-start.2
  41.0 33.3 %all-to-all-start = ((f32[64,3,128]{2,1,0:T(4,128)}), f32[64,3,128]{2,1,0:T(4,128)S(1)}, u32[]{:S(2)}, u32[]{:S(2)}) async-start(f32[64,3,128]{2,1,0:T(4,128)} %copy.10), calls=%async_computation | async-start | bytes 262144 | tf_op jit(solution)/shard_map/all_to_all | solution.py:59

commit v6 on v4

--- a/solution.py
+++ b/solution.py
@@ -8,19 +8,6 @@
 
 
 time_step = 0.3
-
-
-def exchange_halo(cells, width):
-    n_r = lax.axis_size("rad")
-    n_a = lax.axis_size("azi")
-    up = [(i, i + 1) for i in range(n_r - 1)]
-    down = [(i + 1, i) for i in range(n_r - 1)]
-    fwd = [(i, (i + 1) % n_a) for i in range(n_a)]
-    behind = lax.ppermute(cells[:, :, cells.shape[2] - 2 * width :], "azi", fwd)
-    wide = jnp.concatenate([behind, cells], axis=2)
-    south = lax.ppermute(wide[:, -width:, :], "rad", up)
-    north = lax.ppermute(wide[:, :width, :], "rad", down)
-    return jnp.concatenate([south, wide, north], axis=1)
 
 
 def rates(state, viscosity, spin):
@@ -68,13 +55,21 @@
 def body(fields, viscosity, rotation, shift_blocks):
     n_f, heights, radii, cells = fields.shape
     w = HALO
+    n_r = lax.axis_size("rad")
+    n_a = lax.axis_size("azi")
     band = lax.axis_index("rad")
     first_row = band * radii
     total_rows = rotation.shape[0]
-    packed = jnp.concatenate([fields.reshape(n_f * heights, radii, cells), viscosity[None]], axis=0)
-    ext = exchange_halo(packed, w)
-    u0 = ext[: n_f * heights].reshape(n_f, heights, radii + 2 * w, cells + 2 * w)
-    visc = ext[n_f * heights]
+    planes = n_f * heights
+    packed = jnp.concatenate([fields.reshape(planes, radii, cells), viscosity[None]], axis=0)
+
+    up = [(i, i + 1) for i in range(n_r - 1)]
+    down = [(i + 1, i) for i in range(n_r - 1)]
+    south = lax.ppermute(packed[:, -w:], "rad", up)
+    north = lax.ppermute(packed[:, :w], "rad", down)
+    rows = jnp.concatenate([south, packed, north], axis=1)
+    behind = lax.ppermute(rows[:, :, cells - 2 * w :], "azi", [(i, (i + 1) % n_a) for i in range(n_a)])
+
     rot = jnp.concatenate([jnp.zeros((w,), rotation.dtype), rotation, jnp.zeros((w,), rotation.dtype)])
     spin = lax.dynamic_slice_in_dim(rot, first_row, radii + 2 * w)[:, None]
     row = first_row - w + lax.iota(jnp.int32, radii + 2 * w)
@@ -83,16 +78,23 @@
     def trim(x, k):
         return x[..., k : x.shape[-2] - k, k : x.shape[-1] - k]
 
-    def rates_at(state, k):
-        return rates(state, trim(visc, k), spin[k : spin.shape[0] - k])
+    def runge_kutta(ext):
+        u0 = ext[:planes].reshape(n_f, heights, radii + 2 * w, ext.shape[-1])
+        visc = ext[planes]
 
-    def keep(state, k):
-        return jnp.where(inside[k : inside.shape[0] - k], state, 0.0)
+        def rates_at(state, k):
+            return rates(state, trim(visc, k), spin[k : spin.shape[0] - k])
 
-    state = u0
-    first = keep(trim(state, 1) + time_step * rates_at(state, 1), 1)
-    second = keep(0.75 * trim(state, 2) + 0.25 * (trim(first, 1) + time_step * rates_at(first, 2)), 2)
-    state = trim(state, 3) / 3.0 + 2.0 / 3.0 * (trim(second, 1) + time_step * rates_at(second, 3))
+        def keep(state, k):
+            return jnp.where(inside[k : inside.shape[0] - k], state, 0.0)
+
+        first = keep(trim(u0, 1) + time_step * rates_at(u0, 1), 1)
+        second = keep(0.75 * trim(u0, 2) + 0.25 * (trim(first, 1) + time_step * rates_at(first, 2)), 2)
+        return trim(u0, 3) / 3.0 + 2.0 / 3.0 * (trim(second, 1) + time_step * rates_at(second, 3))
+
+    inner = runge_kutta(rows)
+    edge = runge_kutta(jnp.concatenate([behind, rows[:, :, : 2 * w]], axis=2))
+    state = jnp.concatenate([edge, inner], axis=-1)
     for t in range(shift_blocks.shape[0]):
         state = advect(state, shift_blocks[t], first_row, w)
     return state

time: 92.1 us -> 95.1 us (1.033)
  the two profiles are of different devices: /device:TPU:1 before, /device:TPU:256 now
where the time goes in v6:
time: 95.1 us; the launch traced here: 94.8 us
  waiting for transfers between devices  39.7 us (42%)
  blocking collectives  21.5 us (23%)
  starting transfers between devices  20.7 us (22%)
  local copies, waits for them, and re-layouts  5.88 us (6%)
  other arithmetic  4.58 us (5%)
  between operations  2.45 us (3%)
    ppermute x1, waiting for transfers between devices, body(): lax.ppermute(rows[:, :, cells - 2 * w:], 'azi', [(i, (i + 1) % n_a) for i...  24.7 us
    all_to_all x1, blocking collectives, advect(): back = lax.all_to_all(rolled, 'azi', 0, 0, tiled=True)  21.5 us
    all_to_all x1, waiting for transfers between devices, advect(): ring = lax.all_to_all(lines, 'azi', 0, 0, tiled=True)  14.4 us
    all_to_all x1, starting transfers between devices, advect(): ring = lax.all_to_all(lines, 'azi', 0, 0, tiled=True)  10.4 us
    ppermute x1, starting transfers between devices, body(): north = lax.ppermute(packed[:, :w], 'rad', down)  4.85 us
    ppermute x1, starting transfers between devices, body(): lax.ppermute(rows[:, :, cells - 2 * w:], 'azi', [(i, (i + 1) % n_a) for i...  3.48 us
    ppermute x1, starting transfers between devices, body(): south = lax.ppermute(packed[:, -w:], 'rad', up)  1.92 us
  transfers between devices with their start and end apart: 4, of which 3 were waited for; matrix products, arithmetic and copies ran while one was open for 2% of the time, Pallas kernels for 0%

profile of v6, /device:TPU:256, one launch (start us, length us, event | category | flops | bytes accessed | tf_op | source)
XLA Modules:
  0.0 94.8 jit_solution(15596498491145810189)
XLA Ops:
  0.0 1.1 %fusion.37 = (f32[25,3,128]{2,1,0:T(4,128)S(1)}, f32[25,3,128]{2,1,0:T(4,128)S(1)}) fusion(f32[24,8,128]{2,1,0:T(8,128)} %bitcast.33, f32[1,8,128]{2,1,0:T(8,128)} %bitcast.38), kind=kLoop, calls=%fused_computation.77 | loop fusion | flops 19200 | bytes 179200 | tf_op jit(solution)/shard_map/concatenate | solution.py:64
  1.1 1.9 %collective-permute-start = (f32[25,3,128]{2,1,0:T(4,128)S(1)}, f32[25,3,128]{2,1,0:T(4,128)S(1)}, u32[]{:S(2)}, u32[]{:S(2)}) collective-permute-start(f32[25,3,128]{2,1,0:T(4,128)S(1)} %get-tuple-element.62), channel_id=1, source_target_pairs={{0,64},{64,128},{128,192},{192,256},{256,320},{320,384},{384,448},... | collective-permute-start | bytes 115208 | tf_op jit(solution)/shard_map/ppermute | solution.py:68
  3.0 4.9 %collective-permute-start.1 = (f32[25,3,128]{2,1,0:T(4,128)S(1)}, f32[25,3,128]{2,1,0:T(4,128)S(1)}, u32[]{:S(2)}, u32[]{:S(2)}) collective-permute-start(f32[25,3,128]{2,1,0:T(4,128)S(1)} %get-tuple-element.63), channel_id=1, source_target_pairs={{64,0},{128,64},{192,128},{256,192},{320,256},{384,320},{448,384},... | collective-permute-start | bytes 115208 | tf_op jit(solution)/shard_map/ppermute | solution.py:69
  7.9 0.6 copy-done.3
  9.1 0.5 collective-permute-done.1
  10.1 0.1 fusion.52
  10.2 0.1 fusion.53
  10.4 0.2 subtract_multiply_fusion.1
  10.9 0.1 fusion.56
  11.0 0.1 fusion.57
  11.1 0.2 subtract_multiply_fusion.3
  11.5 0.1 fusion.7
  11.9 3.5 %collective-permute-start.2 = (f32[25,14,6]{2,1,0:T(8,128)S(1)}, f32[25,14,6]{2,1,0:T(8,128)S(1)}, u32[]{:S(2)}, u32[]{:S(2)}) collective-permute-start(f32[25,14,6]{2,1,0:T(8,128)S(1)} %get-tuple-element.21), channel_id=1, source_target_pairs={{0,1},{1,2},{2,3},{3,4},{4,5},{5,6},{6,7},{7,8},{8,9},{9,10},{10,1... | collective-permute-start | bytes 25208 | tf_op jit(solution)/shard_map/ppermute | solution.py:71
  15.3 0.2 subtract_multiply_fusion.7
  15.8 24.7 %collective-permute-done.2 = f32[25,14,6]{2,1,0:T(8,128)S(1)} collective-permute-done((f32[25,14,6]{2,1,0:T(8,128)S(1)}, f32[25,14,6]{2,1,0:T(8,128)S(1)}, u32[]{:S(2)}, u32[]{:S(2)}) %collective-permute-start.2) | collective-permute-done | bytes 8432 | tf_op jit(solution)/shard_map/ppermute | solution.py:71
  40.9 0.3 copy.62
  41.2 0.1 fusion.54
  41.3 0.1 fusion.55
  41.5 0.2 subtract_multiply_fusion.5
  42.3 0.2 subtract_multiply_fusion.9
  43.0 0.2 subtract_multiply_fusion.11
  43.3 0.2 copy.67
  43.7 0.7 copy.69
  44.4 10.4 %all-to-all-start = ((f32[64,3,128]{2,1,0:T(4,128)}), f32[64,3,128]{2,1,0:T(4,128)S(1)}, u32[]{:S(2)}, u32[]{:S(2)}) async-start(f32[64,3,128]{2,1,0:T(4,128)} %copy.69), calls=%async_computation | async-start | bytes 262144 | tf_op jit(solution)/shard_map/all_to_all | solution.py:33
  54.8 0.6 constant_dynamic-slice_fusion
  57.4 14.4 %all-to-all-done = f32[64,3,128]{2,1,0:T(4,128)S(1)} async-done(((f32[64,3,128]{2,1,0:T(4,128)}), f32[64,3,128]{2,1,0:T(4,128)S(1)}, u32[]{:S(2)}, u32[]{:S(2)}) %all-to-all-start) | async-done | bytes 98336 | tf_op jit(solution)/shard_map/all_to_all | solution.py:33
  71.9 0.1 slice.729
  72.0 0.2 maximum_maximum_fusion
  72.3 0.1 fusion.58
  72.4 0.1 maximum_select_fusion
  72.6 21.5 %all_to_all.10 = f32[64,3,128]{2,1,0:T(4,128)S(1)} all-to-all(f32[64,3,128]{2,1,0:T(4,128)S(1)} %maximum_select_fusion), channel_id=1, replica_groups=mesh['rad'=12,'azi'=64] {'azi'}, dimensions={0} | all-to-all | bytes 196608 | tf_op jit(solution)/shard_map/all_to_all | solution.py:51
  94.1 0.6 copy.70
  (57 shorter events, 3.7 us)
Async XLA Ops:
  0.0 54.8 %copy-start = (s32[1,96]{1,0:T(1,128)S(1)}, s32[1,96]{1,0:T(1,128)}, u32[]{:S(2)}) copy-start(s32[1,96]{1,0:T(1,128)} %param.7) | copy-start | bytes 1156
  0.0 9.6 %copy-start.1 = (f32[3,8,8,128]{3,2,1,0:T(8,128)S(1)}, f32[3,8,8,128]{3,2,1,0:T(8,128)}, u32[]{:S(2)}) copy-start(f32[3,8,8,128]{3,2,1,0:T(8,128)} %param.4) | copy-start | bytes 294916
  1.1 8.0 %collective-permute-start = (f32[25,3,128]{2,1,0:T(4,128)S(1)}, f32[25,3,128]{2,1,0:T(4,128)S(1)}, u32[]{:S(2)}, u32[]{:S(2)}) collective-permute-start(f32[25,3,128]{2,1,0:T(4,128)S(1)} %get-tuple-element.62), channel_id=1, source_target_pairs={{0,64},{64,128},{128,192},{192,256},{256,320},{320,384},{384,448},... | collective-permute-start | bytes 115208 | tf_op jit(solution)/shard_map/ppermute | solution.py:68
  3.0 6.6 %collective-permute-start.1 = (f32[25,3,128]{2,1,0:T(4,128)S(1)}, f32[25,3,128]{2,1,0:T(4,128)S(1)}, u32[]{:S(2)}, u32[]{:S(2)}) collective-permute-start(f32[25,3,128]{2,1,0:T(4,128)S(1)} %get-tuple-element.63), channel_id=1, source_target_pairs={{64,0},{128,64},{192,128},{256,192},{320,256},{384,320},{448,384},... | collective-permute-start | bytes 115208 | tf_op jit(solution)/shard_map/ppermute | solution.py:69
  7.9 0.7 copy-start.3
  8.9 0.7 copy-start.2
  11.9 28.6 %collective-permute-start.2 = (f32[25,14,6]{2,1,0:T(8,128)S(1)}, f32[25,14,6]{2,1,0:T(8,128)S(1)}, u32[]{:S(2)}, u32[]{:S(2)}) collective-permute-start(f32[25,14,6]{2,1,0:T(8,128)S(1)} %get-tuple-element.21), channel_id=1, source_target_pairs={{0,1},{1,2},{2,3},{3,4},{4,5},{5,6},{6,7},{7,8},{8,9},{9,10},{10,1... | collective-permute-start | bytes 25208 | tf_op jit(solution)/shard_map/ppermute | solution.py:71
  44.4 27.5 %all-to-all-start = ((f32[64,3,128]{2,1,0:T(4,128)}), f32[64,3,128]{2,1,0:T(4,128)S(1)}, u32[]{:S(2)}, u32[]{:S(2)}) async-start(f32[64,3,128]{2,1,0:T(4,128)} %copy.69), calls=%async_computation | async-start | bytes 262144 | tf_op jit(solution)/shard_map/all_to_all | solution.py:33

commit v7 on v4

--- a/solution.py
+++ b/solution.py
@@ -15,9 +15,9 @@
     n_a = lax.axis_size("azi")
     up = [(i, i + 1) for i in range(n_r - 1)]
     down = [(i + 1, i) for i in range(n_r - 1)]
-    fwd = [(i, (i + 1) % n_a) for i in range(n_a)]
-    behind = lax.ppermute(cells[:, :, cells.shape[2] - 2 * width :], "azi", fwd)
-    wide = jnp.concatenate([behind, cells], axis=2)
+    back = [((i + 1) % n_a, i) for i in range(n_a)]
+    ahead = lax.ppermute(cells[:, :, : 2 * width], "azi", back)
+    wide = jnp.concatenate([cells, ahead], axis=2)
     south = lax.ppermute(wide[:, -width:, :], "rad", up)
     north = lax.ppermute(wide[:, :width, :], "rad", down)
     return jnp.concatenate([south, wide, north], axis=1)
@@ -44,7 +44,7 @@
     fields, heights, radii, cells = state.shape
     lines = jnp.swapaxes(state.reshape(fields, heights * radii, cells), 0, 1)
     ring = lax.all_to_all(lines, "azi", 0, 0, tiled=True)
-    ring = jnp.concatenate([ring[:, :, lag:], jnp.roll(ring, -1, axis=0)[:, :, :lag]], axis=2)
+    ring = jnp.concatenate([jnp.roll(ring, 1, axis=0)[:, :, cells - lag :], ring[:, :, : cells - lag]], axis=2)
     chunks = ring.shape[0]
     me = lax.axis_index("azi")
     shift = lax.dynamic_index_in_dim(shift_row, first_row + me % radii, keepdims=False)

time: 92.1 us -> 97.3 us (1.056)
  starting transfers between devices: 25.5 us -> 44.5 us
  waiting for transfers between devices: 35.5 us -> 22.4 us
    ppermute x1, starting transfers between devices: 4.03 us -> 20.8 us  [exchange_halo(): ahead = lax.ppermute(cells[:, :, :2 * width], 'azi', back)]
    ppermute x1, waiting for transfers between devices: 18.2 us -> 5.21 us  [exchange_halo(): ahead = lax.ppermute(cells[:, :, :2 * width], 'azi', back)]
    all_to_all x1, starting transfers between devices: 9.83 us -> 15.8 us  [advect(): ring = lax.all_to_all(lines, 'azi', 0, 0, tiled=True)]
    ppermute x1, starting transfers between devices: 9.76 us -> 6.04 us  [exchange_halo(): south = lax.ppermute(wide[:, -width:, :], 'rad', up)]
where the time goes in v7:
time: 97.3 us; the launch traced here: 97 us
  starting transfers between devices  44.5 us (46%)
  waiting for transfers between devices  22.4 us (23%)
  blocking collectives  19.9 us (20%)
  local copies, waits for them, and re-layouts  5.22 us (5%)
  other arithmetic  2.66 us (3%)
  between operations  2.31 us (2%)
    ppermute x1, starting transfers between devices, exchange_halo(): ahead = lax.ppermute(cells[:, :, :2 * width], 'azi', back)  20.8 us
    all_to_all x1, blocking collectives, advect(): back = lax.all_to_all(rolled, 'azi', 0, 0, tiled=True)  19.9 us
    all_to_all x1, starting transfers between devices, advect(): ring = lax.all_to_all(lines, 'azi', 0, 0, tiled=True)  15.8 us
    all_to_all x1, waiting for transfers between devices, advect(): ring = lax.all_to_all(lines, 'azi', 0, 0, tiled=True)  13.4 us
    ppermute x1, starting transfers between devices, exchange_halo(): south = lax.ppermute(wide[:, -width:, :], 'rad', up)  6.04 us
    ppermute x1, waiting for transfers between devices, exchange_halo(): ahead = lax.ppermute(cells[:, :, :2 * width], 'azi', back)  5.21 us
    ppermute x1, waiting for transfers between devices, exchange_halo(): north = lax.ppermute(wide[:, :width, :], 'rad', down)  3.84 us
  transfers between devices with their start and end apart: 4, of which 3 were waited for; matrix products, arithmetic and copies ran while one was open for 1% of the time, Pallas kernels for 0%

profile of v7, /device:TPU:1, one launch (start us, length us, event | category | flops | bytes accessed | tf_op | source)
XLA Modules:
  0.0 97.0 jit_solution(5653047027409306856)
XLA Ops:
  0.0 0.9 copy.17
  1.0 20.8 %collective-permute-start = (f32[25,8,6]{2,0,1:T(8,128)S(1)}, f32[25,8,6]{2,0,1:T(8,128)S(1)}, u32[]{:S(2)}, u32[]{:S(2)}) collective-permute-start(f32[25,8,6]{2,0,1:T(8,128)S(1)} %pad_maximum_fusion.2), channel_id=1, source_target_pairs={{1,0},{2,1},{3,2},{4,3},{5,4},{6,5},{7,6},{8,7},{9,8},{10,9},{11,1... | collective-permute-start | bytes 14408 | tf_op jit(solution)/shard_map/ppermute | solution.py:19
  21.8 0.6 copy-done.2
  22.8 5.2 %collective-permute-done = f32[25,8,6]{2,0,1:T(8,128)S(1)} collective-permute-done((f32[25,8,6]{2,0,1:T(8,128)S(1)}, f32[25,8,6]{2,0,1:T(8,128)S(1)}, u32[]{:S(2)}, u32[]{:S(2)}) %collective-permute-start) | collective-permute-done | bytes 4832 | tf_op jit(solution)/shard_map/ppermute | solution.py:19
  28.0 6.0 %collective-permute-start.1 = (f32[25,3,134]{2,0,1:T(8,128)S(1)}, f32[25,3,134]{2,0,1:T(8,128)S(1)}, u32[]{:S(2)}, u32[]{:S(2)}) collective-permute-start(f32[25,3,134]{2,0,1:T(8,128)S(1)} %get-tuple-element.35), channel_id=1, source_target_pairs={{0,64},{64,128},{128,192},{192,256},{256,320},{320,384},{384,448},... | collective-permute-start | bytes 120608 | tf_op jit(solution)/shard_map/ppermute | solution.py:21
  34.1 1.9 %collective-permute-start.2 = (f32[25,3,134]{2,0,1:T(8,128)S(1)}, f32[25,3,134]{2,0,1:T(8,128)S(1)}, u32[]{:S(2)}, u32[]{:S(2)}) collective-permute-start(f32[25,3,134]{2,0,1:T(8,128)S(1)} %get-tuple-element.36), channel_id=1, source_target_pairs={{64,0},{128,64},{192,128},{256,192},{320,256},{384,320},{448,384},... | collective-permute-start | bytes 120608 | tf_op jit(solution)/shard_map/ppermute | solution.py:22
  36.2 3.8 %collective-permute-done.2 = f32[25,3,134]{2,0,1:T(8,128)S(1)} collective-permute-done((f32[25,3,134]{2,0,1:T(8,128)S(1)}, f32[25,3,134]{2,0,1:T(8,128)S(1)}, u32[]{:S(2)}, u32[]{:S(2)}) %collective-permute-start.2) | collective-permute-done | bytes 40232 | tf_op jit(solution)/shard_map/ppermute | solution.py:22
  40.4 0.2 fusion.24
  40.6 0.2 fusion.25
  40.8 0.4 subtract_multiply_fusion.1
  41.2 0.1 fusion.13
  41.3 0.2 fusion.4
  41.5 0.2 fusion.26
  41.7 0.2 fusion.27
  41.9 0.3 subtract_multiply_fusion.3
  42.2 0.1 fusion.21
  42.4 0.2 fusion.6
  42.6 0.1 fusion.28
  42.7 0.1 fusion.29
  42.8 0.2 subtract_multiply_fusion.5
  43.0 0.1 fusion.23
  43.1 0.1 fusion.14
  43.3 0.7 copy.10
  44.0 15.8 %all-to-all-start = ((f32[64,3,128]{2,1,0:T(4,128)}), f32[64,3,128]{2,1,0:T(4,128)S(1)}, u32[]{:S(2)}, u32[]{:S(2)}) async-start(f32[64,3,128]{2,1,0:T(4,128)} %copy.10), calls=%async_computation | async-start | bytes 262144 | tf_op jit(solution)/shard_map/all_to_all | solution.py:46
  59.8 0.6 constant_dynamic-slice_fusion
  62.4 13.4 %all-to-all-done = f32[64,3,128]{2,1,0:T(4,128)S(1)} async-done(((f32[64,3,128]{2,1,0:T(4,128)}), f32[64,3,128]{2,1,0:T(4,128)S(1)}, u32[]{:S(2)}, u32[]{:S(2)}) %all-to-all-start) | async-done | bytes 98336 | tf_op jit(solution)/shard_map/all_to_all | solution.py:46
  75.8 0.1 pad_maximum_fusion.1
  75.9 0.2 maximum_maximum_fusion
  76.2 0.1 fusion.30
  76.3 0.1 maximum_select_fusion
  76.5 19.9 %all_to_all.10 = f32[64,3,128]{2,1,0:T(4,128)S(1)} all-to-all(f32[64,3,128]{2,1,0:T(4,128)S(1)} %maximum_select_fusion), channel_id=1, replica_groups=mesh['rad'=12,'azi'=64] {'azi'}, dimensions={0} | all-to-all | bytes 196608 | tf_op jit(solution)/shard_map/all_to_all | solution.py:64
  96.4 0.6 copy.11
  (29 shorter events, 1.0 us)
Async XLA Ops:
  0.0 59.8 %copy-start = (s32[1,96]{1,0:T(1,128)S(1)}, s32[1,96]{1,0:T(1,128)}, u32[]{:S(2)}) copy-start(s32[1,96]{1,0:T(1,128)} %param.7) | copy-start | bytes 1156
  0.0 0.9 copy-start.1
  1.0 27.0 %collective-permute-start = (f32[25,8,6]{2,0,1:T(8,128)S(1)}, f32[25,8,6]{2,0,1:T(8,128)S(1)}, u32[]{:S(2)}, u32[]{:S(2)}) collective-permute-start(f32[25,8,6]{2,0,1:T(8,128)S(1)} %pad_maximum_fusion.2), channel_id=1, source_target_pairs={{1,0},{2,1},{3,2},{4,3},{5,4},{6,5},{7,6},{8,7},{9,8},{10,9},{11,1... | collective-permute-start | bytes 14408 | tf_op jit(solution)/shard_map/ppermute | solution.py:19
  21.8 0.7 copy-start.2
  28.0 8.1 %collective-permute-start.1 = (f32[25,3,134]{2,0,1:T(8,128)S(1)}, f32[25,3,134]{2,0,1:T(8,128)S(1)}, u32[]{:S(2)}, u32[]{:S(2)}) collective-permute-start(f32[25,3,134]{2,0,1:T(8,128)S(1)} %get-tuple-element.35), channel_id=1, source_target_pairs={{0,64},{64,128},{128,192},{192,256},{256,320},{320,384},{384,448},... | collective-permute-start | bytes 120608 | tf_op jit(solution)/shard_map/ppermute | solution.py:21
  34.1 5.9 %collective-permute-start.2 = (f32[25,3,134]{2,0,1:T(8,128)S(1)}, f32[25,3,134]{2,0,1:T(8,128)S(1)}, u32[]{:S(2)}, u32[]{:S(2)}) collective-permute-start(f32[25,3,134]{2,0,1:T(8,128)S(1)} %get-tuple-element.36), channel_id=1, source_target_pairs={{64,0},{128,64},{192,128},{256,192},{320,256},{384,320},{448,384},... | collective-permute-start | bytes 120608 | tf_op jit(solution)/shard_map/ppermute | solution.py:22
  44.0 31.8 %all-to-all-start = ((f32[64,3,128]{2,1,0:T(4,128)}), f32[64,3,128]{2,1,0:T(4,128)S(1)}, u32[]{:S(2)}, u32[]{:S(2)}) async-start(f32[64,3,128]{2,1,0:T(4,128)} %copy.10), calls=%async_computation | async-start | bytes 262144 | tf_op jit(solution)/shard_map/all_to_all | solution.py:46

commit v8 on v4

--- a/solution.py
+++ b/solution.py
@@ -10,13 +10,13 @@
 time_step = 0.3
 
 
-def exchange_halo(cells, width):
+def exchange_halo(cells, tail, width):
     n_r = lax.axis_size("rad")
     n_a = lax.axis_size("azi")
     up = [(i, i + 1) for i in range(n_r - 1)]
     down = [(i + 1, i) for i in range(n_r - 1)]
     fwd = [(i, (i + 1) % n_a) for i in range(n_a)]
-    behind = lax.ppermute(cells[:, :, cells.shape[2] - 2 * width :], "azi", fwd)
+    behind = lax.ppermute(tail, "azi", fwd)
     wide = jnp.concatenate([behind, cells], axis=2)
     south = lax.ppermute(wide[:, -width:, :], "rad", up)
     north = lax.ppermute(wide[:, :width, :], "rad", down)
@@ -72,7 +72,10 @@
     first_row = band * radii
     total_rows = rotation.shape[0]
     packed = jnp.concatenate([fields.reshape(n_f * heights, radii, cells), viscosity[None]], axis=0)
-    ext = exchange_halo(packed, w)
+    tail = jnp.concatenate(
+        [fields[..., cells - 2 * w :].reshape(n_f * heights, radii, 2 * w), viscosity[None, :, cells - 2 * w :]], axis=0
+    )
+    ext = exchange_halo(packed, tail, w)
     u0 = ext[: n_f * heights].reshape(n_f, heights, radii + 2 * w, cells + 2 * w)
     visc = ext[n_f * heights]
     rot = jnp.concatenate([jnp.zeros((w,), rotation.dtype), rotation, jnp.zeros((w,), rotation.dtype)])

time: 92.1 us -> 89.7 us (0.974)
  the two profiles are of different devices: /device:TPU:1 before, /device:TPU:65 now
where the time goes in v8:
time: 89.7 us; the launch traced here: 89.3 us
  waiting for transfers between devices  34.9 us (39%)
  blocking collectives  21.4 us (24%)
  starting transfers between devices  20.7 us (23%)
  local copies, waits for them, and re-layouts  7.13 us (8%)
  other arithmetic  2.9 us (3%)
  between operations  2.32 us (3%)
    all_to_all x1, blocking collectives, advect(): back = lax.all_to_all(rolled, 'azi', 0, 0, tiled=True)  21.4 us
    ppermute x1, waiting for transfers between devices, exchange_halo(): behind = lax.ppermute(tail, 'azi', fwd)  16 us
    all_to_all x1, waiting for transfers between devices, advect(): ring = lax.all_to_all(lines, 'azi', 0, 0, tiled=True)  15.1 us
    all_to_all x1, starting transfers between devices, advect(): ring = lax.all_to_all(lines, 'azi', 0, 0, tiled=True)  11.6 us
    ppermute x1, starting transfers between devices, exchange_halo(): south = lax.ppermute(wide[:, -width:, :], 'rad', up)  3.93 us
    ppermute x1, waiting for transfers between devices, exchange_halo(): north = lax.ppermute(wide[:, :width, :], 'rad', down)  3.84 us
    ppermute x1, starting transfers between devices, exchange_halo(): behind = lax.ppermute(tail, 'azi', fwd)  3.2 us
    ppermute x1, starting transfers between devices, exchange_halo(): north = lax.ppermute(wide[:, :width, :], 'rad', down)  1.92 us
  transfers between devices with their start and end apart: 4, of which 3 were waited for; matrix products, arithmetic and copies ran while one was open for 1% of the time, Pallas kernels for 0%

profile of v8, /device:TPU:65, one launch (start us, length us, event | category | flops | bytes accessed | tf_op | source)
XLA Modules:
  0.0 89.3 jit_solution(1777436061875118141)
XLA Ops:
  0.0 0.8 slice_bitcast_fusion.1
  0.8 0.1 copy.22
  0.9 1.0 %slice.258 = f32[3,8,8,6]{3,2,1,0:T(8,128)S(1)} slice(f32[3,8,8,128]{3,2,1,0:T(8,128)} %param.4), slice={[0:3], [0:8], [0:8], [122:128]} | slice | bytes 9216 | tf_op jit(solution)/shard_map/slice | solution.py:76
  1.9 0.1 copy.28
  2.1 3.2 %collective-permute-start = (f32[25,8,6]{0,1,2:T(8,128)S(1)}, f32[25,8,6]{0,1,2:T(8,128)S(1)}, u32[]{:S(2)}, u32[]{:S(2)}) collective-permute-start(f32[25,8,6]{0,1,2:T(8,128)S(1)} %pad_maximum_fusion.5), channel_id=1, source_target_pairs={{0,1},{1,2},{2,3},{3,4},{4,5},{5,6},{6,7},{7,8},{8,9},{9,10},{10,1... | collective-permute-start | bytes 14408 | tf_op jit(solution)/shard_map/ppermute | solution.py:19
  5.4 0.6 copy-done.3
  6.4 16.0 %collective-permute-done = f32[25,8,6]{0,1,2:T(8,128)S(1)} collective-permute-done((f32[25,8,6]{0,1,2:T(8,128)S(1)}, f32[25,8,6]{0,1,2:T(8,128)S(1)}, u32[]{:S(2)}, u32[]{:S(2)}) %collective-permute-start) | collective-permute-done | bytes 4832 | tf_op jit(solution)/shard_map/ppermute | solution.py:19
  22.4 0.2 copy.24
  22.5 0.5 copy-done.2
  23.2 3.9 %collective-permute-start.1 = (f32[25,3,134]{2,0,1:T(8,128)S(1)}, f32[25,3,134]{2,0,1:T(8,128)S(1)}, u32[]{:S(2)}, u32[]{:S(2)}) collective-permute-start(f32[25,3,134]{2,0,1:T(8,128)S(1)} %get-tuple-element.35), channel_id=1, source_target_pairs={{0,64},{64,128},{128,192},{192,256},{256,320},{320,384},{384,448},... | collective-permute-start | bytes 120608 | tf_op jit(solution)/shard_map/ppermute | solution.py:21
  27.1 1.9 %collective-permute-start.2 = (f32[25,3,134]{2,0,1:T(8,128)S(1)}, f32[25,3,134]{2,0,1:T(8,128)S(1)}, u32[]{:S(2)}, u32[]{:S(2)}) collective-permute-start(f32[25,3,134]{2,0,1:T(8,128)S(1)} %get-tuple-element.36), channel_id=1, source_target_pairs={{64,0},{128,64},{192,128},{256,192},{320,256},{384,320},{448,384},... | collective-permute-start | bytes 120608 | tf_op jit(solution)/shard_map/ppermute | solution.py:22
  29.2 3.8 %collective-permute-done.2 = f32[25,3,134]{2,0,1:T(8,128)S(1)} collective-permute-done((f32[25,3,134]{2,0,1:T(8,128)S(1)}, f32[25,3,134]{2,0,1:T(8,128)S(1)}, u32[]{:S(2)}, u32[]{:S(2)}) %collective-permute-start.2) | collective-permute-done | bytes 40232 | tf_op jit(solution)/shard_map/ppermute | solution.py:22
  33.4 0.1 pad_maximum_fusion
  33.5 0.2 fusion.24
  33.8 0.2 fusion.25
  34.0 0.4 subtract_multiply_fusion.1
  34.4 0.1 fusion.13
  34.5 0.2 fusion.4
  34.7 0.2 fusion.26
  34.9 0.2 fusion.27
  35.1 0.3 subtract_multiply_fusion.3
  35.4 0.1 fusion.21
  35.6 0.2 fusion.6
  36.0 0.2 subtract_multiply_fusion.5
  36.5 0.7 copy.26
  37.2 11.6 %all-to-all-start = ((f32[64,3,128]{2,1,0:T(4,128)}), f32[64,3,128]{2,1,0:T(4,128)S(1)}, u32[]{:S(2)}, u32[]{:S(2)}) async-start(f32[64,3,128]{2,1,0:T(4,128)} %copy.26), calls=%async_computation | async-start | bytes 262144 | tf_op jit(solution)/shard_map/all_to_all | solution.py:46
  48.8 0.6 constant_dynamic-slice_fusion
  51.4 15.1 %all-to-all-done = f32[64,3,128]{2,1,0:T(4,128)S(1)} async-done(((f32[64,3,128]{2,1,0:T(4,128)}), f32[64,3,128]{2,1,0:T(4,128)S(1)}, u32[]{:S(2)}, u32[]{:S(2)}) %all-to-all-start) | async-done | bytes 98336 | tf_op jit(solution)/shard_map/all_to_all | solution.py:46
  66.7 0.2 maximum_maximum_fusion
  67.1 0.1 maximum_select_fusion
  67.2 21.4 %all_to_all.10 = f32[64,3,128]{2,1,0:T(4,128)S(1)} all-to-all(f32[64,3,128]{2,1,0:T(4,128)S(1)} %maximum_select_fusion), channel_id=1, replica_groups=mesh['rad'=12,'azi'=64] {'azi'}, dimensions={0} | all-to-all | bytes 196608 | tf_op jit(solution)/shard_map/all_to_all | solution.py:64
  88.6 0.6 copy.27
  (37 shorter events, 1.9 us)
Async XLA Ops:
  0.0 48.8 %copy-start = (s32[1,96]{1,0:T(1,128)S(1)}, s32[1,96]{1,0:T(1,128)}, u32[]{:S(2)}) copy-start(s32[1,96]{1,0:T(1,128)} %param.7) | copy-start | bytes 1156
  1.9 4.5 %copy-start.1 = (f32[3,8,8,128]{3,2,1,0:T(8,128)S(1)}, f32[3,8,8,128]{3,2,1,0:T(8,128)}, u32[]{:S(2)}) copy-start(f32[3,8,8,128]{3,2,1,0:T(8,128)} %param.4) | copy-start | bytes 294916
  2.1 20.3 %collective-permute-start = (f32[25,8,6]{0,1,2:T(8,128)S(1)}, f32[25,8,6]{0,1,2:T(8,128)S(1)}, u32[]{:S(2)}, u32[]{:S(2)}) collective-permute-start(f32[25,8,6]{0,1,2:T(8,128)S(1)} %pad_maximum_fusion.5), channel_id=1, source_target_pairs={{0,1},{1,2},{2,3},{3,4},{4,5},{5,6},{6,7},{7,8},{8,9},{9,10},{10,1... | collective-permute-start | bytes 14408 | tf_op jit(solution)/shard_map/ppermute | solution.py:19
  5.3 0.7 copy-start.3
  22.4 0.7 copy-start.2
  23.2 6.0 %collective-permute-start.1 = (f32[25,3,134]{2,0,1:T(8,128)S(1)}, f32[25,3,134]{2,0,1:T(8,128)S(1)}, u32[]{:S(2)}, u32[]{:S(2)}) collective-permute-start(f32[25,3,134]{2,0,1:T(8,128)S(1)} %get-tuple-element.35), channel_id=1, source_target_pairs={{0,64},{64,128},{128,192},{192,256},{256,320},{320,384},{384,448},... | collective-permute-start | bytes 120608 | tf_op jit(solution)/shard_map/ppermute | solution.py:21
  27.1 5.9 %collective-permute-start.2 = (f32[25,3,134]{2,0,1:T(8,128)S(1)}, f32[25,3,134]{2,0,1:T(8,128)S(1)}, u32[]{:S(2)}, u32[]{:S(2)}) collective-permute-start(f32[25,3,134]{2,0,1:T(8,128)S(1)} %get-tuple-element.36), channel_id=1, source_target_pairs={{64,0},{128,64},{192,128},{256,192},{320,256},{384,320},{448,384},... | collective-permute-start | bytes 120608 | tf_op jit(solution)/shard_map/ppermute | solution.py:22
  37.2 29.3 %all-to-all-start = ((f32[64,3,128]{2,1,0:T(4,128)}), f32[64,3,128]{2,1,0:T(4,128)S(1)}, u32[]{:S(2)}, u32[]{:S(2)}) async-start(f32[64,3,128]{2,1,0:T(4,128)} %copy.26), calls=%async_computation | async-start | bytes 262144 | tf_op jit(solution)/shard_map/all_to_all | solution.py:46

commit v9 on v8

--- a/solution.py
+++ b/solution.py
@@ -15,8 +15,7 @@
     n_a = lax.axis_size("azi")
     up = [(i, i + 1) for i in range(n_r - 1)]
     down = [(i + 1, i) for i in range(n_r - 1)]
-    fwd = [(i, (i + 1) % n_a) for i in range(n_a)]
-    behind = lax.ppermute(tail, "azi", fwd)
+    behind = tail
     wide = jnp.concatenate([behind, cells], axis=2)
     south = lax.ppermute(wide[:, -width:, :], "rad", up)
     north = lax.ppermute(wide[:, :width, :], "rad", down)
@@ -72,8 +71,10 @@
     first_row = band * radii
     total_rows = rotation.shape[0]
     packed = jnp.concatenate([fields.reshape(n_f * heights, radii, cells), viscosity[None]], axis=0)
+    n_a = lax.axis_size("azi")
+    got_f, got_v = lax.ppermute((fields, viscosity), "azi", [(i, (i + 1) % n_a) for i in range(n_a)])
     tail = jnp.concatenate(
-        [fields[..., cells - 2 * w :].reshape(n_f * heights, radii, 2 * w), viscosity[None, :, cells - 2 * w :]], axis=0
+        [got_f[..., cells - 2 * w :].reshape(n_f * heights, radii, 2 * w), got_v[None, :, cells - 2 * w :]], axis=0
     )
     ext = exchange_halo(packed, tail, w)
     u0 = ext[: n_f * heights].reshape(n_f, heights, radii + 2 * w, cells + 2 * w)

time: 89.7 us -> 94.9 us (1.058)
  starting transfers between devices: 20.7 us -> 29.1 us
  waiting for transfers between devices: 34.9 us -> 33 us
    all_to_all x1, starting transfers between devices: 11.6 us -> 15.2 us  [advect(): ring = lax.all_to_all(lines, 'azi', 0, 0, tiled=True)]
    ppermute x1 -> x2, starting transfers between devices: 3.2 us -> 6.53 us  [body(): lax.ppermute((fields, viscosity), 'azi', [(i, (i + 1) % n_a) for i in ran...]
    unnamed x10 -> x8, local copies, waits for them, and re-layouts: 1.21 us -> 2.1 us
    ppermute x1 -> x2, waiting for transfers between devices: 16 us -> 15.2 us  [body(): lax.ppermute((fields, viscosity), 'azi', [(i, (i + 1) % n_a) for i in ran...]
  transfers between devices with their start and end apart: 4 -> 5, of which waited for: 3 -> 4; matrix products, arithmetic and copies ran while one was open for 1% -> 2% of each run, Pallas kernels for 0% -> 0%
where the time goes in v9:
time: 94.9 us; the launch traced here: 94.5 us
  waiting for transfers between devices  33 us (35%)
  starting transfers between devices  29.1 us (31%)
  blocking collectives  20.8 us (22%)
  local copies, waits for them, and re-layouts  6.43 us (7%)
  other arithmetic  2.9 us (3%)
  between operations  2.32 us (2%)
    all_to_all x1, blocking collectives, advect(): back = lax.all_to_all(rolled, 'azi', 0, 0, tiled=True)  20.8 us
    all_to_all x1, starting transfers between devices, advect(): ring = lax.all_to_all(lines, 'azi', 0, 0, tiled=True)  15.2 us
    ppermute x2, waiting for transfers between devices, body(): lax.ppermute((fields, viscosity), 'azi', [(i, (i + 1) % n_a) for i in ran...  15.2 us
    all_to_all x1, waiting for transfers between devices, advect(): ring = lax.all_to_all(lines, 'azi', 0, 0, tiled=True)  14.6 us
    ppermute x2, starting transfers between devices, body(): lax.ppermute((fields, viscosity), 'azi', [(i, (i + 1) % n_a) for i in ran...  6.53 us
    ppermute x1, starting transfers between devices, exchange_halo(): south = lax.ppermute(wide[:, -width:, :], 'rad', up)  4.81 us
    ppermute x1, waiting for transfers between devices, exchange_halo(): north = lax.ppermute(wide[:, :width, :], 'rad', down)  3.22 us
    ppermute x1, starting transfers between devices, exchange_halo(): north = lax.ppermute(wide[:, :width, :], 'rad', down)  2.54 us
  transfers between devices with their start and end apart: 5, of which 4 were waited for; matrix products, arithmetic and copies ran while one was open for 2% of the time, Pallas kernels for 0%

profile of v9, /device:TPU:65, one launch (start us, length us, event | category | flops | bytes accessed | tf_op | source)
XLA Modules:
  0.0 94.5 jit_solution(1750999586802769244)
XLA Ops:
  0.0 3.3 %collective-permute-start.1 = (f32[8,128]{1,0:T(8,128)}, f32[8,128]{1,0:T(8,128)S(1)}, u32[]{:S(2)}, u32[]{:S(2)}) collective-permute-start(f32[8,128]{1,0:T(8,128)} %param.5), channel_id=1, source_target_pairs={{0,1},{1,2},{2,3},{3,4},{4,5},{5,6},{6,7},{7,8},{8,9},{9,10},{10,1... | collective-permute-start | bytes 12296 | tf_op jit(solution)/shard_map/ppermute | solution.py:75
  3.3 3.2 %collective-permute-start = (f32[3,8,8,128]{3,2,1,0:T(8,128)}, f32[3,8,8,128]{3,2,1,0:T(8,128)S(1)}, u32[]{:S(2)}, u32[]{:S(2)}) collective-permute-start(f32[3,8,8,128]{3,2,1,0:T(8,128)} %param.4), channel_id=1, source_target_pairs={{0,1},{1,2},{2,3},{3,4},{4,5},{5,6},{6,7},{7,8},{8,9},{9,10},{10,1... | collective-permute-start | bytes 294920 | tf_op jit(solution)/shard_map/ppermute | solution.py:75
  6.6 0.6 copy-done.2
  7.6 0.9 copy.34
  8.5 11.9 %collective-permute-done.1 = f32[8,128]{1,0:T(8,128)S(1)} collective-permute-done((f32[8,128]{1,0:T(8,128)}, f32[8,128]{1,0:T(8,128)S(1)}, u32[]{:S(2)}, u32[]{:S(2)}) %collective-permute-start.1) | collective-permute-done | bytes 4128 | tf_op jit(solution)/shard_map/ppermute | solution.py:75
  20.5 0.1 copy.22
  20.6 3.3 %collective-permute-done = f32[3,8,8,128]{3,2,1,0:T(8,128)S(1)} collective-permute-done((f32[3,8,8,128]{3,2,1,0:T(8,128)}, f32[3,8,8,128]{3,2,1,0:T(8,128)S(1)}, u32[]{:S(2)}, u32[]{:S(2)}) %collective-permute-start) | collective-permute-done | bytes 98336 | tf_op jit(solution)/shard_map/ppermute | solution.py:75
  24.2 0.2 copy.24
  24.4 0.5 copy-done.1
  25.0 4.8 %collective-permute-start.2 = (f32[25,3,134]{2,0,1:T(8,128)S(1)}, f32[25,3,134]{2,0,1:T(8,128)S(1)}, u32[]{:S(2)}, u32[]{:S(2)}) collective-permute-start(f32[25,3,134]{2,0,1:T(8,128)S(1)} %get-tuple-element.35), channel_id=1, source_target_pairs={{0,64},{64,128},{128,192},{192,256},{256,320},{320,384},{384,448},... | collective-permute-start | bytes 120608 | tf_op jit(solution)/shard_map/ppermute | solution.py:20
  29.8 2.5 %collective-permute-start.3 = (f32[25,3,134]{2,0,1:T(8,128)S(1)}, f32[25,3,134]{2,0,1:T(8,128)S(1)}, u32[]{:S(2)}, u32[]{:S(2)}) collective-permute-start(f32[25,3,134]{2,0,1:T(8,128)S(1)} %get-tuple-element.36), channel_id=1, source_target_pairs={{64,0},{128,64},{192,128},{256,192},{320,256},{384,320},{448,384},... | collective-permute-start | bytes 120608 | tf_op jit(solution)/shard_map/ppermute | solution.py:21
  32.5 3.2 %collective-permute-done.3 = f32[25,3,134]{2,0,1:T(8,128)S(1)} collective-permute-done((f32[25,3,134]{2,0,1:T(8,128)S(1)}, f32[25,3,134]{2,0,1:T(8,128)S(1)}, u32[]{:S(2)}, u32[]{:S(2)}) %collective-permute-start.3) | collective-permute-done | bytes 40232 | tf_op jit(solution)/shard_map/ppermute | solution.py:21
  36.1 0.1 pad_maximum_fusion
  36.2 0.2 fusion.24
  36.5 0.2 fusion.25
  36.7 0.4 subtract_multiply_fusion.1
  37.1 0.1 fusion.13
  37.2 0.2 fusion.4
  37.4 0.2 fusion.26
  37.6 0.2 fusion.27
  37.8 0.3 subtract_multiply_fusion.3
  38.1 0.1 fusion.21
  38.3 0.2 fusion.6
  38.7 0.2 subtract_multiply_fusion.5
  39.2 0.7 copy.26
  39.9 15.2 %all-to-all-start = ((f32[64,3,128]{2,1,0:T(4,128)}), f32[64,3,128]{2,1,0:T(4,128)S(1)}, u32[]{:S(2)}, u32[]{:S(2)}) async-start(f32[64,3,128]{2,1,0:T(4,128)} %copy.26), calls=%async_computation | async-start | bytes 262144 | tf_op jit(solution)/shard_map/all_to_all | solution.py:45
  55.1 0.6 constant_dynamic-slice_fusion
  57.7 14.6 %all-to-all-done = f32[64,3,128]{2,1,0:T(4,128)S(1)} async-done(((f32[64,3,128]{2,1,0:T(4,128)}), f32[64,3,128]{2,1,0:T(4,128)S(1)}, u32[]{:S(2)}, u32[]{:S(2)}) %all-to-all-start) | async-done | bytes 98336 | tf_op jit(solution)/shard_map/all_to_all | solution.py:45
  72.5 0.2 maximum_maximum_fusion
  72.9 0.1 maximum_select_fusion
  73.1 20.8 %all_to_all.10 = f32[64,3,128]{2,1,0:T(4,128)S(1)} all-to-all(f32[64,3,128]{2,1,0:T(4,128)S(1)} %maximum_select_fusion), channel_id=1, replica_groups=mesh['rad'=12,'azi'=64] {'azi'}, dimensions={0} | all-to-all | bytes 196608 | tf_op jit(solution)/shard_map/all_to_all | solution.py:63
  93.9 0.6 copy.27
  (37 shorter events, 2.2 us)
Async XLA Ops:
  0.0 55.1 %copy-start = (s32[1,96]{1,0:T(1,128)S(1)}, s32[1,96]{1,0:T(1,128)}, u32[]{:S(2)}) copy-start(s32[1,96]{1,0:T(1,128)} %param.7) | copy-start | bytes 1156
  0.0 20.4 %collective-permute-start.1 = (f32[8,128]{1,0:T(8,128)}, f32[8,128]{1,0:T(8,128)S(1)}, u32[]{:S(2)}, u32[]{:S(2)}) collective-permute-start(f32[8,128]{1,0:T(8,128)} %param.5), channel_id=1, source_target_pairs={{0,1},{1,2},{2,3},{3,4},{4,5},{5,6},{6,7},{7,8},{8,9},{9,10},{10,1... | collective-permute-start | bytes 12296 | tf_op jit(solution)/shard_map/ppermute | solution.py:75
  3.3 20.6 %collective-permute-start = (f32[3,8,8,128]{3,2,1,0:T(8,128)}, f32[3,8,8,128]{3,2,1,0:T(8,128)S(1)}, u32[]{:S(2)}, u32[]{:S(2)}) collective-permute-start(f32[3,8,8,128]{3,2,1,0:T(8,128)} %param.4), channel_id=1, source_target_pairs={{0,1},{1,2},{2,3},{3,4},{4,5},{5,6},{6,7},{7,8},{8,9},{9,10},{10,1... | collective-permute-start | bytes 294920 | tf_op jit(solution)/shard_map/ppermute | solution.py:75
  6.6 0.7 copy-start.2
  24.2 0.7 copy-start.1
  25.0 7.5 %collective-permute-start.2 = (f32[25,3,134]{2,0,1:T(8,128)S(1)}, f32[25,3,134]{2,0,1:T(8,128)S(1)}, u32[]{:S(2)}, u32[]{:S(2)}) collective-permute-start(f32[25,3,134]{2,0,1:T(8,128)S(1)} %get-tuple-element.35), channel_id=1, source_target_pairs={{0,64},{64,128},{128,192},{192,256},{256,320},{320,384},{384,448},... | collective-permute-start | bytes 120608 | tf_op jit(solution)/shard_map/ppermute | solution.py:20
  29.8 5.9 %collective-permute-start.3 = (f32[25,3,134]{2,0,1:T(8,128)S(1)}, f32[25,3,134]{2,0,1:T(8,128)S(1)}, u32[]{:S(2)}, u32[]{:S(2)}) collective-permute-start(f32[25,3,134]{2,0,1:T(8,128)S(1)} %get-tuple-element.36), channel_id=1, source_target_pairs={{64,0},{128,64},{192,128},{256,192},{320,256},{384,320},{448,384},... | collective-permute-start | bytes 120608 | tf_op jit(solution)/shard_map/ppermute | solution.py:21
  39.9 32.4 %all-to-all-start = ((f32[64,3,128]{2,1,0:T(4,128)}), f32[64,3,128]{2,1,0:T(4,128)S(1)}, u32[]{:S(2)}, u32[]{:S(2)}) async-start(f32[64,3,128]{2,1,0:T(4,128)} %copy.26), calls=%async_computation | async-start | bytes 262144 | tf_op jit(solution)/shard_map/all_to_all | solution.py:45

commit v10 on v8

--- a/solution.py
+++ b/solution.py
@@ -2,6 +2,8 @@
 import jax.numpy as jnp
 from jax import lax
 from jax.sharding import PartitionSpec as P
+from jax.experimental import pallas as pl
+from jax.experimental.pallas import tpu as pltpu
 
 BLOCK = 64
 HALO = 3
@@ -40,6 +42,40 @@
     return jnp.stack([rate_density, rate_radial, rate_azimuth])
 
 
+def runge_kutta_kernel(ext_ref, spin_ref, inside_ref, out_ref):
+    n_f, heights, radii, cells = out_ref.shape
+    ext = ext_ref[...]
+    planes = n_f * heights
+    u0 = ext[:planes]
+    visc = ext[planes]
+    spin = spin_ref[...]
+    inside = inside_ref[...] > 0.0
+    rows = ext.shape[1]
+    cols = ext.shape[2]
+
+    def rates_all(u):
+        north = pltpu.roll(u, rows - 1, 1)
+        south = pltpu.roll(u, 1, 1)
+        ahead = pltpu.roll(u, cols - 1, 2)
+        behind = pltpu.roll(u, 1, 2)
+        c = u.reshape(n_f, heights, rows, cols)
+        above = jnp.concatenate([c[:, 1:], c[:, heights - 1 :]], axis=1).reshape(u.shape)
+        below = jnp.concatenate([c[:, :1], c[:, : heights - 1]], axis=1).reshape(u.shape)
+        spread = (visc * (north + south + ahead + behind + above + below - 6.0 * u)).reshape(c.shape)
+        radial_grad = (0.5 * (north - south)).reshape(c.shape)
+        azimuth_grad = (0.5 * (ahead - behind)).reshape(c.shape)
+        rate_density = spread[0] - radial_grad[1] - azimuth_grad[2]
+        rate_radial = spread[1] - radial_grad[0] + 2.0 * spin * c[2]
+        rate_azimuth = spread[2] - azimuth_grad[0] - 0.5 * spin * c[1]
+        return jnp.concatenate([rate_density, rate_radial, rate_azimuth], axis=0)
+
+    first = jnp.where(inside, u0 + time_step * rates_all(u0), 0.0)
+    second = jnp.where(inside, 0.75 * u0 + 0.25 * (first + time_step * rates_all(first)), 0.0)
+    final = u0 / 3.0 + 2.0 / 3.0 * (second + time_step * rates_all(second))
+    final = pltpu.roll(pltpu.roll(final, rows - HALO, 1), cols - HALO, 2)
+    out_ref[...] = final[:, :radii, :cells].reshape(out_ref.shape)
+
+
 def advect(state, shift_row, first_row, lag):
     fields, heights, radii, cells = state.shape
     lines = jnp.swapaxes(state.reshape(fields, heights * radii, cells), 0, 1)
@@ -76,26 +112,20 @@
         [fields[..., cells - 2 * w :].reshape(n_f * heights, radii, 2 * w), viscosity[None, :, cells - 2 * w :]], axis=0
     )
     ext = exchange_halo(packed, tail, w)
-    u0 = ext[: n_f * heights].reshape(n_f, heights, radii + 2 * w, cells + 2 * w)
-    visc = ext[n_f * heights]
     rot = jnp.concatenate([jnp.zeros((w,), rotation.dtype), rotation, jnp.zeros((w,), rotation.dtype)])
-    spin = lax.dynamic_slice_in_dim(rot, first_row, radii + 2 * w)[:, None]
+    spin = lax.dynamic_slice_in_dim(rot, first_row, radii + 2 * w)
     row = first_row - w + lax.iota(jnp.int32, radii + 2 * w)
-    inside = ((row >= 0) & (row < total_rows))[:, None]
-
-    def trim(x, k):
-        return x[..., k : x.shape[-2] - k, k : x.shape[-1] - k]
-
-    def rates_at(state, k):
-        return rates(state, trim(visc, k), spin[k : spin.shape[0] - k])
-
-    def keep(state, k):
-        return jnp.where(inside[k : inside.shape[0] - k], state, 0.0)
-
-    state = u0
-    first = keep(trim(state, 1) + time_step * rates_at(state, 1), 1)
-    second = keep(0.75 * trim(state, 2) + 0.25 * (trim(first, 1) + time_step * rates_at(first, 2)), 2)
-    state = trim(state, 3) / 3.0 + 2.0 / 3.0 * (trim(second, 1) + time_step * rates_at(second, 3))
+    inside = ((row >= 0) & (row < total_rows)).astype(jnp.float32)
+    pad_rows = -(-(radii + 2 * w) // 8) * 8
+    pad_cols = -(-(cells + 2 * w) // 128) * 128
+    extra = pad_rows - (radii + 2 * w)
+    ext = jnp.pad(ext, ((0, 0), (0, extra), (0, pad_cols - cells - 2 * w)))
+    spin = jnp.broadcast_to(jnp.pad(spin, (0, extra))[:, None], (pad_rows, pad_cols))
+    inside = jnp.broadcast_to(jnp.pad(inside, (0, extra))[:, None], (pad_rows, pad_cols))
+    state = pl.pallas_call(
+        runge_kutta_kernel,
+        out_shape=jax.ShapeDtypeStruct((n_f, heights, radii, cells), fields.dtype),
+    )(ext, spin, inside)
     for t in range(shift_blocks.shape[0]):
         state = advect(state, shift_blocks[t], first_row, w)
     return state

time: 89.7 us -> 93.7 us (1.045)
  the two profiles are of different devices: /device:TPU:65 before, /device:TPU:64 now
where the time goes in v10:
time: 93.7 us; the launch traced here: 93.3 us
  waiting for transfers between devices  41.5 us (44%)
  blocking collectives  22.7 us (24%)
  starting transfers between devices  15.9 us (17%)
  local copies, waits for them, and re-layouts  6.34 us (7%)
  Pallas kernels  3.02 us (3%)
  between operations  2.23 us (2%)
  other arithmetic  1.61 us (2%)
    ppermute x1, waiting for transfers between devices, exchange_halo(): behind = lax.ppermute(tail, 'azi', fwd)  23.1 us
    all_to_all x1, blocking collectives, advect(): back = lax.all_to_all(rolled, 'azi', 0, 0, tiled=True)  22.7 us
    all_to_all x1, waiting for transfers between devices, advect(): ring = lax.all_to_all(lines, 'azi', 0, 0, tiled=True)  15 us
    all_to_all x1, starting transfers between devices, advect(): ring = lax.all_to_all(lines, 'azi', 0, 0, tiled=True)  8 us
    ppermute x1, starting transfers between devices, exchange_halo(): behind = lax.ppermute(tail, 'azi', fwd)  3.62 us
    ppermute x1, waiting for transfers between devices, exchange_halo(): south = lax.ppermute(wide[:, -width:, :], 'rad', up)  3.38 us
    pallas_call x1, Pallas kernels, body(): pl.pallas_call(runge_kutta_kernel, out_shape=jax.ShapeDtypeStruct((n_f, h...  3.02 us
    ppermute x1, starting transfers between devices, exchange_halo(): south = lax.ppermute(wide[:, -width:, :], 'rad', up)  2.41 us
  transfers between devices with their start and end apart: 4, of which 3 were waited for; matrix products, arithmetic and copies ran while one was open for 1% of the time, Pallas kernels for 0%

profile of v10, /device:TPU:64, one launch (start us, length us, event | category | flops | bytes accessed | tf_op | source)
XLA Modules:
  0.0 93.3 jit_solution(12166963915951274840)
XLA Ops:
  0.0 0.0 copy-start
  0.0 0.8 slice_bitcast_fusion
  0.8 1.0 %slice.34 = f32[3,8,8,6]{3,2,1,0:T(8,128)S(1)} slice(f32[3,8,8,128]{3,2,1,0:T(8,128)} %param.4), slice={[0:3], [0:8], [0:8], [122:128]} | slice | bytes 9216 | tf_op jit(solution)/shard_map/slice | solution.py:112
  1.8 0.0 copy-start.1
  1.8 3.6 %collective-permute-start = (f32[25,8,6]{2,1,0:T(8,128)S(1)}, f32[25,8,6]{2,1,0:T(8,128)S(1)}, u32[]{:S(2)}, u32[]{:S(2)}) collective-permute-start(f32[25,8,6]{2,1,0:T(8,128)S(1)} %pad_maximum_fusion.1), channel_id=1, source_target_pairs={{0,1},{1,2},{2,3},{3,4},{4,5},{5,6},{6,7},{7,8},{8,9},{9,10},{10,1... | collective-permute-start | bytes 14408 | tf_op jit(solution)/shard_map/ppermute | solution.py:21
  5.4 0.0 copy-start.2
  5.5 23.1 %collective-permute-done = f32[25,8,6]{2,1,0:T(8,128)S(1)} collective-permute-done((f32[25,8,6]{2,1,0:T(8,128)S(1)}, f32[25,8,6]{2,1,0:T(8,128)S(1)}, u32[]{:S(2)}, u32[]{:S(2)}) %collective-permute-start) | collective-permute-done | bytes 4832 | tf_op jit(solution)/shard_map/ppermute | solution.py:21
  28.5 0.0 copy-done.1
  28.5 0.0 copy-done.2
  28.5 0.1 maximum_maximum_fusion.1
  28.7 1.9 %collective-permute-start.2 = (f32[25,3,134]{2,1,0:T(4,128)S(1)}, f32[25,3,134]{2,1,0:T(4,128)S(1)}, u32[]{:S(2)}, u32[]{:S(2)}) collective-permute-start(f32[25,3,134]{2,1,0:T(4,128)S(1)} %get-tuple-element.6), channel_id=1, source_target_pairs={{64,0},{128,64},{192,128},{256,192},{320,256},{384,320},{448,384},... | collective-permute-start | bytes 120608 | tf_op jit(solution)/shard_map/ppermute | solution.py:24
  30.6 0.0 copy-start.3
  30.6 2.4 %collective-permute-start.1 = (f32[25,3,134]{2,1,0:T(4,128)S(1)}, f32[25,3,134]{2,1,0:T(4,128)S(1)}, u32[]{:S(2)}, u32[]{:S(2)}) collective-permute-start(f32[25,3,134]{2,1,0:T(4,128)S(1)} %get-tuple-element.5), channel_id=1, source_target_pairs={{0,64},{64,128},{128,192},{192,256},{256,320},{320,384},{384,448},... | collective-permute-start | bytes 120608 | tf_op jit(solution)/shard_map/ppermute | solution.py:23
  33.1 0.0 copy-done.3
  33.1 0.1 pad_maximum_fusion.2
  33.2 0.1 dynamic_slice.14
  33.2 0.0 collective-permute-done.2
  33.2 3.4 %collective-permute-done.1 = f32[25,3,134]{2,1,0:T(4,128)S(1)} collective-permute-done((f32[25,3,134]{2,1,0:T(4,128)S(1)}, f32[25,3,134]{2,1,0:T(4,128)S(1)}, u32[]{:S(2)}, u32[]{:S(2)}) %collective-permute-start.1) | collective-permute-done | bytes 40232 | tf_op jit(solution)/shard_map/ppermute | solution.py:23
  36.6 1.0 %select_maximum_fusion.ext_ref = f32[25,16,256]{2,1,0:T(8,128)} fusion(f32[25,3,134]{2,1,0:T(4,128)S(1)} %collective-permute-done.2, f32[25,3,134]{2,1,0:T(4,128)S(1)} %collective-permute-done.1, f32[25,8,6]{2,1,0:T(8,128)S(1)} %collective-permute-done, f32[1,8,128]{2,1,0:T(8,128)S(1)} %bitcast.19, f32[24,8,128]{2,1,0:T(8,128)S(1)} %bitcast.14), kind=kLoop, calls=%fused_computation | loop fusion | flops 1740800 | bytes 597200 | tf_op jit(solution)/shard_map/concatenate | solution.py:25
  37.6 0.7 broadcast_in_dim.20.spin_ref
  38.3 0.7 broadcast_in_dim.21.inside_ref
  38.9 3.0 %shard_map.46 = f32[3,8,8,128]{3,2,1,0:T(8,128)} custom-call(f32[25,16,256]{2,1,0:T(8,128)} %select_maximum_fusion.ext_ref, f32[16,256]{1,0:T(8,128)} %broadcast_in_dim.20.spin_ref, f32[16,256]{1,0:T(8,128)} %broadcast_in_dim.21.inside_ref), custom_call_target="tpu_custom_call" | custom-call | tf_op jit(solution)/shard_map/pallas_call | solution.py:125
  41.9 1.6 %copy.21 = f32[3,64,128]{2,0,1:T(4,128)} copy(f32[3,64,128]{2,1,0:T(8,128)} %bitcast.17) | data formatting | bytes 196608 | tf_op jit(solution)/shard_map/reshape | solution.py:81
  43.5 8.0 %all-to-all-start = ((f32[64,3,128]{2,1,0:T(4,128)}), f32[64,3,128]{2,1,0:T(4,128)S(1)}, u32[]{:S(2)}, u32[]{:S(2)}) async-start(f32[64,3,128]{2,1,0:T(4,128)} %bitcast.12), calls=%async_computation | async-start | bytes 262144 | tf_op jit(solution)/shard_map/all_to_all | solution.py:82
  51.6 0.6 constant_dynamic-slice_fusion
  54.2 15.0 %all-to-all-done = f32[64,3,128]{2,1,0:T(4,128)S(1)} async-done(((f32[64,3,128]{2,1,0:T(4,128)}), f32[64,3,128]{2,1,0:T(4,128)S(1)}, u32[]{:S(2)}, u32[]{:S(2)}) %all-to-all-start) | async-done | bytes 98336 | tf_op jit(solution)/shard_map/all_to_all | solution.py:82
  69.3 0.1 slice.46
  69.4 0.2 maximum_maximum_fusion
  69.7 0.1 fusion.10
  69.8 0.1 maximum_select_fusion
  70.0 22.7 %all_to_all.10 = f32[64,3,128]{2,1,0:T(4,128)S(1)} all-to-all(f32[64,3,128]{2,1,0:T(4,128)S(1)} %maximum_select_fusion), channel_id=1, replica_groups=mesh['rad'=12,'azi'=64] {'azi'}, dimensions={0} | all-to-all | bytes 196608 | tf_op jit(solution)/shard_map/all_to_all | solution.py:100
  92.7 0.6 copy.18
  (12 shorter events, 0.2 us)
Async XLA Ops:
  0.0 51.6 %copy-start = (s32[1,96]{1,0:T(1,128)S(1)}, s32[1,96]{1,0:T(1,128)}, u32[]{:S(2)}) copy-start(s32[1,96]{1,0:T(1,128)} %param.7) | copy-start | bytes 1156
  1.8 26.8 %copy-start.1 = (f32[3,8,8,128]{3,2,1,0:T(8,128)S(1)}, f32[3,8,8,128]{3,2,1,0:T(8,128)}, u32[]{:S(2)}) copy-start(f32[3,8,8,128]{3,2,1,0:T(8,128)} %param.4) | copy-start | bytes 294916
  1.8 26.8 %collective-permute-start = (f32[25,8,6]{2,1,0:T(8,128)S(1)}, f32[25,8,6]{2,1,0:T(8,128)S(1)}, u32[]{:S(2)}, u32[]{:S(2)}) collective-permute-start(f32[25,8,6]{2,1,0:T(8,128)S(1)} %pad_maximum_fusion.1), channel_id=1, source_target_pairs={{0,1},{1,2},{2,3},{3,4},{4,5},{5,6},{6,7},{7,8},{8,9},{9,10},{10,1... | collective-permute-start | bytes 14408 | tf_op jit(solution)/shard_map/ppermute | solution.py:21
  5.4 23.1 %copy-start.2 = (f32[8,128]{1,0:T(8,128)S(1)}, f32[8,128]{1,0:T(8,128)}, u32[]{:S(2)}) copy-start(f32[8,128]{1,0:T(8,128)} %param.5) | copy-start | bytes 12292
  28.7 4.5 %collective-permute-start.2 = (f32[25,3,134]{2,1,0:T(4,128)S(1)}, f32[25,3,134]{2,1,0:T(4,128)S(1)}, u32[]{:S(2)}, u32[]{:S(2)}) collective-permute-start(f32[25,3,134]{2,1,0:T(4,128)S(1)} %get-tuple-element.6), channel_id=1, source_target_pairs={{64,0},{128,64},{192,128},{256,192},{320,256},{384,320},{448,384},... | collective-permute-start | bytes 120608 | tf_op jit(solution)/shard_map/ppermute | solution.py:24
  30.6 2.4 %copy-start.3 = (f32[96]{0:T(128)S(1)}, f32[96]{0:T(128)}, u32[]{:S(2)}) copy-start(f32[96]{0:T(128)} %param.6) | copy-start | bytes 1156
  30.6 6.0 %collective-permute-start.1 = (f32[25,3,134]{2,1,0:T(4,128)S(1)}, f32[25,3,134]{2,1,0:T(4,128)S(1)}, u32[]{:S(2)}, u32[]{:S(2)}) collective-permute-start(f32[25,3,134]{2,1,0:T(4,128)S(1)} %get-tuple-element.5), channel_id=1, source_target_pairs={{0,64},{64,128},{128,192},{192,256},{256,320},{320,384},{384,448},... | collective-permute-start | bytes 120608 | tf_op jit(solution)/shard_map/ppermute | solution.py:23
  43.5 25.7 %all-to-all-start = ((f32[64,3,128]{2,1,0:T(4,128)}), f32[64,3,128]{2,1,0:T(4,128)S(1)}, u32[]{:S(2)}, u32[]{:S(2)}) async-start(f32[64,3,128]{2,1,0:T(4,128)} %bitcast.12), calls=%async_computation | async-start | bytes 262144 | tf_op jit(solution)/shard_map/all_to_all | solution.py:82

commit v11 on v8

--- a/solution.py
+++ b/solution.py
@@ -1,10 +1,11 @@
 import jax
 import jax.numpy as jnp
 from jax import lax
-from jax.sharding import PartitionSpec as P
+from jax.sharding import Mesh, PartitionSpec as P
 
 BLOCK = 64
 HALO = 3
+AZI = ("zh", "xy")
 
 
 time_step = 0.3
@@ -12,11 +13,11 @@
 
 def exchange_halo(cells, tail, width):
     n_r = lax.axis_size("rad")
-    n_a = lax.axis_size("azi")
+    n_a = lax.axis_size(AZI)
     up = [(i, i + 1) for i in range(n_r - 1)]
     down = [(i + 1, i) for i in range(n_r - 1)]
     fwd = [(i, (i + 1) % n_a) for i in range(n_a)]
-    behind = lax.ppermute(tail, "azi", fwd)
+    behind = lax.ppermute(tail, AZI, fwd)
     wide = jnp.concatenate([behind, cells], axis=2)
     south = lax.ppermute(wide[:, -width:, :], "rad", up)
     north = lax.ppermute(wide[:, :width, :], "rad", down)
@@ -42,26 +43,38 @@
 
 def advect(state, shift_row, first_row, lag):
     fields, heights, radii, cells = state.shape
-    lines = jnp.swapaxes(state.reshape(fields, heights * radii, cells), 0, 1)
-    ring = lax.all_to_all(lines, "azi", 0, 0, tiled=True)
-    ring = jnp.concatenate([ring[:, :, lag:], jnp.roll(ring, -1, axis=0)[:, :, :lag]], axis=2)
+    n_lines = heights * radii
+    n_half = lax.axis_size("xy")
+    per = n_lines // n_half
+    lines = jnp.swapaxes(state.reshape(fields, n_lines, cells), 0, 1).reshape(n_half, per * fields, cells)
+    ring = lax.all_to_all(lines, "xy", 0, 0, tiled=True)
+    other = lax.ppermute(ring, "zh", [(0, 1), (1, 0)])
+    upper = lax.axis_index("zh")
+    ring = jnp.where(upper == 0, jnp.concatenate([ring, other], axis=0), jnp.concatenate([other, ring], axis=0))
     chunks = ring.shape[0]
-    me = lax.axis_index("azi")
-    shift = lax.dynamic_index_in_dim(shift_row, first_row + me % radii, keepdims=False)
+    ring = ring.reshape(chunks, per, fields, cells)
+    ring = jnp.concatenate([ring[..., lag:], jnp.roll(ring, -1, axis=0)[..., :lag]], axis=-1)
+    me = lax.axis_index("xy")
     per_chunk = cells // BLOCK
     count = chunks * per_chunk
-    shift = shift % count
-    whole = shift // per_chunk
-    part = shift % per_chunk
     doubled = jnp.concatenate([ring, ring], axis=0)
-    lane = lax.broadcasted_iota(jnp.int32, ring.shape, 2)
-    base = lax.dynamic_slice_in_dim(doubled, (chunks - whole) % chunks, chunks, 0)
-    earlier = lax.dynamic_slice_in_dim(doubled, (chunks - whole - 1) % chunks, chunks, 0)
-    rolled = base
-    for step in range(1, per_chunk):
-        mixed = jnp.roll(jnp.where(lane < cells - step * BLOCK, base, earlier), step * BLOCK, axis=2)
-        rolled = jnp.where(part == step, mixed, rolled)
-    back = lax.all_to_all(rolled, "azi", 0, 0, tiled=True)
+    lane = lax.broadcasted_iota(jnp.int32, (chunks, fields, cells), 2)
+    mine = []
+    for t in range(per):
+        line = doubled[:, t]
+        shift = lax.dynamic_index_in_dim(shift_row, first_row + (me * per + t) % radii, keepdims=False)
+        shift = shift % count
+        whole = shift // per_chunk
+        part = shift % per_chunk
+        base = lax.dynamic_slice_in_dim(line, (chunks - whole) % chunks, chunks, 0)
+        earlier = lax.dynamic_slice_in_dim(line, (chunks - whole - 1) % chunks, chunks, 0)
+        rolled = base
+        for step in range(1, per_chunk):
+            mixed = jnp.roll(jnp.where(lane < cells - step * BLOCK, base, earlier), step * BLOCK, axis=2)
+            rolled = jnp.where(part == step, mixed, rolled)
+        mine.append(lax.dynamic_slice_in_dim(rolled, upper * n_half, n_half, 0))
+    out = jnp.stack(mine, axis=1).reshape(n_half, per * fields, cells)
+    back = lax.all_to_all(out, "xy", 0, 0, tiled=True).reshape(n_lines, fields, cells)
     return jnp.swapaxes(back, 0, 1).reshape(fields, heights, radii, cells)
 
 
@@ -102,10 +115,12 @@
 
 
 def solution(mesh):
+    n_r, n_a = mesh.devices.shape
+    halves = Mesh(mesh.devices.reshape(n_r, 2, n_a // 2), ("rad",) + AZI)
     return jax.shard_map(
         body,
-        mesh=mesh,
-        in_specs=(P(None, None, "rad", "azi"), P("rad", "azi"), P(), P()),
-        out_specs=P(None, None, "rad", "azi"),
+        mesh=halves,
+        in_specs=(P(None, None, "rad", AZI), P("rad", AZI), P(), P()),
+        out_specs=P(None, None, "rad", AZI),
         check_vma=False,
     )

time: 89.7 us -> 90.2 us (level)
  the two profiles are of different devices: /device:TPU:65 before, /device:TPU:64 now
where the time goes in v11:
time: 90.2 us; the launch traced here: 89.7 us
  waiting for transfers between devices  36.3 us (40%)
  starting transfers between devices  19.1 us (21%)
  blocking collectives  15.5 us (17%)
  local copies, waits for them, and re-layouts  7.95 us (9%)
  other arithmetic  6.4 us (7%)
  between operations  4.43 us (5%)
    ppermute x1, waiting for transfers between devices, exchange_halo(): behind = lax.ppermute(tail, AZI, fwd)  17.2 us
    all_to_all x1, blocking collectives, advect(): lax.all_to_all(out, 'xy', 0, 0, tiled=True).reshape(n_lines, fields, cells)  15.5 us
    ppermute x1, waiting for transfers between devices, advect(): other = lax.ppermute(ring, 'zh', [(0, 1), (1, 0)])  7.9 us
    ppermute x1, starting transfers between devices, advect(): other = lax.ppermute(ring, 'zh', [(0, 1), (1, 0)])  7.18 us
    all_to_all x1, waiting for transfers between devices, advect(): ring = lax.all_to_all(lines, 'xy', 0, 0, tiled=True)  5.62 us
    ppermute x1, waiting for transfers between devices, exchange_halo(): south = lax.ppermute(wide[:, -width:, :], 'rad', up)  5.54 us
    all_to_all x1, starting transfers between devices, advect(): ring = lax.all_to_all(lines, 'xy', 0, 0, tiled=True)  3.99 us
    ppermute x1, starting transfers between devices, exchange_halo(): behind = lax.ppermute(tail, AZI, fwd)  3.61 us
  transfers between devices with their start and end apart: 5, of which 4 were waited for; matrix products, arithmetic and copies ran while one was open for 1% of the time, Pallas kernels for 0%

profile of v11, /device:TPU:64, one launch (start us, length us, event | category | flops | bytes accessed | tf_op | source)
XLA Modules:
  0.0 89.7 jit_solution(9887488276667269273)
XLA Ops:
  0.0 0.8 slice_bitcast_fusion
  0.9 1.0 %slice.276 = f32[3,8,8,6]{3,2,1,0:T(8,128)S(1)} slice(f32[3,8,8,128]{3,2,1,0:T(8,128)} %param.4), slice={[0:3], [0:8], [0:8], [122:128]} | slice | bytes 9216 | tf_op jit(solution)/shard_map/slice | solution.py:89
  2.1 3.6 %collective-permute-start = (f32[25,8,6]{0,1,2:T(8,128)S(1)}, f32[25,8,6]{0,1,2:T(8,128)S(1)}, u32[]{:S(2)}, u32[]{:S(2)}) collective-permute-start(f32[25,8,6]{0,1,2:T(8,128)S(1)} %pad_maximum_fusion.5), channel_id=1, source_target_pairs={{0,1},{1,2},{2,3},{3,4},{4,5},{5,6},{6,7},{7,8},{8,9},{9,10},{10,1... | collective-permute-start | bytes 14408 | tf_op jit(solution)/shard_map/ppermute | solution.py:20
  6.1 17.2 %collective-permute-done = f32[25,8,6]{0,1,2:T(8,128)S(1)} collective-permute-done((f32[25,8,6]{0,1,2:T(8,128)S(1)}, f32[25,8,6]{0,1,2:T(8,128)S(1)}, u32[]{:S(2)}, u32[]{:S(2)}) %collective-permute-start) | collective-permute-done | bytes 4832 | tf_op jit(solution)/shard_map/ppermute | solution.py:20
  23.5 0.5 copy-done.1
  24.2 1.9 %collective-permute-start.2 = (f32[25,3,134]{2,1,0:T(4,128)S(1)}, f32[25,3,134]{2,1,0:T(4,128)S(1)}, u32[]{:S(2)}, u32[]{:S(2)}) collective-permute-start(f32[25,3,134]{2,1,0:T(4,128)S(1)} %get-tuple-element.49), channel_id=1, source_target_pairs={{64,0},{128,64},{192,128},{256,192},{320,256},{384,320},{448,384},... | collective-permute-start | bytes 120608 | tf_op jit(solution)/shard_map/ppermute | solution.py:23
  26.1 2.4 %collective-permute-start.1 = (f32[25,3,134]{2,1,0:T(4,128)S(1)}, f32[25,3,134]{2,1,0:T(4,128)S(1)}, u32[]{:S(2)}, u32[]{:S(2)}) collective-permute-start(f32[25,3,134]{2,1,0:T(4,128)S(1)} %get-tuple-element.48), channel_id=1, source_target_pairs={{0,64},{64,128},{128,192},{192,256},{256,320},{320,384},{384,448},... | collective-permute-start | bytes 120608 | tf_op jit(solution)/shard_map/ppermute | solution.py:22
  28.7 5.5 %collective-permute-done.1 = f32[25,3,134]{2,1,0:T(4,128)S(1)} collective-permute-done((f32[25,3,134]{2,1,0:T(4,128)S(1)}, f32[25,3,134]{2,1,0:T(4,128)S(1)}, u32[]{:S(2)}, u32[]{:S(2)}) %collective-permute-start.1) | collective-permute-done | bytes 40232 | tf_op jit(solution)/shard_map/ppermute | solution.py:22
  34.5 0.5 fusion.35
  35.0 0.2 fusion.37
  35.5 0.2 copy.76
  35.7 0.2 copy.73
  36.1 1.4 %subtract_multiply_fusion.1 = (f32[3,8,12,132]{3,0,2,1:T(4,128)S(1)}, f32[3,8,12,132]{3,0,2,1:T(4,128)S(1)}, f32[3,8,12,132]{3,0,2,1:T(4,128)S(1)}) fusion(f32[3,8,12,132]{3,2,1,0:T(8,128)S(1)} %get-tuple-element.35, f32[3,8,12,132]{3,2,1,0:T(8,128)S(1)} %get-tuple-element.36, f32[3,8,12,132]{3,2,1,0:T(8,128)S(1)} %get-tuple-element.32, ...), kind=kLoop, calls=%fused_computation.10 | loop fusion | flops 532224 | bytes 1526976 | tf_op jit(solution)/shard_map/mul | solution.py:36
  37.5 0.5 slice_subtract_fusion.2
  37.9 0.5 fusion.4
  38.5 0.4 fusion.33
  39.0 0.2 slice.362
  39.2 0.7 subtract_multiply_fusion.3
  40.0 0.6 fusion.22
  40.6 0.5 fusion.11
  41.1 0.2 fusion.39
  41.5 0.3 subtract_multiply_fusion.5
  41.9 0.3 fusion.30
  42.1 0.2 fusion.18
  42.4 0.7 reshape.69
  43.1 4.0 %all-to-all-start = ((f32[32,6,128]{2,1,0:T(8,128)}), f32[32,6,128]{2,1,0:T(8,128)S(1)}, u32[]{:S(2)}, u32[]{:S(2)}) async-start(f32[32,6,128]{2,1,0:T(8,128)} %reshape.69), calls=%async_computation | async-start | bytes 262144 | tf_op jit(solution)/shard_map/all_to_all | solution.py:50
  47.1 0.6 constant_dynamic-slice_fusion.1
  51.7 5.6 %all-to-all-done = f32[32,6,128]{2,1,0:T(8,128)S(1)} async-done(((f32[32,6,128]{2,1,0:T(8,128)}), f32[32,6,128]{2,1,0:T(8,128)S(1)}, u32[]{:S(2)}, u32[]{:S(2)}) %all-to-all-start) | async-done | bytes 98336 | tf_op jit(solution)/shard_map/all_to_all | solution.py:50
  57.3 7.2 %collective-permute-start.3 = (f32[32,6,128]{2,1,0:T(8,128)S(1)}, f32[32,6,128]{2,1,0:T(8,128)S(1)}, u32[]{:S(2)}, u32[]{:S(2)}) collective-permute-start(f32[32,6,128]{2,1,0:T(8,128)S(1)} %all-to-all-done), channel_id=1, source_target_pairs={{0,32},{32,0},{1,33},{33,1},{2,34},{34,2},{3,35},{35,3},{4,36},{36... | collective-permute-start | bytes 294920 | tf_op jit(solution)/shard_map/ppermute | solution.py:51
  64.6 7.9 %collective-permute-done.3 = f32[32,6,128]{2,1,0:T(8,128)S(1)} collective-permute-done((f32[32,6,128]{2,1,0:T(8,128)S(1)}, f32[32,6,128]{2,1,0:T(8,128)S(1)}, u32[]{:S(2)}, u32[]{:S(2)}) %collective-permute-start.3) | collective-permute-done | bytes 98336 | tf_op jit(solution)/shard_map/ppermute | solution.py:51
  73.5 15.5 %all_to_all.10 = f32[32,6,128]{2,1,0:T(8,128)S(1)} all-to-all(f32[32,6,128]{2,1,0:T(8,128)S(1)} %copy.63), channel_id=1, replica_groups=mesh['rad'=12,'zh'=2,'xy'=32] {'xy'}, dimensions={0} | all-to-all | bytes 196608 | tf_op jit(solution)/shard_map/all_to_all | solution.py:77
  89.1 0.6 copy.64
  (55 shorter events, 3.2 us)
Async XLA Ops:
  2.0 3.7 %copy-start.3 = (f32[96]{0:T(128)S(1)}, f32[96]{0:T(128)}, u32[]{:S(2)}) copy-start(f32[96]{0:T(128)} %param.6) | copy-start | bytes 1156
  2.1 21.4 %copy-start = (f32[3,8,8,128]{3,2,1,0:T(8,128)S(1)}, f32[3,8,8,128]{3,2,1,0:T(8,128)}, u32[]{:S(2)}) copy-start(f32[3,8,8,128]{3,2,1,0:T(8,128)} %param.4) | copy-start | bytes 294916
  2.1 21.3 %collective-permute-start = (f32[25,8,6]{0,1,2:T(8,128)S(1)}, f32[25,8,6]{0,1,2:T(8,128)S(1)}, u32[]{:S(2)}, u32[]{:S(2)}) collective-permute-start(f32[25,8,6]{0,1,2:T(8,128)S(1)} %pad_maximum_fusion.5), channel_id=1, source_target_pairs={{0,1},{1,2},{2,3},{3,4},{4,5},{5,6},{6,7},{7,8},{8,9},{9,10},{10,1... | collective-permute-start | bytes 14408 | tf_op jit(solution)/shard_map/ppermute | solution.py:20
  23.4 0.7 copy-start.1
  24.2 4.5 %collective-permute-start.2 = (f32[25,3,134]{2,1,0:T(4,128)S(1)}, f32[25,3,134]{2,1,0:T(4,128)S(1)}, u32[]{:S(2)}, u32[]{:S(2)}) collective-permute-start(f32[25,3,134]{2,1,0:T(4,128)S(1)} %get-tuple-element.49), channel_id=1, source_target_pairs={{64,0},{128,64},{192,128},{256,192},{320,256},{384,320},{448,384},... | collective-permute-start | bytes 120608 | tf_op jit(solution)/shard_map/ppermute | solution.py:23
  26.1 8.1 %collective-permute-start.1 = (f32[25,3,134]{2,1,0:T(4,128)S(1)}, f32[25,3,134]{2,1,0:T(4,128)S(1)}, u32[]{:S(2)}, u32[]{:S(2)}) collective-permute-start(f32[25,3,134]{2,1,0:T(4,128)S(1)} %get-tuple-element.48), channel_id=1, source_target_pairs={{0,64},{64,128},{128,192},{192,256},{256,320},{320,384},{384,448},... | collective-permute-start | bytes 120608 | tf_op jit(solution)/shard_map/ppermute | solution.py:22
  43.1 4.0 %copy-start.2 = (s32[1,96]{1,0:T(1,128)S(1)}, s32[1,96]{1,0:T(1,128)}, u32[]{:S(2)}) copy-start(s32[1,96]{1,0:T(1,128)} %param.7) | copy-start | bytes 1156
  43.1 14.3 %all-to-all-start = ((f32[32,6,128]{2,1,0:T(8,128)}), f32[32,6,128]{2,1,0:T(8,128)S(1)}, u32[]{:S(2)}, u32[]{:S(2)}) async-start(f32[32,6,128]{2,1,0:T(8,128)} %reshape.69), calls=%async_computation | async-start | bytes 262144 | tf_op jit(solution)/shard_map/all_to_all | solution.py:50
  57.3 15.1 %collective-permute-start.3 = (f32[32,6,128]{2,1,0:T(8,128)S(1)}, f32[32,6,128]{2,1,0:T(8,128)S(1)}, u32[]{:S(2)}, u32[]{:S(2)}) collective-permute-start(f32[32,6,128]{2,1,0:T(8,128)S(1)} %all-to-all-done), channel_id=1, source_target_pairs={{0,32},{32,0},{1,33},{33,1},{2,34},{34,2},{3,35},{35,3},{4,36},{36... | collective-permute-start | bytes 294920 | tf_op jit(solution)/shard_map/ppermute | solution.py:51

commit v12 on v11

--- a/solution.py
+++ b/solution.py
@@ -46,7 +46,8 @@
     n_lines = heights * radii
     n_half = lax.axis_size("xy")
     per = n_lines // n_half
-    lines = jnp.swapaxes(state.reshape(fields, n_lines, cells), 0, 1).reshape(n_half, per * fields, cells)
+    lines = jnp.swapaxes(state.reshape(fields, n_lines, cells), 0, 1).reshape(per, n_half, fields, cells)
+    lines = jnp.swapaxes(lines, 0, 1).reshape(n_half, per * fields, cells)
     ring = lax.all_to_all(lines, "xy", 0, 0, tiled=True)
     other = lax.ppermute(ring, "zh", [(0, 1), (1, 0)])
     upper = lax.axis_index("zh")
@@ -62,7 +63,7 @@
     mine = []
     for t in range(per):
         line = doubled[:, t]
-        shift = lax.dynamic_index_in_dim(shift_row, first_row + (me * per + t) % radii, keepdims=False)
+        shift = lax.dynamic_index_in_dim(shift_row, first_row + (t * n_half + me) % radii, keepdims=False)
         shift = shift % count
         whole = shift // per_chunk
         part = shift % per_chunk
@@ -74,7 +75,8 @@
             rolled = jnp.where(part == step, mixed, rolled)
         mine.append(lax.dynamic_slice_in_dim(rolled, upper * n_half, n_half, 0))
     out = jnp.stack(mine, axis=1).reshape(n_half, per * fields, cells)
-    back = lax.all_to_all(out, "xy", 0, 0, tiled=True).reshape(n_lines, fields, cells)
+    back = lax.all_to_all(out, "xy", 0, 0, tiled=True).reshape(n_half, per, fields, cells)
+    back = jnp.swapaxes(back, 0, 1).reshape(n_lines, fields, cells)
     return jnp.swapaxes(back, 0, 1).reshape(fields, heights, radii, cells)
 
 

time: 90.2 us -> 85 us (0.942)
  waiting for transfers between devices: 36.3 us -> 31.6 us
  starting transfers between devices: 19.1 us -> 22.1 us
  other arithmetic: 6.4 us -> 3.46 us
  local copies, waits for them, and re-layouts: 7.95 us -> 6.36 us
  blocking collectives: 15.5 us -> 16.8 us
    ppermute x1, waiting for transfers between devices: 5.54 us -> 0.23 us  [exchange_halo(): south = lax.ppermute(wide[:, -width:, :], 'rad', up)]
    ppermute x1, waiting for transfers between devices: 7.9 us -> 6.04 us  [advect(): other = lax.ppermute(ring, 'zh', [(0, 1), (1, 0)])]
    ppermute x1, waiting for transfers between devices: 0.01 us -> 1.83 us  [exchange_halo(): north = lax.ppermute(wide[:, :width, :], 'rad', down)]
    ppermute x1, starting transfers between devices: 7.18 us -> 8.91 us  [advect(): other = lax.ppermute(ring, 'zh', [(0, 1), (1, 0)])]
    ppermute x1, starting transfers between devices: 1.92 us -> 3.64 us  [exchange_halo(): north = lax.ppermute(wide[:, :width, :], 'rad', down)]
    mul x3, other arithmetic: 2.49 us -> 1.14 us  [rates(): radial_grad = 0.5 * (north - south)]
    all_to_all x1, blocking collectives: 15.5 us -> 16.8 us  [advect(): lax.all_to_all(out, 'xy', 0, 0, tiled=True)]
  transfers between devices with their start and end apart: 5 -> 5, of which waited for: 4 -> 5; matrix products, arithmetic and copies ran while one was open for 1% -> 1% of each run, Pallas kernels for 0% -> 0%
where the time goes in v12:
time: 85 us; the launch traced here: 84.5 us
  waiting for transfers between devices  31.6 us (37%)
  starting transfers between devices  22.1 us (26%)
  blocking collectives  16.8 us (20%)
  local copies, waits for them, and re-layouts  6.36 us (7%)
  between operations  4.32 us (5%)
  other arithmetic  3.46 us (4%)
    ppermute x1, waiting for transfers between devices, exchange_halo(): behind = lax.ppermute(tail, AZI, fwd)  17.2 us
    all_to_all x1, blocking collectives, advect(): lax.all_to_all(out, 'xy', 0, 0, tiled=True)  16.8 us
    ppermute x1, starting transfers between devices, advect(): other = lax.ppermute(ring, 'zh', [(0, 1), (1, 0)])  8.91 us
    all_to_all x1, waiting for transfers between devices, advect(): ring = lax.all_to_all(lines, 'xy', 0, 0, tiled=True)  6.22 us
    ppermute x1, waiting for transfers between devices, advect(): other = lax.ppermute(ring, 'zh', [(0, 1), (1, 0)])  6.04 us
    all_to_all x1, starting transfers between devices, advect(): ring = lax.all_to_all(lines, 'xy', 0, 0, tiled=True)  3.99 us
    ppermute x1, starting transfers between devices, exchange_halo(): north = lax.ppermute(wide[:, :width, :], 'rad', down)  3.64 us
    ppermute x1, starting transfers between devices, exchange_halo(): behind = lax.ppermute(tail, AZI, fwd)  3.61 us
  transfers between devices with their start and end apart: 5, of which 5 were waited for; matrix products, arithmetic and copies ran while one was open for 1% of the time, Pallas kernels for 0%

profile of v12, /device:TPU:64, one launch (start us, length us, event | category | flops | bytes accessed | tf_op | source)
XLA Modules:
  0.0 84.5 jit_solution(3962133746669423106)
XLA Ops:
  0.0 0.8 slice_bitcast_fusion
  0.8 0.1 copy.20
  0.9 1.0 %slice.276 = f32[3,8,8,6]{3,2,1,0:T(8,128)S(1)} slice(f32[3,8,8,128]{3,2,1,0:T(8,128)} %param.4), slice={[0:3], [0:8], [0:8], [122:128]} | slice | bytes 9216 | tf_op jit(solution)/shard_map/slice | solution.py:91
  1.9 0.1 copy.31
  2.1 3.6 %collective-permute-start = (f32[25,8,6]{0,1,2:T(8,128)S(1)}, f32[25,8,6]{0,1,2:T(8,128)S(1)}, u32[]{:S(2)}, u32[]{:S(2)}) collective-permute-start(f32[25,8,6]{0,1,2:T(8,128)S(1)} %pad_maximum_fusion.5), channel_id=1, source_target_pairs={{0,1},{1,2},{2,3},{3,4},{4,5},{5,6},{6,7},{7,8},{8,9},{9,10},{10,1... | collective-permute-start | bytes 14408 | tf_op jit(solution)/shard_map/ppermute | solution.py:20
  6.1 17.2 %collective-permute-done = f32[25,8,6]{0,1,2:T(8,128)S(1)} collective-permute-done((f32[25,8,6]{0,1,2:T(8,128)S(1)}, f32[25,8,6]{0,1,2:T(8,128)S(1)}, u32[]{:S(2)}, u32[]{:S(2)}) %collective-permute-start) | collective-permute-done | bytes 4832 | tf_op jit(solution)/shard_map/ppermute | solution.py:20
  23.4 0.2 copy.21
  23.5 0.5 copy-done.1
  24.2 1.9 %collective-permute-start.1 = (f32[25,3,134]{2,1,0:T(4,128)S(1)}, f32[25,3,134]{2,1,0:T(4,128)S(1)}, u32[]{:S(2)}, u32[]{:S(2)}) collective-permute-start(f32[25,3,134]{2,1,0:T(4,128)S(1)} %get-tuple-element.41), channel_id=1, source_target_pairs={{0,64},{64,128},{128,192},{192,256},{256,320},{320,384},{384,448},... | collective-permute-start | bytes 120608 | tf_op jit(solution)/shard_map/ppermute | solution.py:22
  26.1 3.6 %collective-permute-start.2 = (f32[25,3,134]{2,1,0:T(4,128)S(1)}, f32[25,3,134]{2,1,0:T(4,128)S(1)}, u32[]{:S(2)}, u32[]{:S(2)}) collective-permute-start(f32[25,3,134]{2,1,0:T(4,128)S(1)} %get-tuple-element.42), channel_id=1, source_target_pairs={{64,0},{128,64},{192,128},{256,192},{320,256},{384,320},{448,384},... | collective-permute-start | bytes 120608 | tf_op jit(solution)/shard_map/ppermute | solution.py:23
  30.0 0.2 collective-permute-done.1
  30.2 1.8 %collective-permute-done.2 = f32[25,3,134]{2,1,0:T(4,128)S(1)} collective-permute-done((f32[25,3,134]{2,1,0:T(4,128)S(1)}, f32[25,3,134]{2,1,0:T(4,128)S(1)}, u32[]{:S(2)}, u32[]{:S(2)}) %collective-permute-start.2) | collective-permute-done | bytes 40232 | tf_op jit(solution)/shard_map/ppermute | solution.py:23
  32.3 0.2 pad_maximum_fusion
  32.6 0.2 fusion.37
  32.9 0.5 subtract_multiply_fusion.3
  33.4 0.2 slice_subtract_fusion.6
  33.5 0.2 fusion.6
  33.8 0.2 fusion.35
  34.1 0.5 subtract_multiply_fusion.1
  34.5 0.2 slice_subtract_fusion.2
  34.7 0.3 fusion.1
  35.2 0.2 subtract_multiply_fusion.5
  35.6 0.7 copy.23
  36.4 4.0 %all-to-all-start = ((f32[32,6,128]{2,1,0:T(8,128)}), f32[32,6,128]{2,1,0:T(8,128)S(1)}, u32[]{:S(2)}, u32[]{:S(2)}) async-start(f32[32,6,128]{2,1,0:T(8,128)} %copy.23), calls=%async_computation | async-start | bytes 262144 | tf_op jit(solution)/shard_map/all_to_all | solution.py:51
  40.4 0.6 constant_dynamic-slice_fusion.1
  45.0 6.2 %all-to-all-done = f32[32,6,128]{2,1,0:T(8,128)S(1)} async-done(((f32[32,6,128]{2,1,0:T(8,128)}), f32[32,6,128]{2,1,0:T(8,128)S(1)}, u32[]{:S(2)}, u32[]{:S(2)}) %all-to-all-start) | async-done | bytes 98336 | tf_op jit(solution)/shard_map/all_to_all | solution.py:51
  51.2 8.9 %collective-permute-start.3 = (f32[32,6,128]{2,0,1:T(8,128)S(1)}, f32[32,6,128]{2,0,1:T(8,128)S(1)}, u32[]{:S(2)}, u32[]{:S(2)}) collective-permute-start(f32[32,6,128]{2,0,1:T(8,128)S(1)} %copy.24), channel_id=1, source_target_pairs={{0,32},{32,0},{1,33},{33,1},{2,34},{34,2},{3,35},{35,3},{4,36},{36... | collective-permute-start | bytes 294920 | tf_op jit(solution)/shard_map/ppermute | solution.py:52
  60.1 6.0 %collective-permute-done.3 = f32[32,6,128]{2,0,1:T(8,128)S(1)} collective-permute-done((f32[32,6,128]{2,0,1:T(8,128)S(1)}, f32[32,6,128]{2,0,1:T(8,128)S(1)}, u32[]{:S(2)}, u32[]{:S(2)}) %collective-permute-start.3) | collective-permute-done | bytes 98336 | tf_op jit(solution)/shard_map/ppermute | solution.py:52
  66.2 0.2 fusion.12
  66.4 0.2 maximum_maximum_fusion
  67.1 16.8 %all_to_all.10 = f32[32,6,128]{2,1,0:T(8,128)S(1)} all-to-all(f32[32,6,128]{2,1,0:T(8,128)S(1)} %copy.28), channel_id=1, replica_groups=mesh['rad'=12,'zh'=2,'xy'=32] {'xy'}, dimensions={0} | all-to-all | bytes 196608 | tf_op jit(solution)/shard_map/all_to_all | solution.py:78
  83.9 0.6 copy.30
  (45 shorter events, 2.2 us)
Async XLA Ops:
  2.0 3.7 %copy-start.3 = (f32[96]{0:T(128)S(1)}, f32[96]{0:T(128)}, u32[]{:S(2)}) copy-start(f32[96]{0:T(128)} %param.6) | copy-start | bytes 1156
  2.1 21.4 %copy-start = (f32[3,8,8,128]{3,2,1,0:T(8,128)S(1)}, f32[3,8,8,128]{3,2,1,0:T(8,128)}, u32[]{:S(2)}) copy-start(f32[3,8,8,128]{3,2,1,0:T(8,128)} %param.4) | copy-start | bytes 294916
  2.1 21.3 %collective-permute-start = (f32[25,8,6]{0,1,2:T(8,128)S(1)}, f32[25,8,6]{0,1,2:T(8,128)S(1)}, u32[]{:S(2)}, u32[]{:S(2)}) collective-permute-start(f32[25,8,6]{0,1,2:T(8,128)S(1)} %pad_maximum_fusion.5), channel_id=1, source_target_pairs={{0,1},{1,2},{2,3},{3,4},{4,5},{5,6},{6,7},{7,8},{8,9},{9,10},{10,1... | collective-permute-start | bytes 14408 | tf_op jit(solution)/shard_map/ppermute | solution.py:20
  23.4 0.7 copy-start.1
  24.2 6.0 %collective-permute-start.1 = (f32[25,3,134]{2,1,0:T(4,128)S(1)}, f32[25,3,134]{2,1,0:T(4,128)S(1)}, u32[]{:S(2)}, u32[]{:S(2)}) collective-permute-start(f32[25,3,134]{2,1,0:T(4,128)S(1)} %get-tuple-element.41), channel_id=1, source_target_pairs={{0,64},{64,128},{128,192},{192,256},{256,320},{320,384},{384,448},... | collective-permute-start | bytes 120608 | tf_op jit(solution)/shard_map/ppermute | solution.py:22
  26.1 5.9 %collective-permute-start.2 = (f32[25,3,134]{2,1,0:T(4,128)S(1)}, f32[25,3,134]{2,1,0:T(4,128)S(1)}, u32[]{:S(2)}, u32[]{:S(2)}) collective-permute-start(f32[25,3,134]{2,1,0:T(4,128)S(1)} %get-tuple-element.42), channel_id=1, source_target_pairs={{64,0},{128,64},{192,128},{256,192},{320,256},{384,320},{448,384},... | collective-permute-start | bytes 120608 | tf_op jit(solution)/shard_map/ppermute | solution.py:23
  36.4 4.0 %copy-start.2 = (s32[1,96]{1,0:T(1,128)S(1)}, s32[1,96]{1,0:T(1,128)}, u32[]{:S(2)}) copy-start(s32[1,96]{1,0:T(1,128)} %param.7) | copy-start | bytes 1156
  36.4 14.8 %all-to-all-start = ((f32[32,6,128]{2,1,0:T(8,128)}), f32[32,6,128]{2,1,0:T(8,128)S(1)}, u32[]{:S(2)}, u32[]{:S(2)}) async-start(f32[32,6,128]{2,1,0:T(8,128)} %copy.23), calls=%async_computation | async-start | bytes 262144 | tf_op jit(solution)/shard_map/all_to_all | solution.py:51
  51.2 15.0 %collective-permute-start.3 = (f32[32,6,128]{2,0,1:T(8,128)S(1)}, f32[32,6,128]{2,0,1:T(8,128)S(1)}, u32[]{:S(2)}, u32[]{:S(2)}) collective-permute-start(f32[32,6,128]{2,0,1:T(8,128)S(1)} %copy.24), channel_id=1, source_target_pairs={{0,32},{32,0},{1,33},{33,1},{2,34},{34,2},{3,35},{35,3},{4,36},{36... | collective-permute-start | bytes 294920 | tf_op jit(solution)/shard_map/ppermute | solution.py:52

commit v13 on v12

--- a/solution.py
+++ b/solution.py
@@ -87,9 +87,7 @@
     first_row = band * radii
     total_rows = rotation.shape[0]
     packed = jnp.concatenate([fields.reshape(n_f * heights, radii, cells), viscosity[None]], axis=0)
-    tail = jnp.concatenate(
-        [fields[..., cells - 2 * w :].reshape(n_f * heights, radii, 2 * w), viscosity[None, :, cells - 2 * w :]], axis=0
-    )
+    tail = jnp.concatenate([fields.reshape(n_f * heights, radii, cells), viscosity[None]], axis=0)[..., cells - 2 * w :]
     ext = exchange_halo(packed, tail, w)
     u0 = ext[: n_f * heights].reshape(n_f, heights, radii + 2 * w, cells + 2 * w)
     visc = ext[n_f * heights]

time: 85 us -> 85.2 us (level)
  the two profiles are of different devices: /device:TPU:64 before, /device:TPU:1 now
where the time goes in v13:
time: 85.2 us; the launch traced here: 84.8 us
  waiting for transfers between devices  31.9 us (37%)
  starting transfers between devices  25.1 us (29%)
  blocking collectives  14.7 us (17%)
  other arithmetic  4.42 us (5%)
  between operations  4.32 us (5%)
  local copies, waits for them, and re-layouts  4.31 us (5%)
    ppermute x1, waiting for transfers between devices, exchange_halo(): behind = lax.ppermute(tail, AZI, fwd)  17.9 us
    all_to_all x1, blocking collectives, advect(): lax.all_to_all(out, 'xy', 0, 0, tiled=True)  14.7 us
    ppermute x1, starting transfers between devices, exchange_halo(): south = lax.ppermute(wide[:, -width:, :], 'rad', up)  8.96 us
    ppermute x1, starting transfers between devices, advect(): other = lax.ppermute(ring, 'zh', [(0, 1), (1, 0)])  6.23 us
    ppermute x1, waiting for transfers between devices, advect(): other = lax.ppermute(ring, 'zh', [(0, 1), (1, 0)])  5.45 us
    all_to_all x1, waiting for transfers between devices, advect(): ring = lax.all_to_all(lines, 'xy', 0, 0, tiled=True)  4.61 us
    ppermute x1, starting transfers between devices, exchange_halo(): behind = lax.ppermute(tail, AZI, fwd)  4.03 us
    all_to_all x1, starting transfers between devices, advect(): ring = lax.all_to_all(lines, 'xy', 0, 0, tiled=True)  3.99 us
  transfers between devices with their start and end apart: 5, of which 4 were waited for; matrix products, arithmetic and copies ran while one was open for 1% of the time, Pallas kernels for 0%

profile of v13, /device:TPU:1, one launch (start us, length us, event | category | flops | bytes accessed | tf_op | source)
XLA Modules:
  0.0 84.8 jit_solution(7609621625001384551)
XLA Ops:
  0.0 1.0 %pad_maximum_fusion.4 = f32[25,8,6]{2,1,0:T(8,128)S(1)} fusion(f32[1,8,128]{2,1,0:T(8,128)} %bitcast.60, f32[24,8,128]{2,1,0:T(8,128)} %bitcast.49), kind=kLoop, calls=%fused_computation.45 | loop fusion | flops 1200 | bytes 107200 | tf_op jit(solution)/shard_map/concatenate | solution.py:90
  1.1 4.0 %collective-permute-start = (f32[25,8,6]{2,1,0:T(8,128)S(1)}, f32[25,8,6]{2,1,0:T(8,128)S(1)}, u32[]{:S(2)}, u32[]{:S(2)}) collective-permute-start(f32[25,8,6]{2,1,0:T(8,128)S(1)} %pad_maximum_fusion.4), channel_id=1, source_target_pairs={{0,1},{1,2},{2,3},{3,4},{4,5},{5,6},{6,7},{7,8},{8,9},{9,10},{10,1... | collective-permute-start | bytes 14408 | tf_op jit(solution)/shard_map/ppermute | solution.py:20
  5.1 0.6 copy-done.3
  6.1 17.9 %collective-permute-done = f32[25,8,6]{2,1,0:T(8,128)S(1)} collective-permute-done((f32[25,8,6]{2,1,0:T(8,128)S(1)}, f32[25,8,6]{2,1,0:T(8,128)S(1)}, u32[]{:S(2)}, u32[]{:S(2)}) %collective-permute-start) | collective-permute-done | bytes 4832 | tf_op jit(solution)/shard_map/ppermute | solution.py:20
  24.1 0.1 maximum_maximum_fusion.1
  24.3 9.0 %collective-permute-start.1 = (f32[25,3,134]{2,1,0:T(4,128)S(1)}, f32[25,3,134]{2,1,0:T(4,128)S(1)}, u32[]{:S(2)}, u32[]{:S(2)}) collective-permute-start(f32[25,3,134]{2,1,0:T(4,128)S(1)} %get-tuple-element.41), channel_id=1, source_target_pairs={{0,64},{64,128},{128,192},{192,256},{256,320},{320,384},{384,448},... | collective-permute-start | bytes 120608 | tf_op jit(solution)/shard_map/ppermute | solution.py:22
  33.2 1.9 %collective-permute-start.2 = (f32[25,3,134]{2,1,0:T(4,128)S(1)}, f32[25,3,134]{2,1,0:T(4,128)S(1)}, u32[]{:S(2)}, u32[]{:S(2)}) collective-permute-start(f32[25,3,134]{2,1,0:T(4,128)S(1)} %get-tuple-element.42), channel_id=1, source_target_pairs={{64,0},{128,64},{192,128},{256,192},{320,256},{384,320},{448,384},... | collective-permute-start | bytes 120608 | tf_op jit(solution)/shard_map/ppermute | solution.py:23
  35.3 3.9 %collective-permute-done.2 = f32[25,3,134]{2,1,0:T(4,128)S(1)} collective-permute-done((f32[25,3,134]{2,1,0:T(4,128)S(1)}, f32[25,3,134]{2,1,0:T(4,128)S(1)}, u32[]{:S(2)}, u32[]{:S(2)}) %collective-permute-start.2) | collective-permute-done | bytes 40232 | tf_op jit(solution)/shard_map/ppermute | solution.py:23
  39.5 0.2 pad_maximum_fusion
  39.8 0.2 fusion.37
  40.1 0.5 subtract_multiply_fusion.3
  40.6 0.2 slice_subtract_fusion.6
  40.7 0.2 fusion.6
  41.0 0.2 fusion.35
  41.2 0.5 subtract_multiply_fusion.1
  41.7 0.2 slice_subtract_fusion.2
  41.9 0.3 fusion.1
  42.3 0.1 fusion.33
  42.4 0.2 subtract_multiply_fusion.5
  42.6 0.1 fusion.30
  42.7 0.1 fusion.17
  42.8 0.7 copy.8
  43.5 4.0 %all-to-all-start = ((f32[32,6,128]{2,1,0:T(8,128)}), f32[32,6,128]{2,1,0:T(8,128)S(1)}, u32[]{:S(2)}, u32[]{:S(2)}) async-start(f32[32,6,128]{2,1,0:T(8,128)} %copy.8), calls=%async_computation | async-start | bytes 262144 | tf_op jit(solution)/shard_map/all_to_all | solution.py:51
  47.6 0.6 constant_dynamic-slice_fusion.1
  52.1 4.6 %all-to-all-done = f32[32,6,128]{2,1,0:T(8,128)S(1)} async-done(((f32[32,6,128]{2,1,0:T(8,128)}), f32[32,6,128]{2,1,0:T(8,128)S(1)}, u32[]{:S(2)}, u32[]{:S(2)}) %all-to-all-start) | async-done | bytes 98336 | tf_op jit(solution)/shard_map/all_to_all | solution.py:51
  56.8 6.2 %collective-permute-start.3 = (f32[32,6,128]{2,0,1:T(8,128)S(1)}, f32[32,6,128]{2,0,1:T(8,128)S(1)}, u32[]{:S(2)}, u32[]{:S(2)}) collective-permute-start(f32[32,6,128]{2,0,1:T(8,128)S(1)} %copy.9), channel_id=1, source_target_pairs={{0,32},{32,0},{1,33},{33,1},{2,34},{34,2},{3,35},{35,3},{4,36},{36... | collective-permute-start | bytes 294920 | tf_op jit(solution)/shard_map/ppermute | solution.py:52
  63.0 5.5 %collective-permute-done.3 = f32[32,6,128]{2,0,1:T(8,128)S(1)} collective-permute-done((f32[32,6,128]{2,0,1:T(8,128)S(1)}, f32[32,6,128]{2,0,1:T(8,128)S(1)}, u32[]{:S(2)}, u32[]{:S(2)}) %collective-permute-start.3) | collective-permute-done | bytes 98336 | tf_op jit(solution)/shard_map/ppermute | solution.py:52
  68.5 0.2 fusion.12
  68.7 0.2 maximum_maximum_fusion
  69.2 0.1 fusion.25
  69.4 14.7 %all_to_all.10 = f32[32,6,128]{2,1,0:T(8,128)S(1)} all-to-all(f32[32,6,128]{2,1,0:T(8,128)S(1)} %copy.13), channel_id=1, replica_groups=mesh['rad'=12,'zh'=2,'xy'=32] {'xy'}, dimensions={0} | all-to-all | bytes 196608 | tf_op jit(solution)/shard_map/all_to_all | solution.py:78
  84.1 0.6 copy.15
  (40 shorter events, 1.6 us)
Async XLA Ops:
  0.0 24.1 %copy-start = (f32[3,8,8,128]{3,2,1,0:T(8,128)S(1)}, f32[3,8,8,128]{3,2,1,0:T(8,128)}, u32[]{:S(2)}) copy-start(f32[3,8,8,128]{3,2,1,0:T(8,128)} %param.4) | copy-start | bytes 294916
  1.1 23.0 %collective-permute-start = (f32[25,8,6]{2,1,0:T(8,128)S(1)}, f32[25,8,6]{2,1,0:T(8,128)S(1)}, u32[]{:S(2)}, u32[]{:S(2)}) collective-permute-start(f32[25,8,6]{2,1,0:T(8,128)S(1)} %pad_maximum_fusion.4), channel_id=1, source_target_pairs={{0,1},{1,2},{2,3},{3,4},{4,5},{5,6},{6,7},{7,8},{8,9},{9,10},{10,1... | collective-permute-start | bytes 14408 | tf_op jit(solution)/shard_map/ppermute | solution.py:20
  5.1 0.7 copy-start.3
  5.9 18.2 %copy-start.1 = (f32[8,128]{1,0:T(8,128)S(1)}, f32[8,128]{1,0:T(8,128)}, u32[]{:S(2)}) copy-start(f32[8,128]{1,0:T(8,128)} %param.5) | copy-start | bytes 12292
  24.3 11.1 %collective-permute-start.1 = (f32[25,3,134]{2,1,0:T(4,128)S(1)}, f32[25,3,134]{2,1,0:T(4,128)S(1)}, u32[]{:S(2)}, u32[]{:S(2)}) collective-permute-start(f32[25,3,134]{2,1,0:T(4,128)S(1)} %get-tuple-element.41), channel_id=1, source_target_pairs={{0,64},{64,128},{128,192},{192,256},{256,320},{320,384},{384,448},... | collective-permute-start | bytes 120608 | tf_op jit(solution)/shard_map/ppermute | solution.py:22
  33.2 6.0 %collective-permute-start.2 = (f32[25,3,134]{2,1,0:T(4,128)S(1)}, f32[25,3,134]{2,1,0:T(4,128)S(1)}, u32[]{:S(2)}, u32[]{:S(2)}) collective-permute-start(f32[25,3,134]{2,1,0:T(4,128)S(1)} %get-tuple-element.42), channel_id=1, source_target_pairs={{64,0},{128,64},{192,128},{256,192},{320,256},{384,320},{448,384},... | collective-permute-start | bytes 120608 | tf_op jit(solution)/shard_map/ppermute | solution.py:23
  43.5 4.0 %copy-start.2 = (s32[1,96]{1,0:T(1,128)S(1)}, s32[1,96]{1,0:T(1,128)}, u32[]{:S(2)}) copy-start(s32[1,96]{1,0:T(1,128)} %param.7) | copy-start | bytes 1156
  43.5 13.2 %all-to-all-start = ((f32[32,6,128]{2,1,0:T(8,128)}), f32[32,6,128]{2,1,0:T(8,128)S(1)}, u32[]{:S(2)}, u32[]{:S(2)}) async-start(f32[32,6,128]{2,1,0:T(8,128)} %copy.8), calls=%async_computation | async-start | bytes 262144 | tf_op jit(solution)/shard_map/all_to_all | solution.py:51
  56.8 11.7 %collective-permute-start.3 = (f32[32,6,128]{2,0,1:T(8,128)S(1)}, f32[32,6,128]{2,0,1:T(8,128)S(1)}, u32[]{:S(2)}, u32[]{:S(2)}) collective-permute-start(f32[32,6,128]{2,0,1:T(8,128)S(1)} %copy.9), channel_id=1, source_target_pairs={{0,32},{32,0},{1,33},{33,1},{2,34},{34,2},{3,35},{35,3},{4,36},{36... | collective-permute-start | bytes 294920 | tf_op jit(solution)/shard_map/ppermute | solution.py:52

commit v14 on v12

--- a/solution.py
+++ b/solution.py
@@ -5,7 +5,9 @@
 
 BLOCK = 64
 HALO = 3
-AZI = ("zh", "xy")
+OUTER = ("zh", "xh")
+INNER = ("xl", "y")
+AZI = OUTER + INNER
 
 
 time_step = 0.3
@@ -44,18 +46,21 @@
 def advect(state, shift_row, first_row, lag):
     fields, heights, radii, cells = state.shape
     n_lines = heights * radii
-    n_half = lax.axis_size("xy")
-    per = n_lines // n_half
-    lines = jnp.swapaxes(state.reshape(fields, n_lines, cells), 0, 1).reshape(per, n_half, fields, cells)
-    lines = jnp.swapaxes(lines, 0, 1).reshape(n_half, per * fields, cells)
-    ring = lax.all_to_all(lines, "xy", 0, 0, tiled=True)
-    other = lax.ppermute(ring, "zh", [(0, 1), (1, 0)])
-    upper = lax.axis_index("zh")
-    ring = jnp.where(upper == 0, jnp.concatenate([ring, other], axis=0), jnp.concatenate([other, ring], axis=0))
+    n_grp = lax.axis_size(INNER)
+    per = n_lines // n_grp
+    lines = jnp.swapaxes(state.reshape(fields, n_lines, cells), 0, 1).reshape(per, n_grp, fields, cells)
+    lines = jnp.swapaxes(lines, 0, 1).reshape(n_grp, per * fields, cells)
+    ring = lax.all_to_all(lines, INNER, 0, 0, tiled=True)
+    start = 0
+    for axis in OUTER[::-1]:
+        other = lax.ppermute(ring, axis, [(0, 1), (1, 0)])
+        side = lax.axis_index(axis)
+        start = start + side * ring.shape[0]
+        ring = jnp.where(side == 0, jnp.concatenate([ring, other], axis=0), jnp.concatenate([other, ring], axis=0))
     chunks = ring.shape[0]
     ring = ring.reshape(chunks, per, fields, cells)
     ring = jnp.concatenate([ring[..., lag:], jnp.roll(ring, -1, axis=0)[..., :lag]], axis=-1)
-    me = lax.axis_index("xy")
+    me = lax.axis_index(INNER)
     per_chunk = cells // BLOCK
     count = chunks * per_chunk
     doubled = jnp.concatenate([ring, ring], axis=0)
@@ -63,7 +68,7 @@
     mine = []
     for t in range(per):
         line = doubled[:, t]
-        shift = lax.dynamic_index_in_dim(shift_row, first_row + (t * n_half + me) % radii, keepdims=False)
+        shift = lax.dynamic_index_in_dim(shift_row, first_row + (t * n_grp + me) % radii, keepdims=False)
         shift = shift % count
         whole = shift // per_chunk
         part = shift % per_chunk
@@ -73,9 +78,9 @@
         for step in range(1, per_chunk):
             mixed = jnp.roll(jnp.where(lane < cells - step * BLOCK, base, earlier), step * BLOCK, axis=2)
             rolled = jnp.where(part == step, mixed, rolled)
-        mine.append(lax.dynamic_slice_in_dim(rolled, upper * n_half, n_half, 0))
-    out = jnp.stack(mine, axis=1).reshape(n_half, per * fields, cells)
-    back = lax.all_to_all(out, "xy", 0, 0, tiled=True).reshape(n_half, per, fields, cells)
+        mine.append(lax.dynamic_slice_in_dim(rolled, start, n_grp, 0))
+    out = jnp.stack(mine, axis=1).reshape(n_grp, per * fields, cells)
+    back = lax.all_to_all(out, INNER, 0, 0, tiled=True).reshape(n_grp, per, fields, cells)
     back = jnp.swapaxes(back, 0, 1).reshape(n_lines, fields, cells)
     return jnp.swapaxes(back, 0, 1).reshape(fields, heights, radii, cells)
 
@@ -118,10 +123,10 @@
 
 def solution(mesh):
     n_r, n_a = mesh.devices.shape
-    halves = Mesh(mesh.devices.reshape(n_r, 2, n_a // 2), ("rad",) + AZI)
+    quarters = Mesh(mesh.devices.reshape(n_r, 2, 2, 2, n_a // 8), ("rad",) + AZI)
     return jax.shard_map(
         body,
-        mesh=halves,
+        mesh=quarters,
         in_specs=(P(None, None, "rad", AZI), P("rad", AZI), P(), P()),
         out_specs=P(None, None, "rad", AZI),
         check_vma=False,

time: 85 us -> 96.3 us (1.13)
  the two profiles are of different devices: /device:TPU:64 before, /device:TPU:68 now
where the time goes in v14:
time: 96.3 us; the launch traced here: 95.8 us
  blocking collectives  33.8 us (35%)
  starting transfers between devices  24.3 us (25%)
  waiting for transfers between devices  19.7 us (20%)
  between operations  8.12 us (8%)
  local copies, waits for them, and re-layouts  5.95 us (6%)
  other arithmetic  3.87 us (4%)
    all_to_all x1, blocking collectives, advect(): ring = lax.all_to_all(lines, INNER, 0, 0, tiled=True)  21.2 us
    ppermute x2, starting transfers between devices, advect(): other = lax.ppermute(ring, axis, [(0, 1), (1, 0)])  15.1 us
    ppermute x2, waiting for transfers between devices, advect(): other = lax.ppermute(ring, axis, [(0, 1), (1, 0)])  13.8 us
    all_to_all x1, blocking collectives, advect(): lax.all_to_all(out, INNER, 0, 0, tiled=True)  12.6 us
    ppermute x1, waiting for transfers between devices, exchange_halo(): behind = lax.ppermute(tail, AZI, fwd)  3.93 us
    ppermute x1, starting transfers between devices, exchange_halo(): north = lax.ppermute(wide[:, :width, :], 'rad', down)  3.64 us
    ppermute x1, starting transfers between devices, exchange_halo(): behind = lax.ppermute(tail, AZI, fwd)  3.61 us
  transfers between devices with their start and end apart: 5, of which 4 were waited for; matrix products, arithmetic and copies ran while one was open for 1% of the time, Pallas kernels for 0%

profile of v14, /device:TPU:68, one launch (start us, length us, event | category | flops | bytes accessed | tf_op | source)
XLA Modules:
  0.0 95.8 jit_solution(3093369784175267673)
XLA Ops:
  0.0 0.8 slice_bitcast_fusion
  0.8 0.1 copy.20
  0.9 1.0 %slice.294 = f32[3,8,8,6]{3,2,1,0:T(8,128)S(1)} slice(f32[3,8,8,128]{3,2,1,0:T(8,128)} %param.4), slice={[0:3], [0:8], [0:8], [122:128]} | slice | bytes 9216 | tf_op jit(solution)/shard_map/slice | solution.py:96
  1.9 0.1 copy.31
  2.1 3.6 %collective-permute-start = (f32[25,8,6]{0,1,2:T(8,128)S(1)}, f32[25,8,6]{0,1,2:T(8,128)S(1)}, u32[]{:S(2)}, u32[]{:S(2)}) collective-permute-start(f32[25,8,6]{0,1,2:T(8,128)S(1)} %pad_maximum_fusion.5), channel_id=1, source_target_pairs={{0,1},{1,2},{2,3},{3,4},{4,5},{5,6},{6,7},{7,8},{8,9},{9,10},{10,1... | collective-permute-start | bytes 14408 | tf_op jit(solution)/shard_map/ppermute | solution.py:22
  6.1 3.9 %collective-permute-done = f32[25,8,6]{0,1,2:T(8,128)S(1)} collective-permute-done((f32[25,8,6]{0,1,2:T(8,128)S(1)}, f32[25,8,6]{0,1,2:T(8,128)S(1)}, u32[]{:S(2)}, u32[]{:S(2)}) %collective-permute-start) | collective-permute-done | bytes 4832 | tf_op jit(solution)/shard_map/ppermute | solution.py:22
  10.1 0.2 copy.21
  10.2 0.5 copy-done.1
  10.9 1.9 %collective-permute-start.1 = (f32[25,3,134]{2,1,0:T(4,128)S(1)}, f32[25,3,134]{2,1,0:T(4,128)S(1)}, u32[]{:S(2)}, u32[]{:S(2)}) collective-permute-start(f32[25,3,134]{2,1,0:T(4,128)S(1)} %get-tuple-element.47), channel_id=1, source_target_pairs={{0,64},{64,128},{128,192},{192,256},{256,320},{320,384},{384,448},... | collective-permute-start | bytes 120608 | tf_op jit(solution)/shard_map/ppermute | solution.py:24
  12.8 3.6 %collective-permute-start.2 = (f32[25,3,134]{2,1,0:T(4,128)S(1)}, f32[25,3,134]{2,1,0:T(4,128)S(1)}, u32[]{:S(2)}, u32[]{:S(2)}) collective-permute-start(f32[25,3,134]{2,1,0:T(4,128)S(1)} %get-tuple-element.48), channel_id=1, source_target_pairs={{64,0},{128,64},{192,128},{256,192},{320,256},{384,320},{448,384},... | collective-permute-start | bytes 120608 | tf_op jit(solution)/shard_map/ppermute | solution.py:25
  16.6 0.2 collective-permute-done.1
  16.9 1.8 %collective-permute-done.2 = f32[25,3,134]{2,1,0:T(4,128)S(1)} collective-permute-done((f32[25,3,134]{2,1,0:T(4,128)S(1)}, f32[25,3,134]{2,1,0:T(4,128)S(1)}, u32[]{:S(2)}, u32[]{:S(2)}) %collective-permute-start.2) | collective-permute-done | bytes 40232 | tf_op jit(solution)/shard_map/ppermute | solution.py:25
  19.0 0.2 pad_maximum_fusion
  19.3 0.2 fusion.43
  19.6 0.5 subtract_multiply_fusion.3
  20.1 0.2 slice_subtract_fusion.6
  20.2 0.2 fusion.7
  20.5 0.2 fusion.41
  20.7 0.5 subtract_multiply_fusion.1
  21.2 0.2 slice_subtract_fusion.2
  21.4 0.3 fusion.2
  21.9 0.2 subtract_multiply_fusion.5
  22.2 0.1 fusion.17
  22.4 21.2 %all_to_all.10 = f32[16,12,128]{2,1,0:T(8,128)S(1)} all-to-all(f32[16,12,128]{2,1,0:T(8,128)S(1)} %copy.23), channel_id=1, replica_groups=mesh['rad'=12,'zh'=2,'xh'=2,'xl'=2,'y'=8] {'xl','y'}, dimensions={0} | all-to-all | bytes 196608 | tf_op jit(solution)/shard_map/all_to_all | solution.py:53
  43.6 5.8 %collective-permute-start.3 = (f32[16,12,128]{2,0,1:T(8,128)S(1)}, f32[16,12,128]{2,0,1:T(8,128)S(1)}, u32[]{:S(2)}, u32[]{:S(2)}) collective-permute-start(f32[16,12,128]{2,0,1:T(8,128)S(1)} %copy.24), channel_id=1, source_target_pairs={{0,16},{16,0},{1,17},{17,1},{2,18},{18,2},{3,19},{19,3},{4,20},{20... | collective-permute-start | bytes 294920 | tf_op jit(solution)/shard_map/ppermute | solution.py:56
  49.5 0.7 constant_dynamic-slice_fusion.3
  57.9 9.3 %collective-permute-start.4 = (f32[32,12,128]{2,0,1:T(8,128)S(1)}, f32[32,12,128]{2,0,1:T(8,128)S(1)}, u32[]{:S(2)}, u32[]{:S(2)}) collective-permute-start(f32[32,12,128]{2,0,1:T(8,128)S(1)} %maximum_select_fusion.2), channel_id=1, source_target_pairs={{0,32},{32,0},{1,33},{33,1},{2,34},{34,2},{3,35},{35,3},{4,36},{36... | collective-permute-start | bytes 589832 | tf_op jit(solution)/shard_map/ppermute | solution.py:56
  67.2 13.8 %collective-permute-done.4 = f32[32,12,128]{2,0,1:T(8,128)S(1)} collective-permute-done((f32[32,12,128]{2,0,1:T(8,128)S(1)}, f32[32,12,128]{2,0,1:T(8,128)S(1)}, u32[]{:S(2)}, u32[]{:S(2)}) %collective-permute-start.4) | collective-permute-done | bytes 196640 | tf_op jit(solution)/shard_map/ppermute | solution.py:56
  81.1 0.3 fusion
  81.4 0.3 maximum_maximum_fusion
  82.5 12.6 %all_to_all.11 = f32[16,12,128]{2,1,0:T(8,128)S(1)} all-to-all(f32[16,12,128]{2,1,0:T(8,128)S(1)} %copy.28), channel_id=1, replica_groups=mesh['rad'=12,'zh'=2,'xh'=2,'xl'=2,'y'=8] {'xl','y'}, dimensions={0} | all-to-all | bytes 196608 | tf_op jit(solution)/shard_map/all_to_all | solution.py:83
  95.1 0.6 copy.30
  (51 shorter events, 2.6 us)
Async XLA Ops:
  2.0 3.7 %copy-start.3 = (f32[96]{0:T(128)S(1)}, f32[96]{0:T(128)}, u32[]{:S(2)}) copy-start(f32[96]{0:T(128)} %param.6) | copy-start | bytes 1156
  2.1 8.1 %copy-start = (f32[3,8,8,128]{3,2,1,0:T(8,128)S(1)}, f32[3,8,8,128]{3,2,1,0:T(8,128)}, u32[]{:S(2)}) copy-start(f32[3,8,8,128]{3,2,1,0:T(8,128)} %param.4) | copy-start | bytes 294916
  2.1 8.0 %collective-permute-start = (f32[25,8,6]{0,1,2:T(8,128)S(1)}, f32[25,8,6]{0,1,2:T(8,128)S(1)}, u32[]{:S(2)}, u32[]{:S(2)}) collective-permute-start(f32[25,8,6]{0,1,2:T(8,128)S(1)} %pad_maximum_fusion.5), channel_id=1, source_target_pairs={{0,1},{1,2},{2,3},{3,4},{4,5},{5,6},{6,7},{7,8},{8,9},{9,10},{10,1... | collective-permute-start | bytes 14408 | tf_op jit(solution)/shard_map/ppermute | solution.py:22
  10.1 0.7 copy-start.1
  10.9 6.0 %collective-permute-start.1 = (f32[25,3,134]{2,1,0:T(4,128)S(1)}, f32[25,3,134]{2,1,0:T(4,128)S(1)}, u32[]{:S(2)}, u32[]{:S(2)}) collective-permute-start(f32[25,3,134]{2,1,0:T(4,128)S(1)} %get-tuple-element.47), channel_id=1, source_target_pairs={{0,64},{64,128},{128,192},{192,256},{256,320},{320,384},{384,448},... | collective-permute-start | bytes 120608 | tf_op jit(solution)/shard_map/ppermute | solution.py:24
  12.8 5.9 %collective-permute-start.2 = (f32[25,3,134]{2,1,0:T(4,128)S(1)}, f32[25,3,134]{2,1,0:T(4,128)S(1)}, u32[]{:S(2)}, u32[]{:S(2)}) collective-permute-start(f32[25,3,134]{2,1,0:T(4,128)S(1)} %get-tuple-element.48), channel_id=1, source_target_pairs={{64,0},{128,64},{192,128},{256,192},{320,256},{384,320},{448,384},... | collective-permute-start | bytes 120608 | tf_op jit(solution)/shard_map/ppermute | solution.py:25
  43.6 5.9 %copy-start.2 = (s32[1,96]{1,0:T(1,128)S(1)}, s32[1,96]{1,0:T(1,128)}, u32[]{:S(2)}) copy-start(s32[1,96]{1,0:T(1,128)} %param.7) | copy-start | bytes 1156
  43.6 14.2 %collective-permute-start.3 = (f32[16,12,128]{2,0,1:T(8,128)S(1)}, f32[16,12,128]{2,0,1:T(8,128)S(1)}, u32[]{:S(2)}, u32[]{:S(2)}) collective-permute-start(f32[16,12,128]{2,0,1:T(8,128)S(1)} %copy.24), channel_id=1, source_target_pairs={{0,16},{16,0},{1,17},{17,1},{2,18},{18,2},{3,19},{19,3},{4,20},{20... | collective-permute-start | bytes 294920 | tf_op jit(solution)/shard_map/ppermute | solution.py:56
  57.9 23.1 %collective-permute-start.4 = (f32[32,12,128]{2,0,1:T(8,128)S(1)}, f32[32,12,128]{2,0,1:T(8,128)S(1)}, u32[]{:S(2)}, u32[]{:S(2)}) collective-permute-start(f32[32,12,128]{2,0,1:T(8,128)S(1)} %maximum_select_fusion.2), channel_id=1, source_target_pairs={{0,32},{32,0},{1,33},{33,1},{2,34},{34,2},{3,35},{35,3},{4,36},{36... | collective-permute-start | bytes 589832 | tf_op jit(solution)/shard_map/ppermute | solution.py:56

commit v15 on v12

--- a/solution.py
+++ b/solution.py
@@ -49,9 +49,9 @@
     lines = jnp.swapaxes(state.reshape(fields, n_lines, cells), 0, 1).reshape(per, n_half, fields, cells)
     lines = jnp.swapaxes(lines, 0, 1).reshape(n_half, per * fields, cells)
     ring = lax.all_to_all(lines, "xy", 0, 0, tiled=True)
-    other = lax.ppermute(ring, "zh", [(0, 1), (1, 0)])
     upper = lax.axis_index("zh")
-    ring = jnp.where(upper == 0, jnp.concatenate([ring, other], axis=0), jnp.concatenate([other, ring], axis=0))
+    empty = jnp.zeros_like(ring)
+    ring = jnp.where(upper == 0, jnp.concatenate([ring, empty], axis=0), jnp.concatenate([empty, ring], axis=0))
     chunks = ring.shape[0]
     ring = ring.reshape(chunks, per, fields, cells)
     ring = jnp.concatenate([ring[..., lag:], jnp.roll(ring, -1, axis=0)[..., :lag]], axis=-1)
@@ -60,7 +60,7 @@
     count = chunks * per_chunk
     doubled = jnp.concatenate([ring, ring], axis=0)
     lane = lax.broadcasted_iota(jnp.int32, (chunks, fields, cells), 2)
-    mine = []
+    moved = []
     for t in range(per):
         line = doubled[:, t]
         shift = lax.dynamic_index_in_dim(shift_row, first_row + (t * n_half + me) % radii, keepdims=False)
@@ -73,11 +73,18 @@
         for step in range(1, per_chunk):
             mixed = jnp.roll(jnp.where(lane < cells - step * BLOCK, base, earlier), step * BLOCK, axis=2)
             rolled = jnp.where(part == step, mixed, rolled)
-        mine.append(lax.dynamic_slice_in_dim(rolled, upper * n_half, n_half, 0))
-    out = jnp.stack(mine, axis=1).reshape(n_half, per * fields, cells)
-    back = lax.all_to_all(out, "xy", 0, 0, tiled=True).reshape(n_half, per, fields, cells)
-    back = jnp.swapaxes(back, 0, 1).reshape(n_lines, fields, cells)
-    return jnp.swapaxes(back, 0, 1).reshape(fields, heights, radii, cells)
+        moved.append(rolled)
+    out = jnp.stack(moved, axis=1).reshape(chunks, per * fields, cells)
+    back = lax.all_to_all(out, AZI, 0, 0, tiled=True).reshape(2, n_half, per, fields, cells)
+    sender = lax.broadcasted_iota(jnp.int32, (n_half, per), 0)
+    t_idx = lax.broadcasted_iota(jnp.int32, (n_half, per), 1)
+    k = jnp.take(shift_row, first_row + (t_idx * n_half + sender) % radii) % count
+    cell = lax.axis_index(AZI) * cells + lax.broadcasted_iota(jnp.int32, (n_half, per, cells), 2)
+    source = (cell - BLOCK * k[:, :, None]) % (chunks * cells)
+    lower = (source < n_half * cells - lag) | (source >= chunks * cells - lag)
+    kept = jnp.where(lower[:, :, None, :], back[0], back[1])
+    kept = jnp.swapaxes(kept, 0, 1).reshape(n_lines, fields, cells)
+    return jnp.swapaxes(kept, 0, 1).reshape(fields, heights, radii, cells)
 
 
 def body(fields, viscosity, rotation, shift_blocks):

time: 85 us -> 88.4 us (1.040)
  waiting for transfers between devices: 31.6 us -> 50 us
  blocking collectives: 16.8 us -> 0 us
  local copies, waits for them, and re-layouts: 6.36 us -> 8.33 us
    all_to_all x0 -> x1, waiting for transfers between devices: none -> 21.8 us  [advect(): lax.all_to_all(out, AZI, 0, 0, tiled=True)]
    all_to_all x1 -> x0, blocking collectives: 16.8 us -> none  [advect(): lax.all_to_all(out, 'xy', 0, 0, tiled=True)]
    all_to_all x0 -> x1, starting transfers between devices: none -> 9.69 us  [advect(): lax.all_to_all(out, AZI, 0, 0, tiled=True)]
    ppermute x1 -> x0, starting transfers between devices: 8.91 us -> none  [advect(): other = lax.ppermute(ring, 'zh', [(0, 1), (1, 0)])]
    ppermute x1 -> x0, waiting for transfers between devices: 6.04 us -> none  [advect(): other = lax.ppermute(ring, 'zh', [(0, 1), (1, 0)])]
    ppermute x1, waiting for transfers between devices: 0.23 us -> 5.54 us  [exchange_halo(): south = lax.ppermute(wide[:, -width:, :], 'rad', up)]
    ppermute x1, waiting for transfers between devices: 1.83 us -> 0.01 us  [exchange_halo(): north = lax.ppermute(wide[:, :width, :], 'rad', down)]
    ppermute x1, starting transfers between devices: 3.64 us -> 1.92 us  [exchange_halo(): north = lax.ppermute(wide[:, :width, :], 'rad', down)]
  transfers between devices with their start and end apart: 5 -> 5, of which waited for: 5 -> 4; matrix products, arithmetic and copies ran while one was open for 1% -> 3% of each run, Pallas kernels for 0% -> 0%
where the time goes in v15:
time: 88.4 us; the launch traced here: 88 us
  waiting for transfers between devices  50 us (57%)
  starting transfers between devices  21.6 us (24%)
  local copies, waits for them, and re-layouts  8.33 us (9%)
  between operations  4.44 us (5%)
  other arithmetic  3.55 us (4%)
    all_to_all x1, waiting for transfers between devices, advect(): lax.all_to_all(out, AZI, 0, 0, tiled=True)  21.8 us
    ppermute x1, waiting for transfers between devices, exchange_halo(): behind = lax.ppermute(tail, AZI, fwd)  17.2 us
    all_to_all x1, starting transfers between devices, advect(): lax.all_to_all(out, AZI, 0, 0, tiled=True)  9.69 us
    ppermute x1, waiting for transfers between devices, exchange_halo(): south = lax.ppermute(wide[:, -width:, :], 'rad', up)  5.54 us
    all_to_all x1, waiting for transfers between devices, advect(): ring = lax.all_to_all(lines, 'xy', 0, 0, tiled=True)  5.46 us
    all_to_all x1, starting transfers between devices, advect(): ring = lax.all_to_all(lines, 'xy', 0, 0, tiled=True)  3.99 us
    ppermute x1, starting transfers between devices, exchange_halo(): behind = lax.ppermute(tail, AZI, fwd)  3.61 us
    ppermute x1, starting transfers between devices, exchange_halo(): south = lax.ppermute(wide[:, -width:, :], 'rad', up)  2.41 us
  transfers between devices with their start and end apart: 5, of which 4 were waited for; matrix products, arithmetic and copies ran while one was open for 3% of the time, Pallas kernels for 0%

profile of v15, /device:TPU:64, one launch (start us, length us, event | category | flops | bytes accessed | tf_op | source)
XLA Modules:
  0.0 88.0 jit_solution(17077290093065378269)
XLA Ops:
  0.0 0.8 slice_bitcast_fusion.4
  0.8 0.1 copy.38
  0.9 1.0 %slice.284 = f32[3,8,8,6]{3,2,1,0:T(8,128)S(1)} slice(f32[3,8,8,128]{3,2,1,0:T(8,128)} %param.4), slice={[0:3], [0:8], [0:8], [122:128]} | slice | bytes 9216 | tf_op jit(solution)/shard_map/slice | solution.py:98
  1.9 0.1 copy.48
  2.1 3.6 %collective-permute-start = (f32[25,8,6]{0,1,2:T(8,128)S(1)}, f32[25,8,6]{0,1,2:T(8,128)S(1)}, u32[]{:S(2)}, u32[]{:S(2)}) collective-permute-start(f32[25,8,6]{0,1,2:T(8,128)S(1)} %pad_maximum_fusion.3), channel_id=1, source_target_pairs={{0,1},{1,2},{2,3},{3,4},{4,5},{5,6},{6,7},{7,8},{8,9},{9,10},{10,1... | collective-permute-start | bytes 14408 | tf_op jit(solution)/shard_map/ppermute | solution.py:20
  6.1 17.2 %collective-permute-done = f32[25,8,6]{0,1,2:T(8,128)S(1)} collective-permute-done((f32[25,8,6]{0,1,2:T(8,128)S(1)}, f32[25,8,6]{0,1,2:T(8,128)S(1)}, u32[]{:S(2)}, u32[]{:S(2)}) %collective-permute-start) | collective-permute-done | bytes 4832 | tf_op jit(solution)/shard_map/ppermute | solution.py:20
  23.4 0.2 copy.39
  23.5 0.5 copy-done.2
  24.2 1.9 %collective-permute-start.2 = (f32[25,3,134]{2,1,0:T(4,128)S(1)}, f32[25,3,134]{2,1,0:T(4,128)S(1)}, u32[]{:S(2)}, u32[]{:S(2)}) collective-permute-start(f32[25,3,134]{2,1,0:T(4,128)S(1)} %get-tuple-element.40), channel_id=1, source_target_pairs={{64,0},{128,64},{192,128},{256,192},{320,256},{384,320},{448,384},... | collective-permute-start | bytes 120608 | tf_op jit(solution)/shard_map/ppermute | solution.py:23
  26.1 2.4 %collective-permute-start.1 = (f32[25,3,134]{2,1,0:T(4,128)S(1)}, f32[25,3,134]{2,1,0:T(4,128)S(1)}, u32[]{:S(2)}, u32[]{:S(2)}) collective-permute-start(f32[25,3,134]{2,1,0:T(4,128)S(1)} %get-tuple-element.39), channel_id=1, source_target_pairs={{0,64},{64,128},{128,192},{192,256},{256,320},{320,384},{384,448},... | collective-permute-start | bytes 120608 | tf_op jit(solution)/shard_map/ppermute | solution.py:22
  28.7 5.5 %collective-permute-done.1 = f32[25,3,134]{2,1,0:T(4,128)S(1)} collective-permute-done((f32[25,3,134]{2,1,0:T(4,128)S(1)}, f32[25,3,134]{2,1,0:T(4,128)S(1)}, u32[]{:S(2)}, u32[]{:S(2)}) %collective-permute-start.1) | collective-permute-done | bytes 40232 | tf_op jit(solution)/shard_map/ppermute | solution.py:22
  34.3 0.2 pad_maximum_fusion
  34.5 0.2 fusion.40
  35.0 0.5 subtract_multiply_fusion.3
  35.5 0.2 slice_subtract_fusion.6
  35.6 0.2 fusion.6
  35.8 0.2 fusion.38
  36.2 0.5 subtract_multiply_fusion.1
  36.7 0.2 slice_subtract_fusion.2
  36.9 0.3 fusion.1
  37.5 0.2 subtract_multiply_fusion.5
  37.9 0.7 copy.41
  38.6 4.0 %all-to-all-start = ((f32[32,6,128]{2,1,0:T(8,128)}), f32[32,6,128]{2,1,0:T(8,128)S(1)}, u32[]{:S(2)}, u32[]{:S(2)}) async-start(f32[32,6,128]{2,1,0:T(8,128)} %copy.41), calls=%async_computation | async-start | bytes 262144 | tf_op jit(solution)/shard_map/all_to_all | solution.py:51
  42.7 0.6 constant_dynamic-slice_fusion.1
  47.4 5.5 %all-to-all-done = f32[32,6,128]{2,1,0:T(8,128)S(1)} async-done(((f32[32,6,128]{2,1,0:T(8,128)}), f32[32,6,128]{2,1,0:T(8,128)S(1)}, u32[]{:S(2)}, u32[]{:S(2)}) %all-to-all-start) | async-done | bytes 98336 | tf_op jit(solution)/shard_map/all_to_all | solution.py:51
  53.1 0.2 maximum_maximum_fusion
  53.6 0.1 maximum_select_fusion
  53.7 0.8 copy.44
  54.5 9.7 %all-to-all-start.1 = ((f32[64,6,128]{2,1,0:T(8,128)}), f32[64,6,128]{2,1,0:T(8,128)S(1)}, u32[]{:S(2)}, u32[]{:S(2)}) async-start(f32[64,6,128]{2,1,0:T(8,128)} %copy.44), calls=%async_computation.1 | async-start | bytes 524288 | tf_op jit(solution)/shard_map/all_to_all | solution.py:78
  64.2 0.8 gather_fusion
  65.4 21.8 %all-to-all-done.1 = f32[64,6,128]{2,1,0:T(8,128)S(1)} async-done(((f32[64,6,128]{2,1,0:T(8,128)}), f32[64,6,128]{2,1,0:T(8,128)S(1)}, u32[]{:S(2)}, u32[]{:S(2)}) %all-to-all-start.1) | async-done | bytes 196640 | tf_op jit(solution)/shard_map/all_to_all | solution.py:78
  87.3 0.6 copy.47
  (57 shorter events, 2.7 us)
Async XLA Ops:
  2.0 3.7 %copy-start.3 = (f32[96]{0:T(128)S(1)}, f32[96]{0:T(128)}, u32[]{:S(2)}) copy-start(f32[96]{0:T(128)} %param.6) | copy-start | bytes 1156
  2.1 21.4 %copy-start.1 = (f32[3,8,8,128]{3,2,1,0:T(8,128)S(1)}, f32[3,8,8,128]{3,2,1,0:T(8,128)}, u32[]{:S(2)}) copy-start(f32[3,8,8,128]{3,2,1,0:T(8,128)} %param.4) | copy-start | bytes 294916
  2.1 21.3 %collective-permute-start = (f32[25,8,6]{0,1,2:T(8,128)S(1)}, f32[25,8,6]{0,1,2:T(8,128)S(1)}, u32[]{:S(2)}, u32[]{:S(2)}) collective-permute-start(f32[25,8,6]{0,1,2:T(8,128)S(1)} %pad_maximum_fusion.3), channel_id=1, source_target_pairs={{0,1},{1,2},{2,3},{3,4},{4,5},{5,6},{6,7},{7,8},{8,9},{9,10},{10,1... | collective-permute-start | bytes 14408 | tf_op jit(solution)/shard_map/ppermute | solution.py:20
  23.4 0.7 copy-start.2
  24.2 4.5 %collective-permute-start.2 = (f32[25,3,134]{2,1,0:T(4,128)S(1)}, f32[25,3,134]{2,1,0:T(4,128)S(1)}, u32[]{:S(2)}, u32[]{:S(2)}) collective-permute-start(f32[25,3,134]{2,1,0:T(4,128)S(1)} %get-tuple-element.40), channel_id=1, source_target_pairs={{64,0},{128,64},{192,128},{256,192},{320,256},{384,320},{448,384},... | collective-permute-start | bytes 120608 | tf_op jit(solution)/shard_map/ppermute | solution.py:23
  26.1 8.1 %collective-permute-start.1 = (f32[25,3,134]{2,1,0:T(4,128)S(1)}, f32[25,3,134]{2,1,0:T(4,128)S(1)}, u32[]{:S(2)}, u32[]{:S(2)}) collective-permute-start(f32[25,3,134]{2,1,0:T(4,128)S(1)} %get-tuple-element.39), channel_id=1, source_target_pairs={{0,64},{64,128},{128,192},{192,256},{256,320},{320,384},{384,448},... | collective-permute-start | bytes 120608 | tf_op jit(solution)/shard_map/ppermute | solution.py:22
  38.6 4.1 %copy-start = (s32[1,96]{1,0:T(1,128)S(1)}, s32[1,96]{1,0:T(1,128)}, u32[]{:S(2)}) copy-start(s32[1,96]{1,0:T(1,128)} %param.7) | copy-start | bytes 1156
  38.6 14.3 %all-to-all-start = ((f32[32,6,128]{2,1,0:T(8,128)}), f32[32,6,128]{2,1,0:T(8,128)S(1)}, u32[]{:S(2)}, u32[]{:S(2)}) async-start(f32[32,6,128]{2,1,0:T(8,128)} %copy.41), calls=%async_computation | async-start | bytes 262144 | tf_op jit(solution)/shard_map/all_to_all | solution.py:51
  54.5 32.7 %all-to-all-start.1 = ((f32[64,6,128]{2,1,0:T(8,128)}), f32[64,6,128]{2,1,0:T(8,128)S(1)}, u32[]{:S(2)}, u32[]{:S(2)}) async-start(f32[64,6,128]{2,1,0:T(8,128)} %copy.44), calls=%async_computation.1 | async-start | bytes 524288 | tf_op jit(solution)/shard_map/all_to_all | solution.py:78

commit v16 on v12

--- a/solution.py
+++ b/solution.py
@@ -59,11 +59,12 @@
     per_chunk = cells // BLOCK
     count = chunks * per_chunk
     doubled = jnp.concatenate([ring, ring], axis=0)
-    lane = lax.broadcasted_iota(jnp.int32, (chunks, fields, cells), 2)
+    groups = [list(range(per))] if n_half % radii == 0 else [[t] for t in range(per)]
     mine = []
-    for t in range(per):
-        line = doubled[:, t]
-        shift = lax.dynamic_index_in_dim(shift_row, first_row + (t * n_half + me) % radii, keepdims=False)
+    for group in groups:
+        line = doubled[:, group[0] : group[-1] + 1]
+        lane = lax.broadcasted_iota(jnp.int32, (chunks,) + line.shape[1:], line.ndim - 1)
+        shift = lax.dynamic_index_in_dim(shift_row, first_row + (group[0] * n_half + me) % radii, keepdims=False)
         shift = shift % count
         whole = shift // per_chunk
         part = shift % per_chunk
@@ -71,10 +72,10 @@
         earlier = lax.dynamic_slice_in_dim(line, (chunks - whole - 1) % chunks, chunks, 0)
         rolled = base
         for step in range(1, per_chunk):
-            mixed = jnp.roll(jnp.where(lane < cells - step * BLOCK, base, earlier), step * BLOCK, axis=2)
+            mixed = jnp.roll(jnp.where(lane < cells - step * BLOCK, base, earlier), step * BLOCK, axis=-1)
             rolled = jnp.where(part == step, mixed, rolled)
         mine.append(lax.dynamic_slice_in_dim(rolled, upper * n_half, n_half, 0))
-    out = jnp.stack(mine, axis=1).reshape(n_half, per * fields, cells)
+    out = jnp.concatenate(mine, axis=1).reshape(n_half, per * fields, cells)
     back = lax.all_to_all(out, "xy", 0, 0, tiled=True).reshape(n_half, per, fields, cells)
     back = jnp.swapaxes(back, 0, 1).reshape(n_lines, fields, cells)
     return jnp.swapaxes(back, 0, 1).reshape(fields, heights, radii, cells)

time: 85 us -> 83.8 us (0.986)
  between operations: 4.32 us -> 2.35 us
  waiting for transfers between devices: 31.6 us -> 33.5 us
  blocking collectives: 16.8 us -> 15.9 us
    all_to_all x1, waiting for transfers between devices: 6.22 us -> 8.18 us  [advect(): ring = lax.all_to_all(lines, 'xy', 0, 0, tiled=True)]
    all_to_all x1, blocking collectives: 16.8 us -> 15.9 us  [advect(): lax.all_to_all(out, 'xy', 0, 0, tiled=True)]
where the time goes in v16:
time: 83.8 us; the launch traced here: 83.4 us
  waiting for transfers between devices  33.5 us (40%)
  starting transfers between devices  21.9 us (26%)
  blocking collectives  15.9 us (19%)
  local copies, waits for them, and re-layouts  6.27 us (7%)
  other arithmetic  3.44 us (4%)
  between operations  2.35 us (3%)
    ppermute x1, waiting for transfers between devices, exchange_halo(): behind = lax.ppermute(tail, AZI, fwd)  17.2 us
    all_to_all x1, blocking collectives, advect(): lax.all_to_all(out, 'xy', 0, 0, tiled=True)  15.9 us
    ppermute x1, starting transfers between devices, advect(): other = lax.ppermute(ring, 'zh', [(0, 1), (1, 0)])  8.91 us
    all_to_all x1, waiting for transfers between devices, advect(): ring = lax.all_to_all(lines, 'xy', 0, 0, tiled=True)  8.18 us
    ppermute x1, waiting for transfers between devices, advect(): other = lax.ppermute(ring, 'zh', [(0, 1), (1, 0)])  6.04 us
    all_to_all x1, starting transfers between devices, advect(): ring = lax.all_to_all(lines, 'xy', 0, 0, tiled=True)  3.85 us
    ppermute x1, starting transfers between devices, exchange_halo(): north = lax.ppermute(wide[:, :width, :], 'rad', down)  3.64 us
    ppermute x1, starting transfers between devices, exchange_halo(): behind = lax.ppermute(tail, AZI, fwd)  3.61 us
  transfers between devices with their start and end apart: 5, of which 5 were waited for; matrix products, arithmetic and copies ran while one was open for 1% of the time, Pallas kernels for 0%

profile of v16, /device:TPU:64, one launch (start us, length us, event | category | flops | bytes accessed | tf_op | source)
XLA Modules:
  0.0 83.4 jit_solution(10715150015495103418)
XLA Ops:
  0.0 0.8 slice_bitcast_fusion
  0.8 0.1 copy.20
  0.9 1.0 %slice.264 = f32[3,8,8,6]{3,2,1,0:T(8,128)S(1)} slice(f32[3,8,8,128]{3,2,1,0:T(8,128)} %param.4), slice={[0:3], [0:8], [0:8], [122:128]} | slice | bytes 9216 | tf_op jit(solution)/shard_map/slice | solution.py:92
  1.9 0.1 copy.31
  2.1 3.6 %collective-permute-start = (f32[25,8,6]{0,1,2:T(8,128)S(1)}, f32[25,8,6]{0,1,2:T(8,128)S(1)}, u32[]{:S(2)}, u32[]{:S(2)}) collective-permute-start(f32[25,8,6]{0,1,2:T(8,128)S(1)} %pad_maximum_fusion.4), channel_id=1, source_target_pairs={{0,1},{1,2},{2,3},{3,4},{4,5},{5,6},{6,7},{7,8},{8,9},{9,10},{10,1... | collective-permute-start | bytes 14408 | tf_op jit(solution)/shard_map/ppermute | solution.py:20
  6.1 17.2 %collective-permute-done = f32[25,8,6]{0,1,2:T(8,128)S(1)} collective-permute-done((f32[25,8,6]{0,1,2:T(8,128)S(1)}, f32[25,8,6]{0,1,2:T(8,128)S(1)}, u32[]{:S(2)}, u32[]{:S(2)}) %collective-permute-start) | collective-permute-done | bytes 4832 | tf_op jit(solution)/shard_map/ppermute | solution.py:20
  23.4 0.2 copy.21
  23.5 0.5 copy-done.2
  24.2 1.9 %collective-permute-start.1 = (f32[25,3,134]{2,1,0:T(4,128)S(1)}, f32[25,3,134]{2,1,0:T(4,128)S(1)}, u32[]{:S(2)}, u32[]{:S(2)}) collective-permute-start(f32[25,3,134]{2,1,0:T(4,128)S(1)} %get-tuple-element.35), channel_id=1, source_target_pairs={{0,64},{64,128},{128,192},{192,256},{256,320},{320,384},{384,448},... | collective-permute-start | bytes 120608 | tf_op jit(solution)/shard_map/ppermute | solution.py:22
  26.2 3.6 %collective-permute-start.2 = (f32[25,3,134]{2,1,0:T(4,128)S(1)}, f32[25,3,134]{2,1,0:T(4,128)S(1)}, u32[]{:S(2)}, u32[]{:S(2)}) collective-permute-start(f32[25,3,134]{2,1,0:T(4,128)S(1)} %get-tuple-element.36), channel_id=1, source_target_pairs={{64,0},{128,64},{192,128},{256,192},{320,256},{384,320},{448,384},... | collective-permute-start | bytes 120608 | tf_op jit(solution)/shard_map/ppermute | solution.py:23
  30.0 0.2 collective-permute-done.1
  30.2 1.8 %collective-permute-done.2 = f32[25,3,134]{2,1,0:T(4,128)S(1)} collective-permute-done((f32[25,3,134]{2,1,0:T(4,128)S(1)}, f32[25,3,134]{2,1,0:T(4,128)S(1)}, u32[]{:S(2)}, u32[]{:S(2)}) %collective-permute-start.2) | collective-permute-done | bytes 40232 | tf_op jit(solution)/shard_map/ppermute | solution.py:23
  32.3 0.2 pad_maximum_fusion
  32.6 0.2 fusion.32
  32.9 0.5 subtract_multiply_fusion.3
  33.4 0.2 slice_subtract_fusion.6
  33.6 0.2 fusion.6
  33.8 0.2 fusion.30
  34.1 0.5 subtract_multiply_fusion.1
  34.6 0.2 slice_subtract_fusion.2
  34.7 0.3 fusion.1
  35.2 0.2 subtract_multiply_fusion.5
  35.7 0.7 copy.23
  36.4 3.9 %all-to-all-start = ((f32[32,6,128]{2,1,0:T(8,128)}), f32[32,6,128]{2,1,0:T(8,128)S(1)}, u32[]{:S(2)}, u32[]{:S(2)}) async-start(f32[32,6,128]{2,1,0:T(8,128)} %copy.23), calls=%async_computation | async-start | bytes 262144 | tf_op jit(solution)/shard_map/all_to_all | solution.py:51
  40.3 0.6 constant_dynamic-slice_fusion
  42.9 8.2 %all-to-all-done = f32[32,6,128]{2,1,0:T(8,128)S(1)} async-done(((f32[32,6,128]{2,1,0:T(8,128)}), f32[32,6,128]{2,1,0:T(8,128)S(1)}, u32[]{:S(2)}, u32[]{:S(2)}) %all-to-all-start) | async-done | bytes 98336 | tf_op jit(solution)/shard_map/all_to_all | solution.py:51
  51.1 8.9 %collective-permute-start.3 = (f32[32,6,128]{2,0,1:T(8,128)S(1)}, f32[32,6,128]{2,0,1:T(8,128)S(1)}, u32[]{:S(2)}, u32[]{:S(2)}) collective-permute-start(f32[32,6,128]{2,0,1:T(8,128)S(1)} %copy.24), channel_id=1, source_target_pairs={{0,32},{32,0},{1,33},{33,1},{2,34},{34,2},{3,35},{35,3},{4,36},{36... | collective-permute-start | bytes 294920 | tf_op jit(solution)/shard_map/ppermute | solution.py:52
  60.0 6.0 %collective-permute-done.3 = f32[32,6,128]{2,0,1:T(8,128)S(1)} collective-permute-done((f32[32,6,128]{2,0,1:T(8,128)S(1)}, f32[32,6,128]{2,0,1:T(8,128)S(1)}, u32[]{:S(2)}, u32[]{:S(2)}) %collective-permute-start.3) | collective-permute-done | bytes 98336 | tf_op jit(solution)/shard_map/ppermute | solution.py:52
  66.1 0.2 fusion.12
  66.3 0.2 maximum_maximum_fusion
  66.8 15.9 %all_to_all.10 = f32[32,6,128]{2,1,0:T(8,128)S(1)} all-to-all(f32[32,6,128]{2,1,0:T(8,128)S(1)} %copy.28), channel_id=1, replica_groups=mesh['rad'=12,'zh'=2,'xy'=32] {'xy'}, dimensions={0} | all-to-all | bytes 196608 | tf_op jit(solution)/shard_map/all_to_all | solution.py:79
  82.7 0.6 copy.30
  (42 shorter events, 2.1 us)
Async XLA Ops:
  0.0 40.3 %copy-start = (s32[1,96]{1,0:T(1,128)S(1)}, s32[1,96]{1,0:T(1,128)}, u32[]{:S(2)}) copy-start(s32[1,96]{1,0:T(1,128)} %param.7) | copy-start | bytes 1156
  2.0 3.7 %copy-start.3 = (f32[96]{0:T(128)S(1)}, f32[96]{0:T(128)}, u32[]{:S(2)}) copy-start(f32[96]{0:T(128)} %param.6) | copy-start | bytes 1156
  2.1 21.4 %copy-start.1 = (f32[3,8,8,128]{3,2,1,0:T(8,128)S(1)}, f32[3,8,8,128]{3,2,1,0:T(8,128)}, u32[]{:S(2)}) copy-start(f32[3,8,8,128]{3,2,1,0:T(8,128)} %param.4) | copy-start | bytes 294916
  2.1 21.3 %collective-permute-start = (f32[25,8,6]{0,1,2:T(8,128)S(1)}, f32[25,8,6]{0,1,2:T(8,128)S(1)}, u32[]{:S(2)}, u32[]{:S(2)}) collective-permute-start(f32[25,8,6]{0,1,2:T(8,128)S(1)} %pad_maximum_fusion.4), channel_id=1, source_target_pairs={{0,1},{1,2},{2,3},{3,4},{4,5},{5,6},{6,7},{7,8},{8,9},{9,10},{10,1... | collective-permute-start | bytes 14408 | tf_op jit(solution)/shard_map/ppermute | solution.py:20
  23.4 0.7 copy-start.2
  24.2 6.0 %collective-permute-start.1 = (f32[25,3,134]{2,1,0:T(4,128)S(1)}, f32[25,3,134]{2,1,0:T(4,128)S(1)}, u32[]{:S(2)}, u32[]{:S(2)}) collective-permute-start(f32[25,3,134]{2,1,0:T(4,128)S(1)} %get-tuple-element.35), channel_id=1, source_target_pairs={{0,64},{64,128},{128,192},{192,256},{256,320},{320,384},{384,448},... | collective-permute-start | bytes 120608 | tf_op jit(solution)/shard_map/ppermute | solution.py:22
  26.2 5.9 %collective-permute-start.2 = (f32[25,3,134]{2,1,0:T(4,128)S(1)}, f32[25,3,134]{2,1,0:T(4,128)S(1)}, u32[]{:S(2)}, u32[]{:S(2)}) collective-permute-start(f32[25,3,134]{2,1,0:T(4,128)S(1)} %get-tuple-element.36), channel_id=1, source_target_pairs={{64,0},{128,64},{192,128},{256,192},{320,256},{384,320},{448,384},... | collective-permute-start | bytes 120608 | tf_op jit(solution)/shard_map/ppermute | solution.py:23
  36.4 14.7 %all-to-all-start = ((f32[32,6,128]{2,1,0:T(8,128)}), f32[32,6,128]{2,1,0:T(8,128)S(1)}, u32[]{:S(2)}, u32[]{:S(2)}) async-start(f32[32,6,128]{2,1,0:T(8,128)} %copy.23), calls=%async_computation | async-start | bytes 262144 | tf_op jit(solution)/shard_map/all_to_all | solution.py:51
  51.1 15.0 %collective-permute-start.3 = (f32[32,6,128]{2,0,1:T(8,128)S(1)}, f32[32,6,128]{2,0,1:T(8,128)S(1)}, u32[]{:S(2)}, u32[]{:S(2)}) collective-permute-start(f32[32,6,128]{2,0,1:T(8,128)S(1)} %copy.24), channel_id=1, source_target_pairs={{0,32},{32,0},{1,33},{33,1},{2,34},{34,2},{3,35},{35,3},{4,36},{36... | collective-permute-start | bytes 294920 | tf_op jit(solution)/shard_map/ppermute | solution.py:52

commit v17 on v16

--- a/solution.py
+++ b/solution.py
@@ -63,18 +63,18 @@
     mine = []
     for group in groups:
         line = doubled[:, group[0] : group[-1] + 1]
-        lane = lax.broadcasted_iota(jnp.int32, (chunks,) + line.shape[1:], line.ndim - 1)
+        lane = lax.broadcasted_iota(jnp.int32, (n_half,) + line.shape[1:], line.ndim - 1)
         shift = lax.dynamic_index_in_dim(shift_row, first_row + (group[0] * n_half + me) % radii, keepdims=False)
         shift = shift % count
         whole = shift // per_chunk
         part = shift % per_chunk
-        base = lax.dynamic_slice_in_dim(line, (chunks - whole) % chunks, chunks, 0)
-        earlier = lax.dynamic_slice_in_dim(line, (chunks - whole - 1) % chunks, chunks, 0)
+        base = lax.dynamic_slice_in_dim(line, (chunks - whole + upper * n_half) % chunks, n_half, 0)
+        earlier = lax.dynamic_slice_in_dim(line, (chunks - whole - 1 + upper * n_half) % chunks, n_half, 0)
         rolled = base
         for step in range(1, per_chunk):
             mixed = jnp.roll(jnp.where(lane < cells - step * BLOCK, base, earlier), step * BLOCK, axis=-1)
             rolled = jnp.where(part == step, mixed, rolled)
-        mine.append(lax.dynamic_slice_in_dim(rolled, upper * n_half, n_half, 0))
+        mine.append(rolled)
     out = jnp.concatenate(mine, axis=1).reshape(n_half, per * fields, cells)
     back = lax.all_to_all(out, "xy", 0, 0, tiled=True).reshape(n_half, per, fields, cells)
     back = jnp.swapaxes(back, 0, 1).reshape(n_lines, fields, cells)

time: 83.8 us -> 83.8 us (level)
  no operation moved by 1% of the time
where the time goes in v17:
time: 83.8 us; the launch traced here: 83.3 us
  waiting for transfers between devices  33.5 us (40%)
  starting transfers between devices  21.9 us (26%)
  blocking collectives  15.9 us (19%)
  local copies, waits for them, and re-layouts  6.24 us (7%)
  other arithmetic  3.42 us (4%)
  between operations  2.34 us (3%)
    ppermute x1, waiting for transfers between devices, exchange_halo(): behind = lax.ppermute(tail, AZI, fwd)  17.2 us
    all_to_all x1, blocking collectives, advect(): lax.all_to_all(out, 'xy', 0, 0, tiled=True)  15.9 us
    ppermute x1, starting transfers between devices, advect(): other = lax.ppermute(ring, 'zh', [(0, 1), (1, 0)])  8.91 us
    all_to_all x1, waiting for transfers between devices, advect(): ring = lax.all_to_all(lines, 'xy', 0, 0, tiled=True)  8.19 us
    ppermute x1, waiting for transfers between devices, advect(): other = lax.ppermute(ring, 'zh', [(0, 1), (1, 0)])  6.04 us
    all_to_all x1, starting transfers between devices, advect(): ring = lax.all_to_all(lines, 'xy', 0, 0, tiled=True)  3.85 us
    ppermute x1, starting transfers between devices, exchange_halo(): north = lax.ppermute(wide[:, :width, :], 'rad', down)  3.64 us
    ppermute x1, starting transfers between devices, exchange_halo(): behind = lax.ppermute(tail, AZI, fwd)  3.61 us
  transfers between devices with their start and end apart: 5, of which 5 were waited for; matrix products, arithmetic and copies ran while one was open for 1% of the time, Pallas kernels for 0%

profile of v17, /device:TPU:64, one launch (start us, length us, event | category | flops | bytes accessed | tf_op | source)
XLA Modules:
  0.0 83.3 jit_solution(6267519135945850811)
XLA Ops:
  0.0 0.8 slice_bitcast_fusion
  0.8 0.1 copy.20
  0.9 1.0 %slice.264 = f32[3,8,8,6]{3,2,1,0:T(8,128)S(1)} slice(f32[3,8,8,128]{3,2,1,0:T(8,128)} %param.4), slice={[0:3], [0:8], [0:8], [122:128]} | slice | bytes 9216 | tf_op jit(solution)/shard_map/slice | solution.py:92
  1.9 0.1 copy.31
  2.1 3.6 %collective-permute-start = (f32[25,8,6]{0,1,2:T(8,128)S(1)}, f32[25,8,6]{0,1,2:T(8,128)S(1)}, u32[]{:S(2)}, u32[]{:S(2)}) collective-permute-start(f32[25,8,6]{0,1,2:T(8,128)S(1)} %pad_maximum_fusion.4), channel_id=1, source_target_pairs={{0,1},{1,2},{2,3},{3,4},{4,5},{5,6},{6,7},{7,8},{8,9},{9,10},{10,1... | collective-permute-start | bytes 14408 | tf_op jit(solution)/shard_map/ppermute | solution.py:20
  6.1 17.2 %collective-permute-done = f32[25,8,6]{0,1,2:T(8,128)S(1)} collective-permute-done((f32[25,8,6]{0,1,2:T(8,128)S(1)}, f32[25,8,6]{0,1,2:T(8,128)S(1)}, u32[]{:S(2)}, u32[]{:S(2)}) %collective-permute-start) | collective-permute-done | bytes 4832 | tf_op jit(solution)/shard_map/ppermute | solution.py:20
  23.4 0.2 copy.21
  23.5 0.5 copy-done.2
  24.2 1.9 %collective-permute-start.1 = (f32[25,3,134]{2,1,0:T(4,128)S(1)}, f32[25,3,134]{2,1,0:T(4,128)S(1)}, u32[]{:S(2)}, u32[]{:S(2)}) collective-permute-start(f32[25,3,134]{2,1,0:T(4,128)S(1)} %get-tuple-element.35), channel_id=1, source_target_pairs={{0,64},{64,128},{128,192},{192,256},{256,320},{320,384},{384,448},... | collective-permute-start | bytes 120608 | tf_op jit(solution)/shard_map/ppermute | solution.py:22
  26.2 3.6 %collective-permute-start.2 = (f32[25,3,134]{2,1,0:T(4,128)S(1)}, f32[25,3,134]{2,1,0:T(4,128)S(1)}, u32[]{:S(2)}, u32[]{:S(2)}) collective-permute-start(f32[25,3,134]{2,1,0:T(4,128)S(1)} %get-tuple-element.36), channel_id=1, source_target_pairs={{64,0},{128,64},{192,128},{256,192},{320,256},{384,320},{448,384},... | collective-permute-start | bytes 120608 | tf_op jit(solution)/shard_map/ppermute | solution.py:23
  30.0 0.2 collective-permute-done.1
  30.2 1.8 %collective-permute-done.2 = f32[25,3,134]{2,1,0:T(4,128)S(1)} collective-permute-done((f32[25,3,134]{2,1,0:T(4,128)S(1)}, f32[25,3,134]{2,1,0:T(4,128)S(1)}, u32[]{:S(2)}, u32[]{:S(2)}) %collective-permute-start.2) | collective-permute-done | bytes 40232 | tf_op jit(solution)/shard_map/ppermute | solution.py:23
  32.3 0.2 pad_maximum_fusion
  32.6 0.2 fusion.30
  32.9 0.5 subtract_multiply_fusion.3
  33.4 0.2 slice_subtract_fusion.6
  33.6 0.2 fusion.6
  33.8 0.2 fusion.28
  34.1 0.5 subtract_multiply_fusion.1
  34.6 0.2 slice_subtract_fusion.2
  34.7 0.3 fusion.1
  35.2 0.2 subtract_multiply_fusion.5
  35.7 0.7 copy.23
  36.4 3.9 %all-to-all-start = ((f32[32,6,128]{2,1,0:T(8,128)}), f32[32,6,128]{2,1,0:T(8,128)S(1)}, u32[]{:S(2)}, u32[]{:S(2)}) async-start(f32[32,6,128]{2,1,0:T(8,128)} %copy.23), calls=%async_computation | async-start | bytes 262144 | tf_op jit(solution)/shard_map/all_to_all | solution.py:51
  40.3 0.6 constant_dynamic-slice_fusion
  42.9 8.2 %all-to-all-done = f32[32,6,128]{2,1,0:T(8,128)S(1)} async-done(((f32[32,6,128]{2,1,0:T(8,128)}), f32[32,6,128]{2,1,0:T(8,128)S(1)}, u32[]{:S(2)}, u32[]{:S(2)}) %all-to-all-start) | async-done | bytes 98336 | tf_op jit(solution)/shard_map/all_to_all | solution.py:51
  51.1 8.9 %collective-permute-start.3 = (f32[32,6,128]{2,0,1:T(8,128)S(1)}, f32[32,6,128]{2,0,1:T(8,128)S(1)}, u32[]{:S(2)}, u32[]{:S(2)}) collective-permute-start(f32[32,6,128]{2,0,1:T(8,128)S(1)} %copy.24), channel_id=1, source_target_pairs={{0,32},{32,0},{1,33},{33,1},{2,34},{34,2},{3,35},{35,3},{4,36},{36... | collective-permute-start | bytes 294920 | tf_op jit(solution)/shard_map/ppermute | solution.py:52
  60.0 6.0 %collective-permute-done.3 = f32[32,6,128]{2,0,1:T(8,128)S(1)} collective-permute-done((f32[32,6,128]{2,0,1:T(8,128)S(1)}, f32[32,6,128]{2,0,1:T(8,128)S(1)}, u32[]{:S(2)}, u32[]{:S(2)}) %collective-permute-start.3) | collective-permute-done | bytes 98336 | tf_op jit(solution)/shard_map/ppermute | solution.py:52
  66.1 0.2 fusion.12
  66.3 0.2 maximum_maximum_fusion
  66.8 15.9 %all_to_all.10 = f32[32,6,128]{2,1,0:T(8,128)S(1)} all-to-all(f32[32,6,128]{2,1,0:T(8,128)S(1)} %copy.28), channel_id=1, replica_groups=mesh['rad'=12,'zh'=2,'xy'=32] {'xy'}, dimensions={0} | all-to-all | bytes 196608 | tf_op jit(solution)/shard_map/all_to_all | solution.py:79
  82.7 0.6 copy.30
  (42 shorter events, 2.1 us)
Async XLA Ops:
  0.0 40.3 %copy-start = (s32[1,96]{1,0:T(1,128)S(1)}, s32[1,96]{1,0:T(1,128)}, u32[]{:S(2)}) copy-start(s32[1,96]{1,0:T(1,128)} %param.7) | copy-start | bytes 1156
  2.0 3.7 %copy-start.3 = (f32[96]{0:T(128)S(1)}, f32[96]{0:T(128)}, u32[]{:S(2)}) copy-start(f32[96]{0:T(128)} %param.6) | copy-start | bytes 1156
  2.1 21.4 %copy-start.1 = (f32[3,8,8,128]{3,2,1,0:T(8,128)S(1)}, f32[3,8,8,128]{3,2,1,0:T(8,128)}, u32[]{:S(2)}) copy-start(f32[3,8,8,128]{3,2,1,0:T(8,128)} %param.4) | copy-start | bytes 294916
  2.1 21.3 %collective-permute-start = (f32[25,8,6]{0,1,2:T(8,128)S(1)}, f32[25,8,6]{0,1,2:T(8,128)S(1)}, u32[]{:S(2)}, u32[]{:S(2)}) collective-permute-start(f32[25,8,6]{0,1,2:T(8,128)S(1)} %pad_maximum_fusion.4), channel_id=1, source_target_pairs={{0,1},{1,2},{2,3},{3,4},{4,5},{5,6},{6,7},{7,8},{8,9},{9,10},{10,1... | collective-permute-start | bytes 14408 | tf_op jit(solution)/shard_map/ppermute | solution.py:20
  23.4 0.7 copy-start.2
  24.2 6.0 %collective-permute-start.1 = (f32[25,3,134]{2,1,0:T(4,128)S(1)}, f32[25,3,134]{2,1,0:T(4,128)S(1)}, u32[]{:S(2)}, u32[]{:S(2)}) collective-permute-start(f32[25,3,134]{2,1,0:T(4,128)S(1)} %get-tuple-element.35), channel_id=1, source_target_pairs={{0,64},{64,128},{128,192},{192,256},{256,320},{320,384},{384,448},... | collective-permute-start | bytes 120608 | tf_op jit(solution)/shard_map/ppermute | solution.py:22
  26.2 5.9 %collective-permute-start.2 = (f32[25,3,134]{2,1,0:T(4,128)S(1)}, f32[25,3,134]{2,1,0:T(4,128)S(1)}, u32[]{:S(2)}, u32[]{:S(2)}) collective-permute-start(f32[25,3,134]{2,1,0:T(4,128)S(1)} %get-tuple-element.36), channel_id=1, source_target_pairs={{64,0},{128,64},{192,128},{256,192},{320,256},{384,320},{448,384},... | collective-permute-start | bytes 120608 | tf_op jit(solution)/shard_map/ppermute | solution.py:23
  36.4 14.7 %all-to-all-start = ((f32[32,6,128]{2,1,0:T(8,128)}), f32[32,6,128]{2,1,0:T(8,128)S(1)}, u32[]{:S(2)}, u32[]{:S(2)}) async-start(f32[32,6,128]{2,1,0:T(8,128)} %copy.23), calls=%async_computation | async-start | bytes 262144 | tf_op jit(solution)/shard_map/all_to_all | solution.py:51
  51.1 15.0 %collective-permute-start.3 = (f32[32,6,128]{2,0,1:T(8,128)S(1)}, f32[32,6,128]{2,0,1:T(8,128)S(1)}, u32[]{:S(2)}, u32[]{:S(2)}) collective-permute-start(f32[32,6,128]{2,0,1:T(8,128)S(1)} %copy.24), channel_id=1, source_target_pairs={{0,32},{32,0},{1,33},{33,1},{2,34},{34,2},{3,35},{35,3},{4,36},{36... | collective-permute-start | bytes 294920 | tf_op jit(solution)/shard_map/ppermute | solution.py:52
